TPU v7x, 512 devices: a whole 4x4x16 slice. The times are simulated.
512 devices in a mesh: dp: 8 (over x_hi, y), tm: 64 (over x_lo, z, core).
Axes of the slice: x: 4 (x_hi: 2, x_lo: 2; x = x_hi * 2 + x_lo), y: 4, z: 16, core: 2. Of those that a mesh axis runs over, the one named last changes fastest.
Arguments:
- signal: bfloat16 [8, 65536, 256], P('dp', 'tm'), may hold values from -6 to 6
- cotangent: bfloat16 [8, 65536, 256], P('dp', 'tm'), may hold values from -6 to 6
- first_history_weight: bfloat16 [256, 512], replicated, may hold values from -0.25 to 0.25
- first_current_weight: bfloat16 [256, 512], replicated, may hold values from -0.25 to 0.25
- first_residual_weight: bfloat16 [256, 256], replicated, may hold values from -0.375 to 0.375
- second_history_weight: bfloat16 [256, 512], replicated, may hold values from -0.25 to 0.25
- second_current_weight: bfloat16 [256, 512], replicated, may hold values from -0.25 to 0.25
- second_residual_weight: bfloat16 [256, 256], replicated, may hold values from -0.375 to 0.375
Outputs:
- grad_signal: bfloat16 [8, 65536, 256], P('dp', 'tm')
- grad_past_one: bfloat16 [256, 512], replicated
- grad_now_one: bfloat16 [256, 512], replicated
- grad_mix_one: bfloat16 [256, 256], replicated
- grad_past_two: bfloat16 [256, 512], replicated
- grad_now_two: bfloat16 [256, 512], replicated
- grad_mix_two: bfloat16 [256, 256], replicated
All inputs are finite; a program needn't handle non-finite values.
Results may differ from a plain program's by a relative error of at most 0.0068.
Values may be sent and summed in bfloat16 or wider, within the bound.
No kernel may reach another device: no remote copies, remote signals or barrier semaphores. Data moves between devices by JAX's collectives and lax.ppermute only.
A program may use at most 64 MiB of HBM per device.

v0:
```python
import math

import jax
import jax.numpy as jnp
from jax import lax
from jax.sharding import PartitionSpec as P

FIRST_DILATION = 512
SECOND_DILATION = 8192


def shifted(value, axis, steps):
    count = lax.axis_size(axis)
    leading, last = (max(0, -steps), min(count, count - steps))
    return lax.ppermute(value, axis, [(source, source + steps) for source in range(leading, last)])


def forward_layer(input_traces, past_rows, tap_past, tap_now, mixing):
    channels = input_traces.shape[-1]
    flat_now = input_traces.reshape(-1, channels)
    flat_past = past_rows.reshape(-1, channels)
    pre_act = jnp.dot(flat_past, tap_past, preferred_element_type=jnp.float32) + jnp.dot(
        flat_now, tap_now, preferred_element_type=jnp.float32
    )
    half_width = pre_act.shape[1] // 2
    filter_part = jnp.tanh(pre_act[:, :half_width])
    gate_part = jax.nn.sigmoid(pre_act[:, half_width:])
    hidden = (filter_part * gate_part).astype(jnp.bfloat16)
    output = (
        flat_now.astype(jnp.float32) + jnp.dot(hidden, mixing, preferred_element_type=jnp.float32)
    ).astype(jnp.bfloat16)
    return (filter_part, gate_part, hidden, output.reshape(input_traces.shape))


def backward_layer(input_traces, past_rows, saved, incoming_gradient, tap_past, tap_now, mixing):
    filter_part, gate_part, hidden, output = saved
    channels = input_traces.shape[-1]
    flat_now = input_traces.reshape(-1, channels)
    flat_past = past_rows.reshape(-1, channels)
    flat_up = incoming_gradient.reshape(-1, channels)
    hidden_grad = jnp.dot(flat_up, mixing.T, preferred_element_type=jnp.float32)
    filter_grad = hidden_grad * gate_part * (1.0 - filter_part * filter_part)
    gate_grad = hidden_grad * filter_part * gate_part * (1.0 - gate_part)
    pre_grad = jnp.concatenate([filter_grad, gate_grad], axis=1).astype(jnp.bfloat16)
    past_term = jnp.einsum("rc,rg->cg", flat_past, pre_grad, preferred_element_type=jnp.float32)
    now_term = jnp.einsum("rc,rg->cg", flat_now, pre_grad, preferred_element_type=jnp.float32)
    mix_term = jnp.einsum("rh,rc->hc", hidden, flat_up, preferred_element_type=jnp.float32)
    ahead_rows = (
        jnp.dot(pre_grad, tap_past.T, preferred_element_type=jnp.float32)
        .astype(jnp.bfloat16)
        .reshape(input_traces.shape)
    )
    local_grad = (
        flat_up.astype(jnp.float32)
        + jnp.dot(pre_grad, tap_now.T, preferred_element_type=jnp.float32)
    ).reshape(input_traces.shape)
    return (local_grad, ahead_rows, (past_term, now_term, mix_term))


def reduce_grads(term_list, scale_factor):
    past_term, now_term, mix_term = term_list
    summed = lax.psum((past_term, now_term, mix_term), ("dp", "tm"))
    return tuple(((member * scale_factor).astype(jnp.bfloat16) for member in summed))


def body(
    signal,
    cotangent,
    first_history_weight,
    first_current_weight,
    first_residual_weight,
    second_history_weight,
    second_current_weight,
    second_residual_weight,
):
    seq_count, number_of_steps, channels = signal.shape
    rows_all = seq_count * lax.axis_size("dp") * number_of_steps * lax.axis_size("tm")
    scale_factor = 1.0 / math.sqrt(rows_all)
    final_rows = signal[:, number_of_steps - FIRST_DILATION :, :]
    received_rows = shifted(final_rows, "tm", 1)
    first_history_rows = jnp.concatenate(
        [received_rows, signal[:, : number_of_steps - FIRST_DILATION, :]], axis=1
    )
    first_layer_stash = forward_layer(
        signal,
        first_history_rows,
        first_history_weight,
        first_current_weight,
        first_residual_weight,
    )
    hidden_activation = first_layer_stash[3]
    distant_offsets = SECOND_DILATION // number_of_steps
    past_two = shifted(hidden_activation, "tm", distant_offsets)
    second_layer_stash = forward_layer(
        hidden_activation,
        past_two,
        second_history_weight,
        second_current_weight,
        second_residual_weight,
    )
    local_two, ahead_two, second_layer_terms = backward_layer(
        hidden_activation,
        past_two,
        second_layer_stash,
        cotangent,
        second_history_weight,
        second_current_weight,
        second_residual_weight,
    )
    arrived_back = shifted(ahead_two, "tm", -distant_offsets)
    hidden_gradient = (local_two + arrived_back.astype(jnp.float32)).astype(jnp.bfloat16)
    reduced_two = reduce_grads(second_layer_terms, scale_factor)
    local_one, forward_rows_first, first_layer_terms = backward_layer(
        signal,
        first_history_rows,
        first_layer_stash,
        hidden_gradient,
        first_history_weight,
        first_current_weight,
        first_residual_weight,
    )
    leading_rows = forward_rows_first[:, :FIRST_DILATION, :]
    received_head_rows = shifted(leading_rows, "tm", -1)
    trailing_later_rows = jnp.concatenate(
        [forward_rows_first[:, FIRST_DILATION:, :], received_head_rows], axis=1
    )
    grad_signal = (local_one + trailing_later_rows.astype(jnp.float32)).astype(jnp.bfloat16)
    reduced_one = reduce_grads(first_layer_terms, scale_factor)
    return (
        grad_signal,
        reduced_one[0],
        reduced_one[1],
        reduced_one[2],
        reduced_two[0],
        reduced_two[1],
        reduced_two[2],
    )


def solution(mesh):
    in_specs = (P("dp", "tm", None), P("dp", "tm", None), P(), P(), P(), P(), P(), P())
    out_specs = (P("dp", "tm", None), P(), P(), P(), P(), P(), P())
    return jax.shard_map(body, mesh=mesh, in_specs=in_specs, out_specs=out_specs, check_vma=False)
```

profile of v0, /device:TPU:1, one launch (start us, length us, event | category | flops | bytes accessed | tf_op | source)
XLA Modules:
  0.0 615.3 jit_solution(2754087225272459337)
XLA Ops:
  7.2 1.1 fusion.28
  8.4 4.9 collective-permute-start
  13.3 1.6 fusion.17
  14.9 2.6 collective-permute-done
  18.5 0.6 copy-done.1
  19.5 7.9 %collective-permute-start.1 = (bf16[1,1024,256]{2,1,0:T(8,128)(2,1)S(1)}, bf16[1,1024,256]{2,1,0:T(8,128)(2,1)S(1)}, u32[]{:S(2)}, u32[]{:S(2)}) collective-permute-start(bf16[1,1024,256]{2,1,0:T(8,128)(2,1)S(1)} %bitcast.60), channel_id=1, source_target_pairs={{0,8},{1,9},{2,10},{3,11},{4,12},{5,13},{6,14},{7,15},{8,16},{9,17... | collective-permute-start | bytes 1572872 | tf_op jit(solution)/shard_map/ppermute | solution.py:15
  27.9 19.0 %collective-permute-done.1 = bf16[1,1024,256]{2,1,0:T(8,128)(2,1)S(1)} collective-permute-done((bf16[1,1024,256]{2,1,0:T(8,128)(2,1)S(1)}, bf16[1,1024,256]{2,1,0:T(8,128)(2,1)S(1)}, u32[]{:S(2)}, u32[]{:S(2)}) %collective-permute-start.1) | collective-permute-done | bytes 524320 | tf_op jit(solution)/shard_map/ppermute | solution.py:15
  47.4 0.7 multiply_convert_fusion.4
  48.1 1.3 fusion.26
  49.9 1.3 collective-permute-start.2
  51.2 1.3 fusion.13
  52.5 1.3 fusion.12
  53.7 10.9 %collective-permute-done.2 = bf16[1,1024,256]{2,1,0:T(8,128)(2,1)S(1)} collective-permute-done((bf16[1,1024,256]{2,1,0:T(8,128)(2,1)S(1)}, bf16[1,1024,256]{2,1,0:T(8,128)(2,1)S(1)}, u32[]{:S(2)}, u32[]{:S(2)}) %collective-permute-start.2) | collective-permute-done | bytes 524320 | tf_op jit(solution)/shard_map/ppermute | solution.py:15
  65.1 0.7 multiply_convert_fusion.2
  65.8 1.0 fusion.30
  66.8 1.3 convolution_bitcast_fusion
  68.1 1.3 fusion.22
  70.0 30.0 %collective-permute-start.3 = (bf16[1,512,256]{2,1,0:T(8,128)(2,1)S(1)}, bf16[1,512,256]{2,1,0:T(8,128)(2,1)S(1)}, u32[]{:S(2)}, u32[]{:S(2)}) collective-permute-start(bf16[1,512,256]{2,1,0:T(8,128)(2,1)S(1)} %get-tuple-element.18), channel_id=1, source_target_pairs={{1,0},{2,1},{3,2},{4,3},{5,4},{6,5},{7,6},{8,7},{9,8},{10,9},{11,1... | collective-permute-start | bytes 786440 | tf_op jit(solution)/shard_map/ppermute | solution.py:15
  100.0 1.1 collective-permute-done.3
  101.1 1.3 fusion.11
  102.4 501.1 %all-reduce.3.cloned.1.call-done = (f32[256,512]{1,0:T(8,128)}, f32[256,512]{1,0:T(8,128)}, f32[256,256]{1,0:T(8,128)}, f32[256,512]{1,0:T(8,128)}, f32[256,512]{1,0:T(8,128)}, /*index=5*/f32[256,256]{1,0:T(8,128)}) async-done(((f32[256,512]{1,0:T(8,128)}, f32[256,512]{1,0:T(8,128)}, f32[256,256]{1,0:T(8,128)}, f32[256,512]{1,0:T(8,128)}, f32[256,512]{1,0:T(8,128)}, /*index=5*/f32[256,256]{1,0:T(8,128)}), ...) | async-done | bytes 2621456 | tf_op jit(solution)/shard_map/psum | solution.py:62
  603.5 2.2 multiply_convert_fusion.9
  605.7 1.8 multiply_convert_fusion.11
  607.5 0.9 multiply_convert_fusion.7
  (30 shorter events, 3.9 us)
Async XLA Ops:
  7.2 39.7 %copy-start = (bf16[256,512]{1,0:T(8,128)(2,1)S(1)}, bf16[256,512]{1,0:T(8,128)(2,1)}, u32[]{:S(2)}) copy-start(bf16[256,512]{1,0:T(8,128)(2,1)} %param.13) | copy-start | bytes 786436
  7.2 10.4 %copy-start.4 = (bf16[256,512]{1,0:T(8,128)(2,1)S(1)}, bf16[256,512]{1,0:T(8,128)(2,1)}, u32[]{:S(2)}) copy-start(bf16[256,512]{1,0:T(8,128)(2,1)} %param.10) | copy-start | bytes 786436
  7.2 596.3 %all-reduce.3.cloned.1.call-start = ((), (), s32[]{:S(2)}) async-start(), calls=%async_computation | async-start | bytes 5242880 | tf_op jit(solution)/shard_map/psum | solution.py:62
  8.4 9.2 %collective-permute-start = (bf16[1,512,256]{2,1,0:T(8,128)(2,1)S(1)}, bf16[1,512,256]{2,1,0:T(8,128)(2,1)S(1)}, u32[]{:S(2)}, u32[]{:S(2)}) collective-permute-start(bf16[1,512,256]{2,1,0:T(8,128)(2,1)S(1)} %get-tuple-element.19), channel_id=1, source_target_pairs={{0,1},{1,2},{2,3},{3,4},{4,5},{5,6},{6,7},{7,8},{8,9},{9,10},{10,1... | collective-permute-start | bytes 786440 | tf_op jit(solution)/shard_map/ppermute | solution.py:15
  18.0 1.0 copy-start.1
  18.1 1.1 copy-start.7
  18.1 9.3 %copy-start.5 = (bf16[256,512]{1,0:T(8,128)(2,1)S(1)}, bf16[256,512]{1,0:T(8,128)(2,1)}, u32[]{:S(2)}) copy-start(bf16[256,512]{1,0:T(8,128)(2,1)} %param.14) | copy-start | bytes 786436
  19.5 27.4 %collective-permute-start.1 = (bf16[1,1024,256]{2,1,0:T(8,128)(2,1)S(1)}, bf16[1,1024,256]{2,1,0:T(8,128)(2,1)S(1)}, u32[]{:S(2)}, u32[]{:S(2)}) collective-permute-start(bf16[1,1024,256]{2,1,0:T(8,128)(2,1)S(1)} %bitcast.60), channel_id=1, source_target_pairs={{0,8},{1,9},{2,10},{3,11},{4,12},{5,13},{6,14},{7,15},{8,16},{9,17... | collective-permute-start | bytes 1572872 | tf_op jit(solution)/shard_map/ppermute | solution.py:15
  27.9 19.5 %copy-start.8 = (bf16[1,1024,256]{2,1,0:T(8,128)(2,1)S(1)}, bf16[1,1024,256]{2,1,0:T(8,128)(2,1)}, u32[]{:S(2)}) copy-start(bf16[1,1024,256]{2,1,0:T(8,128)(2,1)} %param.9) | copy-start | bytes 1572868
  27.9 19.5 %copy-start.9 = (bf16[256,256]{1,0:T(8,128)(2,1)S(1)}, bf16[256,256]{1,0:T(8,128)(2,1)}, u32[]{:S(2)}) copy-start(bf16[256,256]{1,0:T(8,128)(2,1)} %param.15) | copy-start | bytes 393220
  49.9 14.7 %collective-permute-start.2 = (bf16[1,1024,256]{2,1,0:T(8,128)(2,1)S(1)}, bf16[1,1024,256]{2,1,0:T(8,128)(2,1)S(1)}, u32[]{:S(2)}, u32[]{:S(2)}) collective-permute-start(bf16[1,1024,256]{2,1,0:T(8,128)(2,1)S(1)} %fusion.2), channel_id=1, source_target_pairs={{8,0},{9,1},{10,2},{11,3},{12,4},{13,5},{14,6},{15,7},{16,8},{17,9... | collective-permute-start | bytes 1572872 | tf_op jit(solution)/shard_map/ppermute | solution.py:15
  69.4 31.7 %copy-start.6 = (bf16[256,512]{1,0:T(8,128)(2,1)S(1)}, bf16[256,512]{1,0:T(8,128)(2,1)}, u32[]{:S(2)}) copy-start(bf16[256,512]{1,0:T(8,128)(2,1)} %param.11) | copy-start | bytes 786436
  70.0 31.1 %collective-permute-start.3 = (bf16[1,512,256]{2,1,0:T(8,128)(2,1)S(1)}, bf16[1,512,256]{2,1,0:T(8,128)(2,1)S(1)}, u32[]{:S(2)}, u32[]{:S(2)}) collective-permute-start(bf16[1,512,256]{2,1,0:T(8,128)(2,1)S(1)} %get-tuple-element.18), channel_id=1, source_target_pairs={{1,0},{2,1},{3,2},{4,3},{5,4},{6,5},{7,6},{8,7},{9,8},{10,9},{11,1... | collective-permute-start | bytes 786440 | tf_op jit(solution)/shard_map/ppermute | solution.py:15
  603.5 4.0 copy-start.2
  603.5 4.0 copy-start.3
Sparse Core Ops, SparseCore 0:
  69.5 533.9 all-reduce.2
where the time goes:
time: 617 us; the launch traced here: 615 us
  waiting for transfers between devices  535 us (87%)
  starting transfers between devices  44.2 us (7%)
  matrix products  14.9 us (2%)
  between operations  14.2 us (2%)
    psum x1, waiting for transfers between devices, reduce_grads(): summed = lax.psum((past_term, now_term, mix_term), ('dp', 'tm'))  501 us
    ppermute x4, starting transfers between devices, shifted(): lax.ppermute(value, axis, [(source, source + steps) for source in range(l...  44.1 us
    ppermute x4, waiting for transfers between devices, shifted(): lax.ppermute(value, axis, [(source, source + steps) for source in range(l...  33.6 us
  transfers between devices with their start and end apart: 5, of which 5 were waited for; matrix products, arithmetic and copies ran while one was open for 1% of the time, Pallas kernels for 0%

commit v1 on v0

--- a/solution.py
+++ b/solution.py
@@ -57,10 +57,39 @@
     return (local_grad, ahead_rows, (past_term, now_term, mix_term))
 
 
+REDUCE_STEPS = (("tm", 1), ("tm", 32), ("tm", 2), ("dp", 1), ("dp", 4), ("tm", 4), ("dp", 2), ("tm", 8), ("tm", 16))
+
+
+def exchange(value, axis, mask):
+    count = lax.axis_size(axis)
+    return lax.ppermute(value, axis, [(source, source ^ mask) for source in range(count)])
+
+
+def halving_sum(flat):
+    for axis, mask in REDUCE_STEPS:
+        half = flat.shape[0] // 2
+        upper = (lax.axis_index(axis) & mask) != 0
+        first, second = flat[:half], flat[half:]
+        kept = jnp.where(upper, second, first)
+        sent = jnp.where(upper, first, second)
+        flat = kept + exchange(sent, axis, mask)
+    for axis, mask in reversed(REDUCE_STEPS):
+        upper = (lax.axis_index(axis) & mask) != 0
+        other = exchange(flat, axis, mask)
+        flat = jnp.where(upper, jnp.concatenate([other, flat]), jnp.concatenate([flat, other]))
+    return flat
+
+
 def reduce_grads(term_list, scale_factor):
-    past_term, now_term, mix_term = term_list
-    summed = lax.psum((past_term, now_term, mix_term), ("dp", "tm"))
-    return tuple(((member * scale_factor).astype(jnp.bfloat16) for member in summed))
+    shapes = [member.shape for member in term_list]
+    flat = jnp.concatenate([member.reshape(-1, 128) for member in term_list])
+    summed = halving_sum(flat)
+    out, start = [], 0
+    for shape in shapes:
+        rows = shape[0] * shape[1] // 128
+        out.append((summed[start:start + rows].reshape(shape) * scale_factor).astype(jnp.bfloat16))
+        start += rows
+    return tuple(out)
 
 
 def body(
@@ -109,7 +138,6 @@
     )
     arrived_back = shifted(ahead_two, "tm", -distant_offsets)
     hidden_gradient = (local_two + arrived_back.astype(jnp.float32)).astype(jnp.bfloat16)
-    reduced_two = reduce_grads(second_layer_terms, scale_factor)
     local_one, forward_rows_first, first_layer_terms = backward_layer(
         signal,
         first_history_rows,
@@ -125,7 +153,8 @@
         [forward_rows_first[:, FIRST_DILATION:, :], received_head_rows], axis=1
     )
     grad_signal = (local_one + trailing_later_rows.astype(jnp.float32)).astype(jnp.bfloat16)
-    reduced_one = reduce_grads(first_layer_terms, scale_factor)
+    reduced = reduce_grads(tuple(first_layer_terms) + tuple(second_layer_terms), scale_factor)
+    reduced_one, reduced_two = reduced[:3], reduced[3:]
     return (
         grad_signal,
         reduced_one[0],

time: 617 us -> 316 us (0.51)
  waiting for transfers between devices: 535 us -> 103 us
  starting transfers between devices: 44.2 us -> 165 us
  local copies, waits for them, and re-layouts: 1.82 us -> 19.3 us
  between operations: 14.2 us -> 1.31 us
  matrix products: 14.9 us -> 21.5 us
    psum x1 -> x0, waiting for transfers between devices: 501 us -> none  [reduce_grads(): summed = lax.psum((past_term, now_term, mix_term), ('dp', 'tm'))]
    ppermute x0 -> x18, starting transfers between devices: none -> 148 us  [exchange(): lax.ppermute(value, axis, [(source, source ^ mask) for source in range(co...]
    ppermute x0 -> x18, waiting for transfers between devices: none -> 71.6 us  [exchange(): lax.ppermute(value, axis, [(source, source ^ mask) for source in range(co...]
    ppermute x4, starting transfers between devices: 44.1 us -> 16.8 us  [shifted(): lax.ppermute(value, axis, [(source, source + steps) for source in range(l...]
  transfers between devices with their start and end apart: 5 -> 22, of which waited for: 5 -> 21; matrix products, arithmetic and copies ran while one was open for 1% -> 4% of each run, Pallas kernels for 0% -> 0%
where the time goes in v1:
time: 316 us; the launch traced here: 313 us
  starting transfers between devices  165 us (52%)
  waiting for transfers between devices  103 us (33%)
  matrix products  21.5 us (7%)
  local copies, waits for them, and re-layouts  19.3 us (6%)
  other arithmetic  3.64 us (1%)
    ppermute x18, starting transfers between devices, exchange(): lax.ppermute(value, axis, [(source, source ^ mask) for source in range(co...  148 us
    ppermute x18, waiting for transfers between devices, exchange(): lax.ppermute(value, axis, [(source, source ^ mask) for source in range(co...  71.6 us
    ppermute x4, waiting for transfers between devices, shifted(): lax.ppermute(value, axis, [(source, source + steps) for source in range(l...  31.1 us
    ppermute x4, starting transfers between devices, shifted(): lax.ppermute(value, axis, [(source, source + steps) for source in range(l...  16.8 us
    unnamed x56, local copies, waits for them, and re-layouts  6.81 us
  transfers between devices with their start and end apart: 22, of which 21 were waited for; matrix products, arithmetic and copies ran while one was open for 4% of the time, Pallas kernels for 0%

profile of v1, /device:TPU:1, one launch (start us, length us, event | category | flops | bytes accessed | tf_op | source)
XLA Modules:
  0.0 313.5 jit_solution(12273478066638420397)
XLA Ops:
  1.8 4.9 %collective-permute-start = (bf16[1,512,256]{2,1,0:T(8,128)(2,1)S(1)}, bf16[1,512,256]{2,1,0:T(8,128)(2,1)S(1)}, u32[]{:S(2)}, u32[]{:S(2)}) collective-permute-start(bf16[1,512,256]{2,1,0:T(8,128)(2,1)S(1)} %get-tuple-element.19), channel_id=1, source_target_pairs={{0,1},{1,2},{2,3},{3,4},{4,5},{5,6},{6,7},{7,8},{8,9},{9,10},{10,1... | collective-permute-start | bytes 786440 | tf_op jit(solution)/shard_map/ppermute | solution.py:15
  13.9 8.7 %collective-permute-start.1 = (bf16[1,1024,256]{2,1,0:T(8,128)(2,1)}, bf16[1,1024,256]{2,1,0:T(8,128)(2,1)}, u32[]{:S(2)}, u32[]{:S(2)}) collective-permute-start(bf16[1,1024,256]{2,1,0:T(8,128)(2,1)} %bitcast.3), channel_id=1, source_target_pairs={{0,8},{1,9},{2,10},{3,11},{4,12},{5,13},{6,14},{7,15},{8,16},{9,17... | collective-permute-start | bytes 1572872 | tf_op jit(solution)/shard_map/ppermute | solution.py:15
  24.2 17.5 %collective-permute-done.1 = bf16[1,1024,256]{2,1,0:T(8,128)(2,1)} collective-permute-done((bf16[1,1024,256]{2,1,0:T(8,128)(2,1)}, bf16[1,1024,256]{2,1,0:T(8,128)(2,1)}, u32[]{:S(2)}, u32[]{:S(2)}) %collective-permute-start.1) | collective-permute-done | bytes 524320 | tf_op jit(solution)/shard_map/ppermute | solution.py:15
  64.3 5.2 %collective-permute-done.2 = bf16[1,1024,256]{2,1,0:T(8,128)(2,1)} collective-permute-done((bf16[1,1024,256]{2,1,0:T(8,128)(2,1)}, bf16[1,1024,256]{2,1,0:T(8,128)(2,1)}, u32[]{:S(2)}, u32[]{:S(2)}) %collective-permute-start.2) | collective-permute-done | bytes 524320 | tf_op jit(solution)/shard_map/ppermute | solution.py:15
  75.7 31.3 %collective-permute-start.4 = (f32[2560,128]{1,0:T(8,128)S(1)}, f32[2560,128]{1,0:T(8,128)}, u32[]{:S(2)}, u32[]{:S(2)}) collective-permute-start(f32[2560,128]{1,0:T(8,128)S(1)} %broadcast_select_fusion), channel_id=1, source_target_pairs={{0,1},{1,0},{2,3},{3,2},{4,5},{5,4},{6,7},{7,6},{8,9},{9,8},{10,11... | collective-permute-start | bytes 3932168 | tf_op jit(solution)/shard_map/ppermute | solution.py:65
  111.8 29.3 %collective-permute-start.5 = (f32[1280,128]{1,0:T(8,128)S(1)}, f32[1280,128]{1,0:T(8,128)S(1)}, u32[]{:S(2)}, u32[]{:S(2)}) collective-permute-start(f32[1280,128]{1,0:T(8,128)S(1)} %slice_select_fusion), channel_id=1, source_target_pairs={{0,32},{1,33},{2,34},{3,35},{4,36},{5,37},{6,38},{7,39},{8,40},{9,... | collective-permute-start | bytes 1966088 | tf_op jit(solution)/shard_map/ppermute | solution.py:65
  141.2 15.1 %collective-permute-done.5 = f32[1280,128]{1,0:T(8,128)S(1)} collective-permute-done((f32[1280,128]{1,0:T(8,128)S(1)}, f32[1280,128]{1,0:T(8,128)S(1)}, u32[]{:S(2)}, u32[]{:S(2)}) %collective-permute-start.5) | collective-permute-done | bytes 655392 | tf_op jit(solution)/shard_map/ppermute | solution.py:65
  158.6 8.4 %collective-permute-done.6 = f32[640,128]{1,0:T(8,128)S(1)} collective-permute-done((f32[640,128]{1,0:T(8,128)S(1)}, f32[640,128]{1,0:T(8,128)S(1)}, u32[]{:S(2)}, u32[]{:S(2)}) %collective-permute-start.6) | collective-permute-done | bytes 327712 | tf_op jit(solution)/shard_map/ppermute | solution.py:65
  169.3 3.8 %collective-permute-done.7 = f32[320,128]{1,0:T(8,128)S(1)} collective-permute-done((f32[320,128]{1,0:T(8,128)S(1)}, f32[320,128]{1,0:T(8,128)S(1)}, u32[]{:S(2)}, u32[]{:S(2)}) %collective-permute-start.7) | collective-permute-done | bytes 163872 | tf_op jit(solution)/shard_map/ppermute | solution.py:65
  173.2 4.5 %collective-permute-start.8 = (f32[160,128]{1,0:T(8,128)S(1)}, f32[160,128]{1,0:T(8,128)S(1)}, u32[]{:S(2)}, u32[]{:S(2)}) collective-permute-start(f32[160,128]{1,0:T(8,128)S(1)} %slice_select_fusion.3), channel_id=1, source_target_pairs={{0,256},{64,320},{128,384},{192,448},{256,0},{320,64},{384,128},{4... | collective-permute-start | bytes 245768 | tf_op jit(solution)/shard_map/ppermute | solution.py:65
  185.6 4.4 %collective-permute-start.10 = (f32[40,128]{1,0:T(8,128)S(1)}, f32[40,128]{1,0:T(8,128)S(1)}, u32[]{:S(2)}, u32[]{:S(2)}) collective-permute-start(f32[40,128]{1,0:T(8,128)S(1)} %slice_select_fusion.5), channel_id=1, source_target_pairs={{0,128},{64,192},{128,0},{192,64},{256,384},{320,448},{384,256},{4... | collective-permute-start | bytes 61448 | tf_op jit(solution)/shard_map/ppermute | solution.py:65
  191.7 7.4 %collective-permute-start.11 = (f32[20,128]{1,0:T(8,128)S(1)}, f32[20,128]{1,0:T(8,128)S(1)}, u32[]{:S(2)}, u32[]{:S(2)}) collective-permute-start(f32[20,128]{1,0:T(8,128)S(1)} %slice_select_fusion.6), channel_id=1, source_target_pairs={{0,8},{1,9},{2,10},{3,11},{4,12},{5,13},{6,14},{7,15},{8,0},{9,1},... | collective-permute-start | bytes 30728 | tf_op jit(solution)/shard_map/ppermute | solution.py:65
  200.2 8.3 %collective-permute-start.12 = (f32[10,128]{1,0:T(8,128)S(1)}, f32[10,128]{1,0:T(8,128)S(1)}, u32[]{:S(2)}, u32[]{:S(2)}) collective-permute-start(f32[10,128]{1,0:T(8,128)S(1)} %slice_select_fusion.7), channel_id=1, source_target_pairs={{0,16},{1,17},{2,18},{3,19},{4,20},{5,21},{6,22},{7,23},{8,24},{9,... | collective-permute-start | bytes 15368 | tf_op jit(solution)/shard_map/ppermute | solution.py:65
  208.5 4.8 %collective-permute-done.12 = f32[10,128]{1,0:T(8,128)S(1)} collective-permute-done((f32[10,128]{1,0:T(8,128)S(1)}, f32[10,128]{1,0:T(8,128)S(1)}, u32[]{:S(2)}, u32[]{:S(2)}) %collective-permute-start.12) | collective-permute-done | bytes 5152 | tf_op jit(solution)/shard_map/ppermute | solution.py:65
  213.3 8.3 %collective-permute-start.13 = (f32[10,128]{1,0:T(8,128)S(1)}, f32[10,128]{1,0:T(8,128)S(1)}, u32[]{:S(2)}, u32[]{:S(2)}) collective-permute-start(f32[10,128]{1,0:T(8,128)S(1)} %select_add_fusion.8), channel_id=1, source_target_pairs={{0,16},{1,17},{2,18},{3,19},{4,20},{5,21},{6,22},{7,23},{8,24},{9,... | collective-permute-start | bytes 15368 | tf_op jit(solution)/shard_map/ppermute | solution.py:65
  221.6 4.8 %collective-permute-done.13 = f32[10,128]{1,0:T(8,128)S(1)} collective-permute-done((f32[10,128]{1,0:T(8,128)S(1)}, f32[10,128]{1,0:T(8,128)S(1)}, u32[]{:S(2)}, u32[]{:S(2)}) %collective-permute-start.13) | collective-permute-done | bytes 5152 | tf_op jit(solution)/shard_map/ppermute | solution.py:65
  226.4 7.3 %collective-permute-start.14 = (f32[20,128]{1,0:T(8,128)S(1)}, f32[20,128]{1,0:T(8,128)S(1)}, u32[]{:S(2)}, u32[]{:S(2)}) collective-permute-start(f32[20,128]{1,0:T(8,128)S(1)} %maximum_select_fusion.8), channel_id=1, source_target_pairs={{0,8},{1,9},{2,10},{3,11},{4,12},{5,13},{6,14},{7,15},{8,0},{9,1},... | collective-permute-start | bytes 30728 | tf_op jit(solution)/shard_map/ppermute | solution.py:65
  235.1 4.6 %collective-permute-start.15 = (f32[40,128]{1,0:T(8,128)S(1)}, f32[40,128]{1,0:T(8,128)S(1)}, u32[]{:S(2)}, u32[]{:S(2)}) collective-permute-start(f32[40,128]{1,0:T(8,128)S(1)} %maximum_select_fusion.7), channel_id=1, source_target_pairs={{0,128},{64,192},{128,0},{192,64},{256,384},{320,448},{384,256},{4... | collective-permute-start | bytes 61448 | tf_op jit(solution)/shard_map/ppermute | solution.py:65
  243.4 3.3 %collective-permute-done.16 = f32[80,128]{1,0:T(8,128)S(1)} collective-permute-done((f32[80,128]{1,0:T(8,128)S(1)}, f32[80,128]{1,0:T(8,128)S(1)}, u32[]{:S(2)}, u32[]{:S(2)}) %collective-permute-start.16) | collective-permute-done | bytes 40992 | tf_op jit(solution)/shard_map/ppermute | solution.py:65
  246.7 4.9 %collective-permute-start.17 = (f32[160,128]{1,0:T(8,128)S(1)}, f32[160,128]{1,0:T(8,128)S(1)}, u32[]{:S(2)}, u32[]{:S(2)}) collective-permute-start(f32[160,128]{1,0:T(8,128)S(1)} %maximum_select_fusion.5), channel_id=1, source_target_pairs={{0,256},{64,320},{128,384},{192,448},{256,0},{320,64},{384,128},{4... | collective-permute-start | bytes 245768 | tf_op jit(solution)/shard_map/ppermute | solution.py:65
  262.8 4.8 %collective-permute-done.19 = f32[640,128]{1,0:T(8,128)S(1)} collective-permute-done((f32[640,128]{1,0:T(8,128)S(1)}, f32[640,128]{1,0:T(8,128)S(1)}, u32[]{:S(2)}, u32[]{:S(2)}) %collective-permute-start.19) | collective-permute-done | bytes 327712 | tf_op jit(solution)/shard_map/ppermute | solution.py:65
  270.6 8.3 %collective-permute-done.20 = f32[1280,128]{1,0:T(8,128)S(1)} collective-permute-done((f32[1280,128]{1,0:T(8,128)S(1)}, f32[1280,128]{1,0:T(8,128)S(1)}, u32[]{:S(2)}, u32[]{:S(2)}) %collective-permute-start.20) | collective-permute-done | bytes 655392 | tf_op jit(solution)/shard_map/ppermute | solution.py:65
  279.1 19.4 %collective-permute-start.21 = (f32[2560,128]{1,0:T(8,128)S(1)}, f32[2560,128]{1,0:T(8,128)S(1)}, u32[]{:S(2)}, u32[]{:S(2)}) collective-permute-start(f32[2560,128]{1,0:T(8,128)S(1)} %maximum_select_fusion.1), channel_id=1, source_target_pairs={{0,1},{1,0},{2,3},{3,2},{4,5},{5,4},{6,7},{7,6},{8,9},{9,8},{10,11... | collective-permute-start | bytes 3932168 | tf_op jit(solution)/shard_map/ppermute | solution.py:65
  301.0 5.8 %collective-permute-done.3 = bf16[1,512,256]{2,1,0:T(8,128)(2,1)S(1)} collective-permute-done((bf16[1,512,256]{2,1,0:T(8,128)(2,1)S(1)}, bf16[1,512,256]{2,1,0:T(8,128)(2,1)S(1)}, u32[]{:S(2)}, u32[]{:S(2)}) %collective-permute-start.3) | collective-permute-done | bytes 262176 | tf_op jit(solution)/shard_map/ppermute | solution.py:15
  (139 shorter events, 87.1 us)
Async XLA Ops:
  0.6 41.0 %copy-start = (bf16[256,512]{1,0:T(8,128)(2,1)S(1)}, bf16[256,512]{1,0:T(8,128)(2,1)}, u32[]{:S(2)}) copy-start(bf16[256,512]{1,0:T(8,128)(2,1)} %param.13) | copy-start | bytes 786436
  1.8 9.2 %collective-permute-start = (bf16[1,512,256]{2,1,0:T(8,128)(2,1)S(1)}, bf16[1,512,256]{2,1,0:T(8,128)(2,1)S(1)}, u32[]{:S(2)}, u32[]{:S(2)}) collective-permute-start(bf16[1,512,256]{2,1,0:T(8,128)(2,1)S(1)} %get-tuple-element.19), channel_id=1, source_target_pairs={{0,1},{1,2},{2,3},{3,4},{4,5},{5,6},{6,7},{7,8},{8,9},{9,10},{10,1... | collective-permute-start | bytes 786440 | tf_op jit(solution)/shard_map/ppermute | solution.py:15
  13.9 27.7 %collective-permute-start.1 = (bf16[1,1024,256]{2,1,0:T(8,128)(2,1)}, bf16[1,1024,256]{2,1,0:T(8,128)(2,1)}, u32[]{:S(2)}, u32[]{:S(2)}) collective-permute-start(bf16[1,1024,256]{2,1,0:T(8,128)(2,1)} %bitcast.3), channel_id=1, source_target_pairs={{0,8},{1,9},{2,10},{3,11},{4,12},{5,13},{6,14},{7,15},{8,16},{9,17... | collective-permute-start | bytes 1572872 | tf_op jit(solution)/shard_map/ppermute | solution.py:15
  54.6 15.0 %collective-permute-start.2 = (bf16[1,1024,256]{2,1,0:T(8,128)(2,1)}, bf16[1,1024,256]{2,1,0:T(8,128)(2,1)}, u32[]{:S(2)}, u32[]{:S(2)}) collective-permute-start(bf16[1,1024,256]{2,1,0:T(8,128)(2,1)} %fusion.2), channel_id=1, source_target_pairs={{8,0},{9,1},{10,2},{11,3},{12,4},{13,5},{14,6},{15,7},{16,8},{17,9... | collective-permute-start | bytes 1572872 | tf_op jit(solution)/shard_map/ppermute | solution.py:15
  75.7 34.1 %collective-permute-start.4 = (f32[2560,128]{1,0:T(8,128)S(1)}, f32[2560,128]{1,0:T(8,128)}, u32[]{:S(2)}, u32[]{:S(2)}) collective-permute-start(f32[2560,128]{1,0:T(8,128)S(1)} %broadcast_select_fusion), channel_id=1, source_target_pairs={{0,1},{1,0},{2,3},{3,2},{4,5},{5,4},{6,7},{7,6},{8,9},{9,8},{10,11... | collective-permute-start | bytes 3932168 | tf_op jit(solution)/shard_map/ppermute | solution.py:65
  111.8 44.5 %collective-permute-start.5 = (f32[1280,128]{1,0:T(8,128)S(1)}, f32[1280,128]{1,0:T(8,128)S(1)}, u32[]{:S(2)}, u32[]{:S(2)}) collective-permute-start(f32[1280,128]{1,0:T(8,128)S(1)} %slice_select_fusion), channel_id=1, source_target_pairs={{0,32},{1,33},{2,34},{3,35},{4,36},{5,37},{6,38},{7,39},{8,40},{9,... | collective-permute-start | bytes 1966088 | tf_op jit(solution)/shard_map/ppermute | solution.py:65
  156.4 10.6 %collective-permute-start.6 = (f32[640,128]{1,0:T(8,128)S(1)}, f32[640,128]{1,0:T(8,128)S(1)}, u32[]{:S(2)}, u32[]{:S(2)}) collective-permute-start(f32[640,128]{1,0:T(8,128)S(1)} %slice_select_fusion.1), channel_id=1, source_target_pairs={{0,2},{1,3},{2,0},{3,1},{4,6},{5,7},{6,4},{7,5},{8,10},{9,11},{10,... | collective-permute-start | bytes 983048 | tf_op jit(solution)/shard_map/ppermute | solution.py:65
  167.1 6.1 %collective-permute-start.7 = (f32[320,128]{1,0:T(8,128)S(1)}, f32[320,128]{1,0:T(8,128)S(1)}, u32[]{:S(2)}, u32[]{:S(2)}) collective-permute-start(f32[320,128]{1,0:T(8,128)S(1)} %slice_select_fusion.2), channel_id=1, source_target_pairs={{0,64},{64,0},{128,192},{192,128},{256,320},{320,256},{384,448},{4... | collective-permute-start | bytes 491528 | tf_op jit(solution)/shard_map/ppermute | solution.py:65
  173.2 6.7 %collective-permute-start.8 = (f32[160,128]{1,0:T(8,128)S(1)}, f32[160,128]{1,0:T(8,128)S(1)}, u32[]{:S(2)}, u32[]{:S(2)}) collective-permute-start(f32[160,128]{1,0:T(8,128)S(1)} %slice_select_fusion.3), channel_id=1, source_target_pairs={{0,256},{64,320},{128,384},{192,448},{256,0},{320,64},{384,128},{4... | collective-permute-start | bytes 245768 | tf_op jit(solution)/shard_map/ppermute | solution.py:65
  180.0 5.6 %collective-permute-start.9 = (f32[80,128]{1,0:T(8,128)S(1)}, f32[80,128]{1,0:T(8,128)S(1)}, u32[]{:S(2)}, u32[]{:S(2)}) collective-permute-start(f32[80,128]{1,0:T(8,128)S(1)} %slice_select_fusion.4), channel_id=1, source_target_pairs={{0,4},{1,5},{2,6},{3,7},{4,0},{5,1},{6,2},{7,3},{8,12},{9,13},{10,... | collective-permute-start | bytes 122888 | tf_op jit(solution)/shard_map/ppermute | solution.py:65
  185.6 6.0 %collective-permute-start.10 = (f32[40,128]{1,0:T(8,128)S(1)}, f32[40,128]{1,0:T(8,128)S(1)}, u32[]{:S(2)}, u32[]{:S(2)}) collective-permute-start(f32[40,128]{1,0:T(8,128)S(1)} %slice_select_fusion.5), channel_id=1, source_target_pairs={{0,128},{64,192},{128,0},{192,64},{256,384},{320,448},{384,256},{4... | collective-permute-start | bytes 61448 | tf_op jit(solution)/shard_map/ppermute | solution.py:65
  191.7 8.5 %collective-permute-start.11 = (f32[20,128]{1,0:T(8,128)S(1)}, f32[20,128]{1,0:T(8,128)S(1)}, u32[]{:S(2)}, u32[]{:S(2)}) collective-permute-start(f32[20,128]{1,0:T(8,128)S(1)} %slice_select_fusion.6), channel_id=1, source_target_pairs={{0,8},{1,9},{2,10},{3,11},{4,12},{5,13},{6,14},{7,15},{8,0},{9,1},... | collective-permute-start | bytes 30728 | tf_op jit(solution)/shard_map/ppermute | solution.py:65
  200.2 13.1 %collective-permute-start.12 = (f32[10,128]{1,0:T(8,128)S(1)}, f32[10,128]{1,0:T(8,128)S(1)}, u32[]{:S(2)}, u32[]{:S(2)}) collective-permute-start(f32[10,128]{1,0:T(8,128)S(1)} %slice_select_fusion.7), channel_id=1, source_target_pairs={{0,16},{1,17},{2,18},{3,19},{4,20},{5,21},{6,22},{7,23},{8,24},{9,... | collective-permute-start | bytes 15368 | tf_op jit(solution)/shard_map/ppermute | solution.py:65
  213.3 13.1 %collective-permute-start.13 = (f32[10,128]{1,0:T(8,128)S(1)}, f32[10,128]{1,0:T(8,128)S(1)}, u32[]{:S(2)}, u32[]{:S(2)}) collective-permute-start(f32[10,128]{1,0:T(8,128)S(1)} %select_add_fusion.8), channel_id=1, source_target_pairs={{0,16},{1,17},{2,18},{3,19},{4,20},{5,21},{6,22},{7,23},{8,24},{9,... | collective-permute-start | bytes 15368 | tf_op jit(solution)/shard_map/ppermute | solution.py:65
  226.4 8.6 %collective-permute-start.14 = (f32[20,128]{1,0:T(8,128)S(1)}, f32[20,128]{1,0:T(8,128)S(1)}, u32[]{:S(2)}, u32[]{:S(2)}) collective-permute-start(f32[20,128]{1,0:T(8,128)S(1)} %maximum_select_fusion.8), channel_id=1, source_target_pairs={{0,8},{1,9},{2,10},{3,11},{4,12},{5,13},{6,14},{7,15},{8,0},{9,1},... | collective-permute-start | bytes 30728 | tf_op jit(solution)/shard_map/ppermute | solution.py:65
  235.1 6.0 %collective-permute-start.15 = (f32[40,128]{1,0:T(8,128)S(1)}, f32[40,128]{1,0:T(8,128)S(1)}, u32[]{:S(2)}, u32[]{:S(2)}) collective-permute-start(f32[40,128]{1,0:T(8,128)S(1)} %maximum_select_fusion.7), channel_id=1, source_target_pairs={{0,128},{64,192},{128,0},{192,64},{256,384},{320,448},{384,256},{4... | collective-permute-start | bytes 61448 | tf_op jit(solution)/shard_map/ppermute | solution.py:65
  241.1 5.6 %collective-permute-start.16 = (f32[80,128]{1,0:T(8,128)S(1)}, f32[80,128]{1,0:T(8,128)S(1)}, u32[]{:S(2)}, u32[]{:S(2)}) collective-permute-start(f32[80,128]{1,0:T(8,128)S(1)} %maximum_select_fusion.6), channel_id=1, source_target_pairs={{0,4},{1,5},{2,6},{3,7},{4,0},{5,1},{6,2},{7,3},{8,12},{9,13},{10,... | collective-permute-start | bytes 122888 | tf_op jit(solution)/shard_map/ppermute | solution.py:65
  246.7 6.7 %collective-permute-start.17 = (f32[160,128]{1,0:T(8,128)S(1)}, f32[160,128]{1,0:T(8,128)S(1)}, u32[]{:S(2)}, u32[]{:S(2)}) collective-permute-start(f32[160,128]{1,0:T(8,128)S(1)} %maximum_select_fusion.5), channel_id=1, source_target_pairs={{0,256},{64,320},{128,384},{192,448},{256,0},{320,64},{384,128},{4... | collective-permute-start | bytes 245768 | tf_op jit(solution)/shard_map/ppermute | solution.py:65
  253.5 6.1 %collective-permute-start.18 = (f32[320,128]{1,0:T(8,128)S(1)}, f32[320,128]{1,0:T(8,128)S(1)}, u32[]{:S(2)}, u32[]{:S(2)}) collective-permute-start(f32[320,128]{1,0:T(8,128)S(1)} %maximum_select_fusion.4), channel_id=1, source_target_pairs={{0,64},{64,0},{128,192},{192,128},{256,320},{320,256},{384,448},{4... | collective-permute-start | bytes 491528 | tf_op jit(solution)/shard_map/ppermute | solution.py:65
  259.5 38.9 %copy-start.9 = (bf16[256,512]{1,0:T(8,128)(2,1)S(1)}, bf16[256,512]{1,0:T(8,128)(2,1)}, u32[]{:S(2)}) copy-start(bf16[256,512]{1,0:T(8,128)(2,1)} %param.10) | copy-start | bytes 786436
  259.6 8.0 %collective-permute-start.19 = (f32[640,128]{1,0:T(8,128)S(1)}, f32[640,128]{1,0:T(8,128)S(1)}, u32[]{:S(2)}, u32[]{:S(2)}) collective-permute-start(f32[640,128]{1,0:T(8,128)S(1)} %maximum_select_fusion.3), channel_id=1, source_target_pairs={{0,2},{1,3},{2,0},{3,1},{4,6},{5,7},{6,4},{7,5},{8,10},{9,11},{10,... | collective-permute-start | bytes 983048 | tf_op jit(solution)/shard_map/ppermute | solution.py:65
  267.6 11.3 %collective-permute-start.20 = (f32[1280,128]{1,0:T(8,128)S(1)}, f32[1280,128]{1,0:T(8,128)S(1)}, u32[]{:S(2)}, u32[]{:S(2)}) collective-permute-start(f32[1280,128]{1,0:T(8,128)S(1)} %maximum_select_fusion.2), channel_id=1, source_target_pairs={{0,32},{1,33},{2,34},{3,35},{4,36},{5,37},{6,38},{7,39},{8,40},{9,... | collective-permute-start | bytes 1966088 | tf_op jit(solution)/shard_map/ppermute | solution.py:65
  279.1 29.0 %collective-permute-start.21 = (f32[2560,128]{1,0:T(8,128)S(1)}, f32[2560,128]{1,0:T(8,128)S(1)}, u32[]{:S(2)}, u32[]{:S(2)}) collective-permute-start(f32[2560,128]{1,0:T(8,128)S(1)} %maximum_select_fusion.1), channel_id=1, source_target_pairs={{0,1},{1,0},{2,3},{3,2},{4,5},{5,4},{6,7},{7,6},{8,9},{9,8},{10,11... | collective-permute-start | bytes 3932168 | tf_op jit(solution)/shard_map/ppermute | solution.py:65
  299.0 7.7 %collective-permute-start.3 = (bf16[1,512,256]{2,1,0:T(8,128)(2,1)S(1)}, bf16[1,512,256]{2,1,0:T(8,128)(2,1)S(1)}, u32[]{:S(2)}, u32[]{:S(2)}) collective-permute-start(bf16[1,512,256]{2,1,0:T(8,128)(2,1)S(1)} %get-tuple-element.18), channel_id=1, source_target_pairs={{1,0},{2,1},{3,2},{4,3},{5,4},{6,5},{7,6},{8,7},{9,8},{10,9},{11,1... | collective-permute-start | bytes 786440 | tf_op jit(solution)/shard_map/ppermute | solution.py:15
  (24 other events, 245.9 us)

commit v2 on v0

--- a/solution.py
+++ b/solution.py
@@ -57,10 +57,58 @@
     return (local_grad, ahead_rows, (past_term, now_term, mix_term))
 
 
+ROUNDS = ((1,), (32, 64), (2, 4), (256, 128), (8, 16))
+AXES = ("dp", "tm")
+
+
+def spread(code, bits):
+    return sum(bit for place, bit in enumerate(bits) if code >> place & 1)
+
+
+def position(bits):
+    index = lax.axis_index(AXES)
+    return sum(((index // bit) % 2) << place for place, bit in enumerate(bits))
+
+
+def partner_pairs(mask):
+    count = lax.axis_size(AXES)
+    return [(source, source ^ mask) for source in range(count)]
+
+
+def scatter_round(flat, bits):
+    ways = 1 << len(bits)
+    me = position(bits)
+    pieces = flat.reshape((ways, flat.shape[0] // ways) + flat.shape[1:])
+    total = lax.dynamic_index_in_dim(pieces, me, keepdims=False)
+    for code in range(1, ways):
+        sent = lax.dynamic_index_in_dim(pieces, me ^ code, keepdims=False)
+        total = total + lax.ppermute(sent, AXES, partner_pairs(spread(code, bits)))
+    return total
+
+
+def gather_round(piece, bits):
+    ways = 1 << len(bits)
+    me = position(bits)
+    arrived = [piece] + [lax.ppermute(piece, AXES, partner_pairs(spread(code, bits))) for code in range(1, ways)]
+    stacked = jnp.stack(arrived)
+    order = jnp.arange(ways) ^ me
+    return jnp.take(stacked, order, axis=0).reshape((-1,) + piece.shape[1:])
+
+
 def reduce_grads(term_list, scale_factor):
-    past_term, now_term, mix_term = term_list
-    summed = lax.psum((past_term, now_term, mix_term), ("dp", "tm"))
-    return tuple(((member * scale_factor).astype(jnp.bfloat16) for member in summed))
+    shapes = [member.shape for member in term_list]
+    flat = jnp.concatenate([member.reshape(-1, 128) for member in term_list])
+    for bits in ROUNDS:
+        flat = scatter_round(flat, bits)
+    flat = (flat * scale_factor).astype(jnp.bfloat16)
+    for bits in reversed(ROUNDS):
+        flat = gather_round(flat, bits)
+    out, start = [], 0
+    for shape in shapes:
+        rows = shape[0] * shape[1] // 128
+        out.append(flat[start:start + rows].reshape(shape))
+        start += rows
+    return tuple(out)
 
 
 def body(
@@ -109,7 +157,6 @@
     )
     arrived_back = shifted(ahead_two, "tm", -distant_offsets)
     hidden_gradient = (local_two + arrived_back.astype(jnp.float32)).astype(jnp.bfloat16)
-    reduced_two = reduce_grads(second_layer_terms, scale_factor)
     local_one, forward_rows_first, first_layer_terms = backward_layer(
         signal,
         first_history_rows,
@@ -125,7 +172,8 @@
         [forward_rows_first[:, FIRST_DILATION:, :], received_head_rows], axis=1
     )
     grad_signal = (local_one + trailing_later_rows.astype(jnp.float32)).astype(jnp.bfloat16)
-    reduced_one = reduce_grads(first_layer_terms, scale_factor)
+    reduced = reduce_grads(tuple(first_layer_terms) + tuple(second_layer_terms), scale_factor)
+    reduced_one, reduced_two = reduced[:3], reduced[3:]
     return (
         grad_signal,
         reduced_one[0],

time: 617 us -> 303 us (0.49)
  waiting for transfers between devices: 535 us -> 67.2 us
  starting transfers between devices: 44.2 us -> 178 us
  local copies, waits for them, and re-layouts: 1.82 us -> 24.7 us
  between operations: 14.2 us -> 1.9 us
  matrix products: 14.9 us -> 22 us
    psum x1 -> x0, waiting for transfers between devices: 501 us -> none  [reduce_grads(): summed = lax.psum((past_term, now_term, mix_term), ('dp', 'tm'))]
    ppermute x0 -> x26, starting transfers between devices: none -> 159 us  [the longest x13 101 us: scatter_round(): total = total + lax.ppermute(sent, AXES, partner_pairs(spread(code, bits)))]
    ppermute x0 -> x26, waiting for transfers between devices: none -> 42.5 us  [the longest x13 29.2 us: scatter_round(): total = total + lax.ppermute(sent, AXES, partner_pairs(spread(code, bits)))]
    ppermute x4, starting transfers between devices: 44.1 us -> 18.5 us  [shifted(): lax.ppermute(value, axis, [(source, source + steps) for source in range(l...]
    reshape x0 -> x13, local copies, waits for them, and re-layouts: none -> 12.7 us  [the longest x6 7.81 us: reduce_grads(): flat = jnp.concatenate([member.reshape(-1, 128) for member in term_list])]
    ppermute x4, waiting for transfers between devices: 33.6 us -> 24.7 us  [shifted(): lax.ppermute(value, axis, [(source, source + steps) for source in range(l...]
  transfers between devices with their start and end apart: 5 -> 30, of which waited for: 5 -> 19; matrix products, arithmetic and copies ran while one was open for 1% -> 6% of each run, Pallas kernels for 0% -> 0%
where the time goes in v2:
time: 303 us; the launch traced here: 302 us
  starting transfers between devices  178 us (59%)
  waiting for transfers between devices  67.2 us (22%)
  local copies, waits for them, and re-layouts  24.7 us (8%)
  matrix products  22 us (7%)
  other arithmetic  8.35 us (3%)
    ppermute x13, starting transfers between devices, scatter_round(): total = total + lax.ppermute(sent, AXES, partner_pairs(spread(code, bits)))  101 us
    ppermute x13, starting transfers between devices, gather_round(): lax.ppermute(piece, AXES, partner_pairs(spread(code, bits)))  57.9 us
    ppermute x13, waiting for transfers between devices, scatter_round(): total = total + lax.ppermute(sent, AXES, partner_pairs(spread(code, bits)))  29.2 us
    ppermute x4, waiting for transfers between devices, shifted(): lax.ppermute(value, axis, [(source, source + steps) for source in range(l...  24.7 us
    ppermute x4, starting transfers between devices, shifted(): lax.ppermute(value, axis, [(source, source + steps) for source in range(l...  18.5 us
    ppermute x13, waiting for transfers between devices, gather_round(): lax.ppermute(piece, AXES, partner_pairs(spread(code, bits)))  13.3 us
    reshape x6, local copies, waits for them, and re-layouts, reduce_grads(): flat = jnp.concatenate([member.reshape(-1, 128) for member in term_list])  7.81 us
  transfers between devices with their start and end apart: 30, of which 19 were waited for; matrix products, arithmetic and copies ran while one was open for 6% of the time, Pallas kernels for 0%

profile of v2, /device:TPU:1, one launch (start us, length us, event | category | flops | bytes accessed | tf_op | source)
XLA Modules:
  0.0 301.9 jit_solution(18056241308848910167)
XLA Ops:
  1.8 4.9 %collective-permute-start = (bf16[1,512,256]{2,1,0:T(8,128)(2,1)S(1)}, bf16[1,512,256]{2,1,0:T(8,128)(2,1)S(1)}, u32[]{:S(2)}, u32[]{:S(2)}) collective-permute-start(bf16[1,512,256]{2,1,0:T(8,128)(2,1)S(1)} %get-tuple-element.22), channel_id=1, source_target_pairs={{0,1},{1,2},{2,3},{3,4},{4,5},{5,6},{6,7},{7,8},{8,9},{9,10},{10,1... | collective-permute-start | bytes 786440 | tf_op jit(solution)/shard_map/ppermute | solution.py:15
  13.9 8.7 %collective-permute-start.1 = (bf16[1,1024,256]{2,1,0:T(8,128)(2,1)}, bf16[1,1024,256]{2,1,0:T(8,128)(2,1)}, u32[]{:S(2)}, u32[]{:S(2)}) collective-permute-start(bf16[1,1024,256]{2,1,0:T(8,128)(2,1)} %bitcast.3), channel_id=1, source_target_pairs={{0,8},{1,9},{2,10},{3,11},{4,12},{5,13},{6,14},{7,15},{8,16},{9,17... | collective-permute-start | bytes 1572872 | tf_op jit(solution)/shard_map/ppermute | solution.py:15
  24.2 17.4 %collective-permute-done.1 = bf16[1,1024,256]{2,1,0:T(8,128)(2,1)} collective-permute-done((bf16[1,1024,256]{2,1,0:T(8,128)(2,1)}, bf16[1,1024,256]{2,1,0:T(8,128)(2,1)}, u32[]{:S(2)}, u32[]{:S(2)}) %collective-permute-start.1) | collective-permute-done | bytes 524320 | tf_op jit(solution)/shard_map/ppermute | solution.py:15
  61.1 4.6 %collective-permute-done.2 = bf16[1,1024,256]{2,1,0:T(8,128)(2,1)} collective-permute-done((bf16[1,1024,256]{2,1,0:T(8,128)(2,1)}, bf16[1,1024,256]{2,1,0:T(8,128)(2,1)}, u32[]{:S(2)}, u32[]{:S(2)}) %collective-permute-start.2) | collective-permute-done | bytes 524320 | tf_op jit(solution)/shard_map/ppermute | solution.py:15
  76.8 30.0 %collective-permute-start.4 = (f32[2560,128]{1,0:T(8,128)}, f32[2560,128]{1,0:T(8,128)}, u32[]{:S(2)}, u32[]{:S(2)}) collective-permute-start(f32[2560,128]{1,0:T(8,128)} %dynamic-slice_bitcast_fusion), channel_id=1, source_target_pairs={{0,1},{1,0},{2,3},{3,2},{4,5},{5,4},{6,7},{7,6},{8,9},{9,8},{10,11... | collective-permute-start | bytes 3932168 | tf_op jit(solution)/shard_map/ppermute | solution.py:85
  111.3 29.4 %collective-permute-start.5 = (f32[640,128]{1,0:T(8,128)S(1)}, f32[640,128]{1,0:T(8,128)S(1)}, u32[]{:S(2)}, u32[]{:S(2)}) collective-permute-start(f32[640,128]{1,0:T(8,128)S(1)} %get-tuple-element.17), channel_id=1, source_target_pairs={{0,32},{1,33},{2,34},{3,35},{4,36},{5,37},{6,38},{7,39},{8,40},{9,... | collective-permute-start | bytes 983048 | tf_op jit(solution)/shard_map/ppermute | solution.py:85
  148.5 8.1 %collective-permute-done.7 = f32[640,128]{1,0:T(8,128)S(1)} collective-permute-done((f32[640,128]{1,0:T(8,128)S(1)}, f32[640,128]{1,0:T(8,128)S(1)}, u32[]{:S(2)}, u32[]{:S(2)}) %collective-permute-start.7) | collective-permute-done | bytes 327712 | tf_op jit(solution)/shard_map/ppermute | solution.py:85
  156.6 4.6 %collective-permute-done.6 = f32[640,128]{1,0:T(8,128)S(1)} collective-permute-done((f32[640,128]{1,0:T(8,128)S(1)}, f32[640,128]{1,0:T(8,128)S(1)}, u32[]{:S(2)}, u32[]{:S(2)}) %collective-permute-start.6) | collective-permute-done | bytes 327712 | tf_op jit(solution)/shard_map/ppermute | solution.py:85
  166.0 3.8 %collective-permute-start.9 = (f32[160,128]{1,0:T(8,128)S(1)}, f32[160,128]{1,0:T(8,128)S(1)}, u32[]{:S(2)}, u32[]{:S(2)}) collective-permute-start(f32[160,128]{1,0:T(8,128)S(1)} %get-tuple-element.26), channel_id=1, source_target_pairs={{0,4},{1,5},{2,6},{3,7},{4,0},{5,1},{6,2},{7,3},{8,12},{9,13},{10,... | collective-permute-start | bytes 245768 | tf_op jit(solution)/shard_map/ppermute | solution.py:85
  170.5 5.5 %collective-permute-done.9 = f32[160,128]{1,0:T(8,128)S(1)} collective-permute-done((f32[160,128]{1,0:T(8,128)S(1)}, f32[160,128]{1,0:T(8,128)S(1)}, u32[]{:S(2)}, u32[]{:S(2)}) %collective-permute-start.9) | collective-permute-done | bytes 81952 | tf_op jit(solution)/shard_map/ppermute | solution.py:85
  176.0 5.3 %collective-permute-start.11 = (f32[40,128]{1,0:T(8,128)S(1)}, f32[40,128]{1,0:T(8,128)S(1)}, u32[]{:S(2)}, u32[]{:S(2)}) collective-permute-start(f32[40,128]{1,0:T(8,128)S(1)} %get-tuple-element.27), channel_id=1, source_target_pairs={{0,256},{1,257},{2,258},{3,259},{4,260},{5,261},{6,262},{7,263},{8... | collective-permute-start | bytes 61448 | tf_op jit(solution)/shard_map/ppermute | solution.py:85
  181.3 4.3 %collective-permute-start.13 = (f32[40,128]{1,0:T(8,128)S(1)}, f32[40,128]{1,0:T(8,128)S(1)}, u32[]{:S(2)}, u32[]{:S(2)}) collective-permute-start(f32[40,128]{1,0:T(8,128)S(1)} %get-tuple-element.28), channel_id=1, source_target_pairs={{0,384},{1,385},{2,386},{3,387},{4,388},{5,389},{6,390},{7,391},{8... | collective-permute-start | bytes 61448 | tf_op jit(solution)/shard_map/ppermute | solution.py:85
  187.8 3.6 %collective-permute-start.3 = (bf16[1,512,256]{2,1,0:T(8,128)(2,1)S(1)}, bf16[1,512,256]{2,1,0:T(8,128)(2,1)S(1)}, u32[]{:S(2)}, u32[]{:S(2)}) collective-permute-start(bf16[1,512,256]{2,1,0:T(8,128)(2,1)S(1)} %get-tuple-element.21), channel_id=1, source_target_pairs={{1,0},{2,1},{3,2},{4,3},{5,4},{6,5},{7,6},{8,7},{9,8},{10,9},{11,1... | collective-permute-start | bytes 786440 | tf_op jit(solution)/shard_map/ppermute | solution.py:15
  191.9 6.3 %collective-permute-start.14 = (f32[10,128]{1,0:T(8,128)S(1)}, f32[10,128]{1,0:T(8,128)S(1)}, u32[]{:S(2)}, u32[]{:S(2)}) collective-permute-start(f32[10,128]{1,0:T(8,128)S(1)} %get-tuple-element.30), channel_id=1, source_target_pairs={{0,8},{1,9},{2,10},{3,11},{4,12},{5,13},{6,14},{7,15},{8,0},{9,1},... | collective-permute-start | bytes 15368 | tf_op jit(solution)/shard_map/ppermute | solution.py:85
  201.6 7.0 %collective-permute-start.15 = (f32[10,128]{1,0:T(8,128)S(1)}, f32[10,128]{1,0:T(8,128)S(1)}, u32[]{:S(2)}, u32[]{:S(2)}) collective-permute-start(f32[10,128]{1,0:T(8,128)S(1)} %get-tuple-element.32), channel_id=1, source_target_pairs={{0,16},{1,17},{2,18},{3,19},{4,20},{5,21},{6,22},{7,23},{8,24},{9,... | collective-permute-start | bytes 15368 | tf_op jit(solution)/shard_map/ppermute | solution.py:85
  209.3 5.4 %collective-permute-done.15 = f32[10,128]{1,0:T(8,128)S(1)} collective-permute-done((f32[10,128]{1,0:T(8,128)S(1)}, f32[10,128]{1,0:T(8,128)S(1)}, u32[]{:S(2)}, u32[]{:S(2)}) %collective-permute-start.15) | collective-permute-done | bytes 5152 | tf_op jit(solution)/shard_map/ppermute | solution.py:85
  214.7 5.8 %collective-permute-start.19 = (bf16[10,128]{1,0:T(8,128)(2,1)S(1)}, bf16[10,128]{1,0:T(8,128)(2,1)S(1)}, u32[]{:S(2)}, u32[]{:S(2)}) collective-permute-start(bf16[10,128]{1,0:T(8,128)(2,1)S(1)} %fusion.32), channel_id=1, source_target_pairs={{0,24},{1,25},{2,26},{3,27},{4,28},{5,29},{6,30},{7,31},{8,16},{9,... | collective-permute-start | bytes 7688 | tf_op jit(solution)/shard_map/ppermute | solution.py:92
  220.5 8.4 %collective-permute-start.18 = (bf16[10,128]{1,0:T(8,128)(2,1)S(1)}, bf16[10,128]{1,0:T(8,128)(2,1)S(1)}, u32[]{:S(2)}, u32[]{:S(2)}) collective-permute-start(bf16[10,128]{1,0:T(8,128)(2,1)S(1)} %fusion.32), channel_id=1, source_target_pairs={{0,16},{1,17},{2,18},{3,19},{4,20},{5,21},{6,22},{7,23},{8,24},{9,... | collective-permute-start | bytes 7688 | tf_op jit(solution)/shard_map/ppermute | solution.py:92
  233.6 3.9 %collective-permute-done.17 = bf16[10,128]{1,0:T(8,128)(2,1)S(1)} collective-permute-done((bf16[10,128]{1,0:T(8,128)(2,1)S(1)}, bf16[10,128]{1,0:T(8,128)(2,1)S(1)}, u32[]{:S(2)}, u32[]{:S(2)}) %collective-permute-start.17) | collective-permute-done | bytes 2592 | tf_op jit(solution)/shard_map/ppermute | solution.py:92
  238.2 7.2 %collective-permute-start.22 = (bf16[40,128]{1,0:T(8,128)(2,1)S(1)}, bf16[40,128]{1,0:T(8,128)(2,1)S(1)}, u32[]{:S(2)}, u32[]{:S(2)}) collective-permute-start(bf16[40,128]{1,0:T(8,128)(2,1)S(1)} %broadcast_select_fusion), channel_id=1, source_target_pairs={{0,384},{1,385},{2,386},{3,387},{4,388},{5,389},{6,390},{7,391},{8... | collective-permute-start | bytes 30728 | tf_op jit(solution)/shard_map/ppermute | solution.py:92
  254.6 3.5 %collective-permute-start.25 = (bf16[160,128]{1,0:T(8,128)(2,1)S(1)}, bf16[160,128]{1,0:T(8,128)(2,1)S(1)}, u32[]{:S(2)}, u32[]{:S(2)}) collective-permute-start(bf16[160,128]{1,0:T(8,128)(2,1)S(1)} %bitcast_select_fusion.5), channel_id=1, source_target_pairs={{0,6},{1,7},{2,4},{3,5},{4,2},{5,3},{6,0},{7,1},{8,14},{9,15},{10,... | collective-permute-start | bytes 122888 | tf_op jit(solution)/shard_map/ppermute | solution.py:92
  260.0 4.0 %collective-permute-start.23 = (bf16[160,128]{1,0:T(8,128)(2,1)S(1)}, bf16[160,128]{1,0:T(8,128)(2,1)S(1)}, u32[]{:S(2)}, u32[]{:S(2)}) collective-permute-start(bf16[160,128]{1,0:T(8,128)(2,1)S(1)} %bitcast_select_fusion.5), channel_id=1, source_target_pairs={{0,2},{1,3},{2,0},{3,1},{4,6},{5,7},{6,4},{7,5},{8,10},{9,11},{10,... | collective-permute-start | bytes 122888 | tf_op jit(solution)/shard_map/ppermute | solution.py:92
  270.6 4.0 %collective-permute-start.26 = (bf16[640,128]{1,0:T(8,128)(2,1)S(1)}, bf16[640,128]{1,0:T(8,128)(2,1)S(1)}, u32[]{:S(2)}, u32[]{:S(2)}) collective-permute-start(bf16[640,128]{1,0:T(8,128)(2,1)S(1)} %bitcast_select_fusion.3), channel_id=1, source_target_pairs={{0,32},{1,33},{2,34},{3,35},{4,36},{5,37},{6,38},{7,39},{8,40},{9,... | collective-permute-start | bytes 491528 | tf_op jit(solution)/shard_map/ppermute | solution.py:92
  279.4 12.2 %collective-permute-start.29 = (bf16[2560,128]{1,0:T(8,128)(2,1)S(1)}, bf16[2560,128]{1,0:T(8,128)(2,1)S(1)}, u32[]{:S(2)}, u32[]{:S(2)}) collective-permute-start(bf16[2560,128]{1,0:T(8,128)(2,1)S(1)} %bitcast_select_fusion.1), channel_id=1, source_target_pairs={{0,1},{1,0},{2,3},{3,2},{4,5},{5,4},{6,7},{7,6},{8,9},{9,8},{10,11... | collective-permute-start | bytes 1966088 | tf_op jit(solution)/shard_map/ppermute | solution.py:92
  (183 shorter events, 102.1 us)
Async XLA Ops:
  1.8 9.2 %collective-permute-start = (bf16[1,512,256]{2,1,0:T(8,128)(2,1)S(1)}, bf16[1,512,256]{2,1,0:T(8,128)(2,1)S(1)}, u32[]{:S(2)}, u32[]{:S(2)}) collective-permute-start(bf16[1,512,256]{2,1,0:T(8,128)(2,1)S(1)} %get-tuple-element.22), channel_id=1, source_target_pairs={{0,1},{1,2},{2,3},{3,4},{4,5},{5,6},{6,7},{7,8},{8,9},{9,10},{10,1... | collective-permute-start | bytes 786440 | tf_op jit(solution)/shard_map/ppermute | solution.py:15
  13.9 27.7 %collective-permute-start.1 = (bf16[1,1024,256]{2,1,0:T(8,128)(2,1)}, bf16[1,1024,256]{2,1,0:T(8,128)(2,1)}, u32[]{:S(2)}, u32[]{:S(2)}) collective-permute-start(bf16[1,1024,256]{2,1,0:T(8,128)(2,1)} %bitcast.3), channel_id=1, source_target_pairs={{0,8},{1,9},{2,10},{3,11},{4,12},{5,13},{6,14},{7,15},{8,16},{9,17... | collective-permute-start | bytes 1572872 | tf_op jit(solution)/shard_map/ppermute | solution.py:15
  50.7 15.0 %collective-permute-start.2 = (bf16[1,1024,256]{2,1,0:T(8,128)(2,1)}, bf16[1,1024,256]{2,1,0:T(8,128)(2,1)}, u32[]{:S(2)}, u32[]{:S(2)}) collective-permute-start(bf16[1,1024,256]{2,1,0:T(8,128)(2,1)} %fusion.2), channel_id=1, source_target_pairs={{8,0},{9,1},{10,2},{11,3},{12,4},{13,5},{14,6},{15,7},{16,8},{17,9... | collective-permute-start | bytes 1572872 | tf_op jit(solution)/shard_map/ppermute | solution.py:15
  76.8 33.0 %collective-permute-start.4 = (f32[2560,128]{1,0:T(8,128)}, f32[2560,128]{1,0:T(8,128)}, u32[]{:S(2)}, u32[]{:S(2)}) collective-permute-start(f32[2560,128]{1,0:T(8,128)} %dynamic-slice_bitcast_fusion), channel_id=1, source_target_pairs={{0,1},{1,0},{2,3},{3,2},{4,5},{5,4},{6,7},{7,6},{8,9},{9,8},{10,11... | collective-permute-start | bytes 3932168 | tf_op jit(solution)/shard_map/ppermute | solution.py:85
  111.3 37.1 %collective-permute-start.5 = (f32[640,128]{1,0:T(8,128)S(1)}, f32[640,128]{1,0:T(8,128)S(1)}, u32[]{:S(2)}, u32[]{:S(2)}) collective-permute-start(f32[640,128]{1,0:T(8,128)S(1)} %get-tuple-element.17), channel_id=1, source_target_pairs={{0,32},{1,33},{2,34},{3,35},{4,36},{5,37},{6,38},{7,39},{8,40},{9,... | collective-permute-start | bytes 983048 | tf_op jit(solution)/shard_map/ppermute | solution.py:85
  140.7 15.8 %collective-permute-start.7 = (f32[640,128]{1,0:T(8,128)S(1)}, f32[640,128]{1,0:T(8,128)S(1)}, u32[]{:S(2)}, u32[]{:S(2)}) collective-permute-start(f32[640,128]{1,0:T(8,128)S(1)} %get-tuple-element.18), channel_id=1, source_target_pairs={{0,96},{1,97},{2,98},{3,99},{4,100},{5,101},{6,102},{7,103},{8,104... | collective-permute-start | bytes 983048 | tf_op jit(solution)/shard_map/ppermute | solution.py:85
  143.6 17.5 %collective-permute-start.6 = (f32[640,128]{1,0:T(8,128)S(1)}, f32[640,128]{1,0:T(8,128)S(1)}, u32[]{:S(2)}, u32[]{:S(2)}) collective-permute-start(f32[640,128]{1,0:T(8,128)S(1)} %get-tuple-element.19), channel_id=1, source_target_pairs={{0,64},{1,65},{2,66},{3,67},{4,68},{5,69},{6,70},{7,71},{8,72},{9,... | collective-permute-start | bytes 983048 | tf_op jit(solution)/shard_map/ppermute | solution.py:85
  161.3 9.1 %collective-permute-start.8 = (f32[160,128]{1,0:T(8,128)S(1)}, f32[160,128]{1,0:T(8,128)S(1)}, u32[]{:S(2)}, u32[]{:S(2)}) collective-permute-start(f32[160,128]{1,0:T(8,128)S(1)} %get-tuple-element.24), channel_id=1, source_target_pairs={{0,2},{1,3},{2,0},{3,1},{4,6},{5,7},{6,4},{7,5},{8,10},{9,11},{10,... | collective-permute-start | bytes 245768 | tf_op jit(solution)/shard_map/ppermute | solution.py:85
  163.5 7.0 %collective-permute-start.10 = (f32[160,128]{1,0:T(8,128)S(1)}, f32[160,128]{1,0:T(8,128)S(1)}, u32[]{:S(2)}, u32[]{:S(2)}) collective-permute-start(f32[160,128]{1,0:T(8,128)S(1)} %get-tuple-element.25), channel_id=1, source_target_pairs={{0,6},{1,7},{2,4},{3,5},{4,2},{5,3},{6,0},{7,1},{8,14},{9,15},{10,... | collective-permute-start | bytes 245768 | tf_op jit(solution)/shard_map/ppermute | solution.py:85
  166.0 9.9 %collective-permute-start.9 = (f32[160,128]{1,0:T(8,128)S(1)}, f32[160,128]{1,0:T(8,128)S(1)}, u32[]{:S(2)}, u32[]{:S(2)}) collective-permute-start(f32[160,128]{1,0:T(8,128)S(1)} %get-tuple-element.26), channel_id=1, source_target_pairs={{0,4},{1,5},{2,6},{3,7},{4,0},{5,1},{6,2},{7,3},{8,12},{9,13},{10,... | collective-permute-start | bytes 245768 | tf_op jit(solution)/shard_map/ppermute | solution.py:85
  176.0 15.5 %collective-permute-start.11 = (f32[40,128]{1,0:T(8,128)S(1)}, f32[40,128]{1,0:T(8,128)S(1)}, u32[]{:S(2)}, u32[]{:S(2)}) collective-permute-start(f32[40,128]{1,0:T(8,128)S(1)} %get-tuple-element.27), channel_id=1, source_target_pairs={{0,256},{1,257},{2,258},{3,259},{4,260},{5,261},{6,262},{7,263},{8... | collective-permute-start | bytes 61448 | tf_op jit(solution)/shard_map/ppermute | solution.py:85
  181.3 10.2 %collective-permute-start.13 = (f32[40,128]{1,0:T(8,128)S(1)}, f32[40,128]{1,0:T(8,128)S(1)}, u32[]{:S(2)}, u32[]{:S(2)}) collective-permute-start(f32[40,128]{1,0:T(8,128)S(1)} %get-tuple-element.28), channel_id=1, source_target_pairs={{0,384},{1,385},{2,386},{3,387},{4,388},{5,389},{6,390},{7,391},{8... | collective-permute-start | bytes 61448 | tf_op jit(solution)/shard_map/ppermute | solution.py:85
  187.8 43.1 %collective-permute-start.3 = (bf16[1,512,256]{2,1,0:T(8,128)(2,1)S(1)}, bf16[1,512,256]{2,1,0:T(8,128)(2,1)S(1)}, u32[]{:S(2)}, u32[]{:S(2)}) collective-permute-start(bf16[1,512,256]{2,1,0:T(8,128)(2,1)S(1)} %get-tuple-element.21), channel_id=1, source_target_pairs={{1,0},{2,1},{3,2},{4,3},{5,4},{6,5},{7,6},{8,7},{9,8},{10,9},{11,1... | collective-permute-start | bytes 786440 | tf_op jit(solution)/shard_map/ppermute | solution.py:15
  191.9 17.4 %collective-permute-start.14 = (f32[10,128]{1,0:T(8,128)S(1)}, f32[10,128]{1,0:T(8,128)S(1)}, u32[]{:S(2)}, u32[]{:S(2)}) collective-permute-start(f32[10,128]{1,0:T(8,128)S(1)} %get-tuple-element.30), channel_id=1, source_target_pairs={{0,8},{1,9},{2,10},{3,11},{4,12},{5,13},{6,14},{7,15},{8,0},{9,1},... | collective-permute-start | bytes 15368 | tf_op jit(solution)/shard_map/ppermute | solution.py:85
  198.2 11.1 %collective-permute-start.16 = (f32[10,128]{1,0:T(8,128)S(1)}, f32[10,128]{1,0:T(8,128)S(1)}, u32[]{:S(2)}, u32[]{:S(2)}) collective-permute-start(f32[10,128]{1,0:T(8,128)S(1)} %get-tuple-element.31), channel_id=1, source_target_pairs={{0,24},{1,25},{2,26},{3,27},{4,28},{5,29},{6,30},{7,31},{8,16},{9,... | collective-permute-start | bytes 15368 | tf_op jit(solution)/shard_map/ppermute | solution.py:85
  201.6 13.1 %collective-permute-start.15 = (f32[10,128]{1,0:T(8,128)S(1)}, f32[10,128]{1,0:T(8,128)S(1)}, u32[]{:S(2)}, u32[]{:S(2)}) collective-permute-start(f32[10,128]{1,0:T(8,128)S(1)} %get-tuple-element.32), channel_id=1, source_target_pairs={{0,16},{1,17},{2,18},{3,19},{4,20},{5,21},{6,22},{7,23},{8,24},{9,... | collective-permute-start | bytes 15368 | tf_op jit(solution)/shard_map/ppermute | solution.py:85
  214.7 17.5 %collective-permute-start.19 = (bf16[10,128]{1,0:T(8,128)(2,1)S(1)}, bf16[10,128]{1,0:T(8,128)(2,1)S(1)}, u32[]{:S(2)}, u32[]{:S(2)}) collective-permute-start(bf16[10,128]{1,0:T(8,128)(2,1)S(1)} %fusion.32), channel_id=1, source_target_pairs={{0,24},{1,25},{2,26},{3,27},{4,28},{5,29},{6,30},{7,31},{8,16},{9,... | collective-permute-start | bytes 7688 | tf_op jit(solution)/shard_map/ppermute | solution.py:92
  220.5 13.1 %collective-permute-start.18 = (bf16[10,128]{1,0:T(8,128)(2,1)S(1)}, bf16[10,128]{1,0:T(8,128)(2,1)S(1)}, u32[]{:S(2)}, u32[]{:S(2)}) collective-permute-start(bf16[10,128]{1,0:T(8,128)(2,1)S(1)} %fusion.32), channel_id=1, source_target_pairs={{0,16},{1,17},{2,18},{3,19},{4,20},{5,21},{6,22},{7,23},{8,24},{9,... | collective-permute-start | bytes 7688 | tf_op jit(solution)/shard_map/ppermute | solution.py:92
  229.0 8.6 %collective-permute-start.17 = (bf16[10,128]{1,0:T(8,128)(2,1)S(1)}, bf16[10,128]{1,0:T(8,128)(2,1)S(1)}, u32[]{:S(2)}, u32[]{:S(2)}) collective-permute-start(bf16[10,128]{1,0:T(8,128)(2,1)S(1)} %fusion.32), channel_id=1, source_target_pairs={{0,8},{1,9},{2,10},{3,11},{4,12},{5,13},{6,14},{7,15},{8,0},{9,1},... | collective-permute-start | bytes 7688 | tf_op jit(solution)/shard_map/ppermute | solution.py:92
  238.2 11.8 %collective-permute-start.22 = (bf16[40,128]{1,0:T(8,128)(2,1)S(1)}, bf16[40,128]{1,0:T(8,128)(2,1)S(1)}, u32[]{:S(2)}, u32[]{:S(2)}) collective-permute-start(bf16[40,128]{1,0:T(8,128)(2,1)S(1)} %broadcast_select_fusion), channel_id=1, source_target_pairs={{0,384},{1,385},{2,386},{3,387},{4,388},{5,389},{6,390},{7,391},{8... | collective-permute-start | bytes 30728 | tf_op jit(solution)/shard_map/ppermute | solution.py:92
  254.6 9.6 %collective-permute-start.25 = (bf16[160,128]{1,0:T(8,128)(2,1)S(1)}, bf16[160,128]{1,0:T(8,128)(2,1)S(1)}, u32[]{:S(2)}, u32[]{:S(2)}) collective-permute-start(bf16[160,128]{1,0:T(8,128)(2,1)S(1)} %bitcast_select_fusion.5), channel_id=1, source_target_pairs={{0,6},{1,7},{2,4},{3,5},{4,2},{5,3},{6,0},{7,1},{8,14},{9,15},{10,... | collective-permute-start | bytes 122888 | tf_op jit(solution)/shard_map/ppermute | solution.py:92
  266.2 8.6 %collective-permute-start.28 = (bf16[640,128]{1,0:T(8,128)(2,1)S(1)}, bf16[640,128]{1,0:T(8,128)(2,1)S(1)}, u32[]{:S(2)}, u32[]{:S(2)}) collective-permute-start(bf16[640,128]{1,0:T(8,128)(2,1)S(1)} %bitcast_select_fusion.3), channel_id=1, source_target_pairs={{0,96},{1,97},{2,98},{3,99},{4,100},{5,101},{6,102},{7,103},{8,104... | collective-permute-start | bytes 491528 | tf_op jit(solution)/shard_map/ppermute | solution.py:92
  268.1 6.8 %collective-permute-start.27 = (bf16[640,128]{1,0:T(8,128)(2,1)S(1)}, bf16[640,128]{1,0:T(8,128)(2,1)S(1)}, u32[]{:S(2)}, u32[]{:S(2)}) collective-permute-start(bf16[640,128]{1,0:T(8,128)(2,1)S(1)} %bitcast_select_fusion.3), channel_id=1, source_target_pairs={{0,64},{1,65},{2,66},{3,67},{4,68},{5,69},{6,70},{7,71},{8,72},{9,... | collective-permute-start | bytes 491528 | tf_op jit(solution)/shard_map/ppermute | solution.py:92
  279.4 14.0 %collective-permute-start.29 = (bf16[2560,128]{1,0:T(8,128)(2,1)S(1)}, bf16[2560,128]{1,0:T(8,128)(2,1)S(1)}, u32[]{:S(2)}, u32[]{:S(2)}) collective-permute-start(bf16[2560,128]{1,0:T(8,128)(2,1)S(1)} %bitcast_select_fusion.1), channel_id=1, source_target_pairs={{0,1},{1,0},{2,3},{3,2},{4,5},{5,4},{6,7},{7,6},{8,9},{9,8},{10,11... | collective-permute-start | bytes 1966088 | tf_op jit(solution)/shard_map/ppermute | solution.py:92
  (31 other events, 464.9 us)

commit v3 on v1

--- a/solution.py
+++ b/solution.py
@@ -57,7 +57,8 @@
     return (local_grad, ahead_rows, (past_term, now_term, mix_term))
 
 
-REDUCE_STEPS = (("tm", 1), ("tm", 32), ("tm", 2), ("dp", 1), ("dp", 4), ("tm", 4), ("dp", 2), ("tm", 8), ("tm", 16))
+HALVING_STEPS = (("tm", 1), ("tm", 32), ("dp", 1), ("tm", 2), ("dp", 4), ("dp", 2))
+BUTTERFLY_STEPS = (("tm", 4), ("tm", 8), ("tm", 16))
 
 
 def exchange(value, axis, mask):
@@ -65,29 +66,27 @@
     return lax.ppermute(value, axis, [(source, source ^ mask) for source in range(count)])
 
 
-def halving_sum(flat):
-    for axis, mask in REDUCE_STEPS:
+def reduce_grads(term_list, scale_factor):
+    shapes = [member.shape for member in term_list]
+    flat = jnp.concatenate([member.reshape(-1, 128) for member in term_list])
+    for axis, mask in HALVING_STEPS:
         half = flat.shape[0] // 2
         upper = (lax.axis_index(axis) & mask) != 0
         first, second = flat[:half], flat[half:]
         kept = jnp.where(upper, second, first)
         sent = jnp.where(upper, first, second)
         flat = kept + exchange(sent, axis, mask)
-    for axis, mask in reversed(REDUCE_STEPS):
+    for axis, mask in BUTTERFLY_STEPS:
+        flat = flat + exchange(flat, axis, mask)
+    flat = (flat * scale_factor).astype(jnp.bfloat16)
+    for axis, mask in reversed(HALVING_STEPS):
         upper = (lax.axis_index(axis) & mask) != 0
         other = exchange(flat, axis, mask)
         flat = jnp.where(upper, jnp.concatenate([other, flat]), jnp.concatenate([flat, other]))
-    return flat
-
-
-def reduce_grads(term_list, scale_factor):
-    shapes = [member.shape for member in term_list]
-    flat = jnp.concatenate([member.reshape(-1, 128) for member in term_list])
-    summed = halving_sum(flat)
     out, start = [], 0
     for shape in shapes:
         rows = shape[0] * shape[1] // 128
-        out.append((summed[start:start + rows].reshape(shape) * scale_factor).astype(jnp.bfloat16))
+        out.append(flat[start:start + rows].reshape(shape))
         start += rows
     return tuple(out)
 

time: 316 us -> 279 us (0.88)
  starting transfers between devices: 165 us -> 145 us
  waiting for transfers between devices: 103 us -> 85.2 us
    ppermute x18 -> x15, starting transfers between devices: 148 us -> 128 us  [exchange(): lax.ppermute(value, axis, [(source, source ^ mask) for source in range(co...]
    ppermute x18 -> x15, waiting for transfers between devices: 71.6 us -> 54.1 us  [exchange(): lax.ppermute(value, axis, [(source, source ^ mask) for source in range(co...]
    convert_element_type x6 -> x0, local copies, waits for them, and re-layouts: 4.86 us -> none  [reduce_grads(): (summed[start:start + rows].reshape(shape) * scale_factor).astype(jnp.bfl...]
    reshape x0 -> x6, local copies, waits for them, and re-layouts: none -> 4.86 us  [reduce_grads(): out.append(flat[start:start + rows].reshape(shape))]
  transfers between devices with their start and end apart: 22 -> 19, of which waited for: 21 -> 18; matrix products, arithmetic and copies ran while one was open for 4% -> 5% of each run, Pallas kernels for 0% -> 0%
where the time goes in v3:
time: 279 us; the launch traced here: 276 us
  starting transfers between devices  145 us (52%)
  waiting for transfers between devices  85.2 us (31%)
  matrix products  21.5 us (8%)
  local copies, waits for them, and re-layouts  19.4 us (7%)
  other arithmetic  3.49 us (1%)
    ppermute x15, starting transfers between devices, exchange(): lax.ppermute(value, axis, [(source, source ^ mask) for source in range(co...  128 us
    ppermute x15, waiting for transfers between devices, exchange(): lax.ppermute(value, axis, [(source, source ^ mask) for source in range(co...  54.1 us
    ppermute x4, waiting for transfers between devices, shifted(): lax.ppermute(value, axis, [(source, source + steps) for source in range(l...  31.1 us
    ppermute x4, starting transfers between devices, shifted(): lax.ppermute(value, axis, [(source, source + steps) for source in range(l...  16.8 us
    unnamed x56, local copies, waits for them, and re-layouts  6.83 us
  transfers between devices with their start and end apart: 19, of which 18 were waited for; matrix products, arithmetic and copies ran while one was open for 5% of the time, Pallas kernels for 0%

profile of v3, /device:TPU:1, one launch (start us, length us, event | category | flops | bytes accessed | tf_op | source)
XLA Modules:
  0.0 276.0 jit_solution(15750336283277572060)
XLA Ops:
  1.8 4.9 %collective-permute-start = (bf16[1,512,256]{2,1,0:T(8,128)(2,1)S(1)}, bf16[1,512,256]{2,1,0:T(8,128)(2,1)S(1)}, u32[]{:S(2)}, u32[]{:S(2)}) collective-permute-start(bf16[1,512,256]{2,1,0:T(8,128)(2,1)S(1)} %get-tuple-element.19), channel_id=1, source_target_pairs={{0,1},{1,2},{2,3},{3,4},{4,5},{5,6},{6,7},{7,8},{8,9},{9,10},{10,1... | collective-permute-start | bytes 786440 | tf_op jit(solution)/shard_map/ppermute | solution.py:15
  13.9 8.7 %collective-permute-start.1 = (bf16[1,1024,256]{2,1,0:T(8,128)(2,1)}, bf16[1,1024,256]{2,1,0:T(8,128)(2,1)}, u32[]{:S(2)}, u32[]{:S(2)}) collective-permute-start(bf16[1,1024,256]{2,1,0:T(8,128)(2,1)} %bitcast.3), channel_id=1, source_target_pairs={{0,8},{1,9},{2,10},{3,11},{4,12},{5,13},{6,14},{7,15},{8,16},{9,17... | collective-permute-start | bytes 1572872 | tf_op jit(solution)/shard_map/ppermute | solution.py:15
  24.2 17.5 %collective-permute-done.1 = bf16[1,1024,256]{2,1,0:T(8,128)(2,1)} collective-permute-done((bf16[1,1024,256]{2,1,0:T(8,128)(2,1)}, bf16[1,1024,256]{2,1,0:T(8,128)(2,1)}, u32[]{:S(2)}, u32[]{:S(2)}) %collective-permute-start.1) | collective-permute-done | bytes 524320 | tf_op jit(solution)/shard_map/ppermute | solution.py:15
  64.4 5.2 %collective-permute-done.2 = bf16[1,1024,256]{2,1,0:T(8,128)(2,1)} collective-permute-done((bf16[1,1024,256]{2,1,0:T(8,128)(2,1)}, bf16[1,1024,256]{2,1,0:T(8,128)(2,1)}, u32[]{:S(2)}, u32[]{:S(2)}) %collective-permute-start.2) | collective-permute-done | bytes 524320 | tf_op jit(solution)/shard_map/ppermute | solution.py:15
  75.8 31.3 %collective-permute-start.4 = (f32[2560,128]{1,0:T(8,128)S(1)}, f32[2560,128]{1,0:T(8,128)}, u32[]{:S(2)}, u32[]{:S(2)}) collective-permute-start(f32[2560,128]{1,0:T(8,128)S(1)} %broadcast_select_fusion), channel_id=1, source_target_pairs={{0,1},{1,0},{2,3},{3,2},{4,5},{5,4},{6,7},{7,6},{8,9},{9,8},{10,11... | collective-permute-start | bytes 3932168 | tf_op jit(solution)/shard_map/ppermute | solution.py:66
  111.9 24.8 %collective-permute-start.5 = (f32[1280,128]{1,0:T(8,128)S(1)}, f32[1280,128]{1,0:T(8,128)S(1)}, u32[]{:S(2)}, u32[]{:S(2)}) collective-permute-start(f32[1280,128]{1,0:T(8,128)S(1)} %slice_select_fusion), channel_id=1, source_target_pairs={{0,32},{1,33},{2,34},{3,35},{4,36},{5,37},{6,38},{7,39},{8,40},{9,... | collective-permute-start | bytes 1966088 | tf_op jit(solution)/shard_map/ppermute | solution.py:66
  136.7 15.1 %collective-permute-done.5 = f32[1280,128]{1,0:T(8,128)S(1)} collective-permute-done((f32[1280,128]{1,0:T(8,128)S(1)}, f32[1280,128]{1,0:T(8,128)S(1)}, u32[]{:S(2)}, u32[]{:S(2)}) %collective-permute-start.5) | collective-permute-done | bytes 655392 | tf_op jit(solution)/shard_map/ppermute | solution.py:66
  153.9 8.7 %collective-permute-done.6 = f32[640,128]{1,0:T(8,128)S(1)} collective-permute-done((f32[640,128]{1,0:T(8,128)S(1)}, f32[640,128]{1,0:T(8,128)S(1)}, u32[]{:S(2)}, u32[]{:S(2)}) %collective-permute-start.6) | collective-permute-done | bytes 327712 | tf_op jit(solution)/shard_map/ppermute | solution.py:66
  162.7 6.8 %collective-permute-start.7 = (f32[320,128]{1,0:T(8,128)S(1)}, f32[320,128]{1,0:T(8,128)S(1)}, u32[]{:S(2)}, u32[]{:S(2)}) collective-permute-start(f32[320,128]{1,0:T(8,128)S(1)} %slice_select_fusion.2), channel_id=1, source_target_pairs={{0,2},{1,3},{2,0},{3,1},{4,6},{5,7},{6,4},{7,5},{8,10},{9,11},{10,... | collective-permute-start | bytes 491528 | tf_op jit(solution)/shard_map/ppermute | solution.py:66
  169.5 3.1 %collective-permute-done.7 = f32[320,128]{1,0:T(8,128)S(1)} collective-permute-done((f32[320,128]{1,0:T(8,128)S(1)}, f32[320,128]{1,0:T(8,128)S(1)}, u32[]{:S(2)}, u32[]{:S(2)}) %collective-permute-start.7) | collective-permute-done | bytes 163872 | tf_op jit(solution)/shard_map/ppermute | solution.py:66
  172.6 5.5 %collective-permute-start.8 = (f32[160,128]{1,0:T(8,128)S(1)}, f32[160,128]{1,0:T(8,128)S(1)}, u32[]{:S(2)}, u32[]{:S(2)}) collective-permute-start(f32[160,128]{1,0:T(8,128)S(1)} %slice_select_fusion.3), channel_id=1, source_target_pairs={{0,256},{64,320},{128,384},{192,448},{256,0},{320,64},{384,128},{4... | collective-permute-start | bytes 245768 | tf_op jit(solution)/shard_map/ppermute | solution.py:66
  179.9 4.8 %collective-permute-start.9 = (f32[80,128]{1,0:T(8,128)S(1)}, f32[80,128]{1,0:T(8,128)S(1)}, u32[]{:S(2)}, u32[]{:S(2)}) collective-permute-start(f32[80,128]{1,0:T(8,128)S(1)} %slice_select_fusion.4), channel_id=1, source_target_pairs={{0,128},{64,192},{128,0},{192,64},{256,384},{320,448},{384,256},{4... | collective-permute-start | bytes 122888 | tf_op jit(solution)/shard_map/ppermute | solution.py:66
  188.9 3.0 %collective-permute-done.10 = f32[80,128]{1,0:T(8,128)S(1)} collective-permute-done((f32[80,128]{1,0:T(8,128)S(1)}, f32[80,128]{1,0:T(8,128)S(1)}, u32[]{:S(2)}, u32[]{:S(2)}) %collective-permute-start.10) | collective-permute-done | bytes 40992 | tf_op jit(solution)/shard_map/ppermute | solution.py:66
  191.9 7.3 %collective-permute-start.11 = (f32[80,128]{1,0:T(8,128)S(1)}, f32[80,128]{1,0:T(8,128)S(1)}, u32[]{:S(2)}, u32[]{:S(2)}) collective-permute-start(f32[80,128]{1,0:T(8,128)S(1)} %add.70), channel_id=1, source_target_pairs={{0,8},{1,9},{2,10},{3,11},{4,12},{5,13},{6,14},{7,15},{8,0},{9,1},... | collective-permute-start | bytes 122888 | tf_op jit(solution)/shard_map/ppermute | solution.py:66
  200.6 8.7 %collective-permute-start.12 = (f32[80,128]{1,0:T(8,128)S(1)}, f32[80,128]{1,0:T(8,128)S(1)}, u32[]{:S(2)}, u32[]{:S(2)}) collective-permute-start(f32[80,128]{1,0:T(8,128)S(1)} %add.71), channel_id=1, source_target_pairs={{0,16},{1,17},{2,18},{3,19},{4,20},{5,21},{6,22},{7,23},{8,24},{9,... | collective-permute-start | bytes 122888 | tf_op jit(solution)/shard_map/ppermute | solution.py:66
  209.3 4.8 %collective-permute-done.12 = f32[80,128]{1,0:T(8,128)S(1)} collective-permute-done((f32[80,128]{1,0:T(8,128)S(1)}, f32[80,128]{1,0:T(8,128)S(1)}, u32[]{:S(2)}, u32[]{:S(2)}) %collective-permute-start.12) | collective-permute-done | bytes 40992 | tf_op jit(solution)/shard_map/ppermute | solution.py:66
  214.1 4.8 %collective-permute-start.13 = (bf16[80,128]{1,0:T(8,128)(2,1)S(1)}, bf16[80,128]{1,0:T(8,128)(2,1)S(1)}, u32[]{:S(2)}, u32[]{:S(2)}) collective-permute-start(bf16[80,128]{1,0:T(8,128)(2,1)S(1)} %multiply_convert_fusion.7), channel_id=1, source_target_pairs={{0,128},{64,192},{128,0},{192,64},{256,384},{320,448},{384,256},{4... | collective-permute-start | bytes 61448 | tf_op jit(solution)/shard_map/ppermute | solution.py:66
  220.4 4.9 %collective-permute-start.14 = (bf16[160,128]{1,0:T(8,128)(2,1)S(1)}, bf16[160,128]{1,0:T(8,128)(2,1)S(1)}, u32[]{:S(2)}, u32[]{:S(2)}) collective-permute-start(bf16[160,128]{1,0:T(8,128)(2,1)S(1)} %maximum_select_fusion.5), channel_id=1, source_target_pairs={{0,256},{64,320},{128,384},{192,448},{256,0},{320,64},{384,128},{4... | collective-permute-start | bytes 122888 | tf_op jit(solution)/shard_map/ppermute | solution.py:66
  226.7 3.7 %collective-permute-start.15 = (bf16[320,128]{1,0:T(8,128)(2,1)S(1)}, bf16[320,128]{1,0:T(8,128)(2,1)S(1)}, u32[]{:S(2)}, u32[]{:S(2)}) collective-permute-start(bf16[320,128]{1,0:T(8,128)(2,1)S(1)} %maximum_select_fusion.4), channel_id=1, source_target_pairs={{0,2},{1,3},{2,0},{3,1},{4,6},{5,7},{6,4},{7,5},{8,10},{9,11},{10,... | collective-permute-start | bytes 245768 | tf_op jit(solution)/shard_map/ppermute | solution.py:66
  232.3 3.2 %collective-permute-start.16 = (bf16[640,128]{1,0:T(8,128)(2,1)S(1)}, bf16[640,128]{1,0:T(8,128)(2,1)S(1)}, u32[]{:S(2)}, u32[]{:S(2)}) collective-permute-start(bf16[640,128]{1,0:T(8,128)(2,1)S(1)} %maximum_select_fusion.3), channel_id=1, source_target_pairs={{0,64},{64,0},{128,192},{192,128},{256,320},{320,256},{384,448},{4... | collective-permute-start | bytes 491528 | tf_op jit(solution)/shard_map/ppermute | solution.py:66
  238.5 3.0 %collective-permute-start.17 = (bf16[1280,128]{1,0:T(8,128)(2,1)S(1)}, bf16[1280,128]{1,0:T(8,128)(2,1)S(1)}, u32[]{:S(2)}, u32[]{:S(2)}) collective-permute-start(bf16[1280,128]{1,0:T(8,128)(2,1)S(1)} %maximum_select_fusion.2), channel_id=1, source_target_pairs={{0,32},{1,33},{2,34},{3,35},{4,36},{5,37},{6,38},{7,39},{8,40},{9,... | collective-permute-start | bytes 983048 | tf_op jit(solution)/shard_map/ppermute | solution.py:66
  242.0 4.4 %collective-permute-done.17 = bf16[1280,128]{1,0:T(8,128)(2,1)S(1)} collective-permute-done((bf16[1280,128]{1,0:T(8,128)(2,1)S(1)}, bf16[1280,128]{1,0:T(8,128)(2,1)S(1)}, u32[]{:S(2)}, u32[]{:S(2)}) %collective-permute-start.17) | collective-permute-done | bytes 327712 | tf_op jit(solution)/shard_map/ppermute | solution.py:66
  246.6 15.0 %collective-permute-start.18 = (bf16[2560,128]{1,0:T(8,128)(2,1)S(1)}, bf16[2560,128]{1,0:T(8,128)(2,1)S(1)}, u32[]{:S(2)}, u32[]{:S(2)}) collective-permute-start(bf16[2560,128]{1,0:T(8,128)(2,1)S(1)} %maximum_select_fusion.1), channel_id=1, source_target_pairs={{0,1},{1,0},{2,3},{3,2},{4,5},{5,4},{6,7},{7,6},{8,9},{9,8},{10,11... | collective-permute-start | bytes 1966088 | tf_op jit(solution)/shard_map/ppermute | solution.py:66
  263.6 5.8 %collective-permute-done.3 = bf16[1,512,256]{2,1,0:T(8,128)(2,1)S(1)} collective-permute-done((bf16[1,512,256]{2,1,0:T(8,128)(2,1)S(1)}, bf16[1,512,256]{2,1,0:T(8,128)(2,1)S(1)}, u32[]{:S(2)}, u32[]{:S(2)}) %collective-permute-start.3) | collective-permute-done | bytes 262176 | tf_op jit(solution)/shard_map/ppermute | solution.py:15
  (127 shorter events, 69.9 us)
Async XLA Ops:
  0.6 41.0 %copy-start = (bf16[256,512]{1,0:T(8,128)(2,1)S(1)}, bf16[256,512]{1,0:T(8,128)(2,1)}, u32[]{:S(2)}) copy-start(bf16[256,512]{1,0:T(8,128)(2,1)} %param.13) | copy-start | bytes 786436
  1.8 9.2 %collective-permute-start = (bf16[1,512,256]{2,1,0:T(8,128)(2,1)S(1)}, bf16[1,512,256]{2,1,0:T(8,128)(2,1)S(1)}, u32[]{:S(2)}, u32[]{:S(2)}) collective-permute-start(bf16[1,512,256]{2,1,0:T(8,128)(2,1)S(1)} %get-tuple-element.19), channel_id=1, source_target_pairs={{0,1},{1,2},{2,3},{3,4},{4,5},{5,6},{6,7},{7,8},{8,9},{9,10},{10,1... | collective-permute-start | bytes 786440 | tf_op jit(solution)/shard_map/ppermute | solution.py:15
  13.9 27.7 %collective-permute-start.1 = (bf16[1,1024,256]{2,1,0:T(8,128)(2,1)}, bf16[1,1024,256]{2,1,0:T(8,128)(2,1)}, u32[]{:S(2)}, u32[]{:S(2)}) collective-permute-start(bf16[1,1024,256]{2,1,0:T(8,128)(2,1)} %bitcast.3), channel_id=1, source_target_pairs={{0,8},{1,9},{2,10},{3,11},{4,12},{5,13},{6,14},{7,15},{8,16},{9,17... | collective-permute-start | bytes 1572872 | tf_op jit(solution)/shard_map/ppermute | solution.py:15
  54.6 15.0 %collective-permute-start.2 = (bf16[1,1024,256]{2,1,0:T(8,128)(2,1)}, bf16[1,1024,256]{2,1,0:T(8,128)(2,1)}, u32[]{:S(2)}, u32[]{:S(2)}) collective-permute-start(bf16[1,1024,256]{2,1,0:T(8,128)(2,1)} %fusion.2), channel_id=1, source_target_pairs={{8,0},{9,1},{10,2},{11,3},{12,4},{13,5},{14,6},{15,7},{16,8},{17,9... | collective-permute-start | bytes 1572872 | tf_op jit(solution)/shard_map/ppermute | solution.py:15
  75.8 34.1 %collective-permute-start.4 = (f32[2560,128]{1,0:T(8,128)S(1)}, f32[2560,128]{1,0:T(8,128)}, u32[]{:S(2)}, u32[]{:S(2)}) collective-permute-start(f32[2560,128]{1,0:T(8,128)S(1)} %broadcast_select_fusion), channel_id=1, source_target_pairs={{0,1},{1,0},{2,3},{3,2},{4,5},{5,4},{6,7},{7,6},{8,9},{9,8},{10,11... | collective-permute-start | bytes 3932168 | tf_op jit(solution)/shard_map/ppermute | solution.py:66
  111.9 39.9 %collective-permute-start.5 = (f32[1280,128]{1,0:T(8,128)S(1)}, f32[1280,128]{1,0:T(8,128)S(1)}, u32[]{:S(2)}, u32[]{:S(2)}) collective-permute-start(f32[1280,128]{1,0:T(8,128)S(1)} %slice_select_fusion), channel_id=1, source_target_pairs={{0,32},{1,33},{2,34},{3,35},{4,36},{5,37},{6,38},{7,39},{8,40},{9,... | collective-permute-start | bytes 1966088 | tf_op jit(solution)/shard_map/ppermute | solution.py:66
  151.9 10.6 %collective-permute-start.6 = (f32[640,128]{1,0:T(8,128)S(1)}, f32[640,128]{1,0:T(8,128)S(1)}, u32[]{:S(2)}, u32[]{:S(2)}) collective-permute-start(f32[640,128]{1,0:T(8,128)S(1)} %slice_select_fusion.1), channel_id=1, source_target_pairs={{0,64},{64,0},{128,192},{192,128},{256,320},{320,256},{384,448},{4... | collective-permute-start | bytes 983048 | tf_op jit(solution)/shard_map/ppermute | solution.py:66
  162.6 78.9 %copy-start.9 = (bf16[256,512]{1,0:T(8,128)(2,1)S(1)}, bf16[256,512]{1,0:T(8,128)(2,1)}, u32[]{:S(2)}) copy-start(bf16[256,512]{1,0:T(8,128)(2,1)} %param.10) | copy-start | bytes 786436
  162.6 78.9 %copy-start.23 = (bf16[1024,256]{0,1:T(8,128)(2,1)S(1)}, bf16[1024,256]{0,1:T(8,128)(2,1)}, u32[]{:S(2)}) copy-start(bf16[1024,256]{0,1:T(8,128)(2,1)} %copy-done.22) | copy-start | bytes 1572868
  162.6 78.9 %copy-start.25 = (bf16[1024,256]{0,1:T(8,128)(2,1)S(1)}, bf16[1024,256]{0,1:T(8,128)(2,1)}, u32[]{:S(2)}) copy-start(bf16[1024,256]{0,1:T(8,128)(2,1)} %copy-done.24) | copy-start | bytes 1572868
  162.7 9.9 %collective-permute-start.7 = (f32[320,128]{1,0:T(8,128)S(1)}, f32[320,128]{1,0:T(8,128)S(1)}, u32[]{:S(2)}, u32[]{:S(2)}) collective-permute-start(f32[320,128]{1,0:T(8,128)S(1)} %slice_select_fusion.2), channel_id=1, source_target_pairs={{0,2},{1,3},{2,0},{3,1},{4,6},{5,7},{6,4},{7,5},{8,10},{9,11},{10,... | collective-permute-start | bytes 491528 | tf_op jit(solution)/shard_map/ppermute | solution.py:66
  172.6 7.3 %collective-permute-start.8 = (f32[160,128]{1,0:T(8,128)S(1)}, f32[160,128]{1,0:T(8,128)S(1)}, u32[]{:S(2)}, u32[]{:S(2)}) collective-permute-start(f32[160,128]{1,0:T(8,128)S(1)} %slice_select_fusion.3), channel_id=1, source_target_pairs={{0,256},{64,320},{128,384},{192,448},{256,0},{320,64},{384,128},{4... | collective-permute-start | bytes 245768 | tf_op jit(solution)/shard_map/ppermute | solution.py:66
  179.9 6.3 %collective-permute-start.9 = (f32[80,128]{1,0:T(8,128)S(1)}, f32[80,128]{1,0:T(8,128)S(1)}, u32[]{:S(2)}, u32[]{:S(2)}) collective-permute-start(f32[80,128]{1,0:T(8,128)S(1)} %slice_select_fusion.4), channel_id=1, source_target_pairs={{0,128},{64,192},{128,0},{192,64},{256,384},{320,448},{384,256},{4... | collective-permute-start | bytes 122888 | tf_op jit(solution)/shard_map/ppermute | solution.py:66
  186.2 5.6 %collective-permute-start.10 = (f32[80,128]{1,0:T(8,128)S(1)}, f32[80,128]{1,0:T(8,128)S(1)}, u32[]{:S(2)}, u32[]{:S(2)}) collective-permute-start(f32[80,128]{1,0:T(8,128)S(1)} %select_add_fusion.5), channel_id=1, source_target_pairs={{0,4},{1,5},{2,6},{3,7},{4,0},{5,1},{6,2},{7,3},{8,12},{9,13},{10,... | collective-permute-start | bytes 122888 | tf_op jit(solution)/shard_map/ppermute | solution.py:66
  191.9 8.7 %collective-permute-start.11 = (f32[80,128]{1,0:T(8,128)S(1)}, f32[80,128]{1,0:T(8,128)S(1)}, u32[]{:S(2)}, u32[]{:S(2)}) collective-permute-start(f32[80,128]{1,0:T(8,128)S(1)} %add.70), channel_id=1, source_target_pairs={{0,8},{1,9},{2,10},{3,11},{4,12},{5,13},{6,14},{7,15},{8,0},{9,1},... | collective-permute-start | bytes 122888 | tf_op jit(solution)/shard_map/ppermute | solution.py:66
  200.6 13.5 %collective-permute-start.12 = (f32[80,128]{1,0:T(8,128)S(1)}, f32[80,128]{1,0:T(8,128)S(1)}, u32[]{:S(2)}, u32[]{:S(2)}) collective-permute-start(f32[80,128]{1,0:T(8,128)S(1)} %add.71), channel_id=1, source_target_pairs={{0,16},{1,17},{2,18},{3,19},{4,20},{5,21},{6,22},{7,23},{8,24},{9,... | collective-permute-start | bytes 122888 | tf_op jit(solution)/shard_map/ppermute | solution.py:66
  214.1 6.3 %collective-permute-start.13 = (bf16[80,128]{1,0:T(8,128)(2,1)S(1)}, bf16[80,128]{1,0:T(8,128)(2,1)S(1)}, u32[]{:S(2)}, u32[]{:S(2)}) collective-permute-start(bf16[80,128]{1,0:T(8,128)(2,1)S(1)} %multiply_convert_fusion.7), channel_id=1, source_target_pairs={{0,128},{64,192},{128,0},{192,64},{256,384},{320,448},{384,256},{4... | collective-permute-start | bytes 61448 | tf_op jit(solution)/shard_map/ppermute | solution.py:66
  220.4 6.3 %collective-permute-start.14 = (bf16[160,128]{1,0:T(8,128)(2,1)S(1)}, bf16[160,128]{1,0:T(8,128)(2,1)S(1)}, u32[]{:S(2)}, u32[]{:S(2)}) collective-permute-start(bf16[160,128]{1,0:T(8,128)(2,1)S(1)} %maximum_select_fusion.5), channel_id=1, source_target_pairs={{0,256},{64,320},{128,384},{192,448},{256,0},{320,64},{384,128},{4... | collective-permute-start | bytes 122888 | tf_op jit(solution)/shard_map/ppermute | solution.py:66
  226.7 5.5 %collective-permute-start.15 = (bf16[320,128]{1,0:T(8,128)(2,1)S(1)}, bf16[320,128]{1,0:T(8,128)(2,1)S(1)}, u32[]{:S(2)}, u32[]{:S(2)}) collective-permute-start(bf16[320,128]{1,0:T(8,128)(2,1)S(1)} %maximum_select_fusion.4), channel_id=1, source_target_pairs={{0,2},{1,3},{2,0},{3,1},{4,6},{5,7},{6,4},{7,5},{8,10},{9,11},{10,... | collective-permute-start | bytes 245768 | tf_op jit(solution)/shard_map/ppermute | solution.py:66
  232.3 6.1 %collective-permute-start.16 = (bf16[640,128]{1,0:T(8,128)(2,1)S(1)}, bf16[640,128]{1,0:T(8,128)(2,1)S(1)}, u32[]{:S(2)}, u32[]{:S(2)}) collective-permute-start(bf16[640,128]{1,0:T(8,128)(2,1)S(1)} %maximum_select_fusion.3), channel_id=1, source_target_pairs={{0,64},{64,0},{128,192},{192,128},{256,320},{320,256},{384,448},{4... | collective-permute-start | bytes 491528 | tf_op jit(solution)/shard_map/ppermute | solution.py:66
  238.4 30.9 %copy-start.7 = (bf16[1024,256]{1,0:T(8,128)(2,1)S(1)}, bf16[1024,256]{1,0:T(8,128)(2,1)}, u32[]{:S(2)}) copy-start(bf16[1024,256]{1,0:T(8,128)(2,1)} %copy-done.6) | copy-start | bytes 1572868
  238.5 8.0 %collective-permute-start.17 = (bf16[1280,128]{1,0:T(8,128)(2,1)S(1)}, bf16[1280,128]{1,0:T(8,128)(2,1)S(1)}, u32[]{:S(2)}, u32[]{:S(2)}) collective-permute-start(bf16[1280,128]{1,0:T(8,128)(2,1)S(1)} %maximum_select_fusion.2), channel_id=1, source_target_pairs={{0,32},{1,33},{2,34},{3,35},{4,36},{5,37},{6,38},{7,39},{8,40},{9,... | collective-permute-start | bytes 983048 | tf_op jit(solution)/shard_map/ppermute | solution.py:66
  246.6 24.1 %collective-permute-start.18 = (bf16[2560,128]{1,0:T(8,128)(2,1)S(1)}, bf16[2560,128]{1,0:T(8,128)(2,1)S(1)}, u32[]{:S(2)}, u32[]{:S(2)}) collective-permute-start(bf16[2560,128]{1,0:T(8,128)(2,1)S(1)} %maximum_select_fusion.1), channel_id=1, source_target_pairs={{0,1},{1,0},{2,3},{3,2},{4,5},{5,4},{6,7},{7,6},{8,9},{9,8},{10,11... | collective-permute-start | bytes 1966088 | tf_op jit(solution)/shard_map/ppermute | solution.py:66
  261.7 7.7 %collective-permute-start.3 = (bf16[1,512,256]{2,1,0:T(8,128)(2,1)S(1)}, bf16[1,512,256]{2,1,0:T(8,128)(2,1)S(1)}, u32[]{:S(2)}, u32[]{:S(2)}) collective-permute-start(bf16[1,512,256]{2,1,0:T(8,128)(2,1)S(1)} %get-tuple-element.18), channel_id=1, source_target_pairs={{1,0},{2,1},{3,2},{4,3},{5,4},{6,5},{7,6},{8,7},{9,8},{10,9},{11,1... | collective-permute-start | bytes 786440 | tf_op jit(solution)/shard_map/ppermute | solution.py:15
  (21 other events, 143.8 us)

commit v4 on v3

--- a/solution.py
+++ b/solution.py
@@ -118,24 +118,37 @@
     )
     hidden_activation = first_layer_stash[3]
     distant_offsets = SECOND_DILATION // number_of_steps
-    past_two = shifted(hidden_activation, "tm", distant_offsets)
-    second_layer_stash = forward_layer(
-        hidden_activation,
-        past_two,
-        second_history_weight,
-        second_current_weight,
-        second_residual_weight,
-    )
-    local_two, ahead_two, second_layer_terms = backward_layer(
-        hidden_activation,
-        past_two,
-        second_layer_stash,
-        cotangent,
-        second_history_weight,
-        second_current_weight,
-        second_residual_weight,
-    )
-    arrived_back = shifted(ahead_two, "tm", -distant_offsets)
+    chunk_rows = number_of_steps // 2
+    local_parts, arrived_parts, term_parts, past_parts = [], [], [], []
+    for chunk in range(2):
+        rows = slice(chunk * chunk_rows, (chunk + 1) * chunk_rows)
+        hidden_chunk = hidden_activation[:, rows, :]
+        if chunk:
+            hidden_chunk, _ = lax.optimization_barrier((hidden_chunk, past_parts[-1]))
+        past_chunk = shifted(hidden_chunk, "tm", distant_offsets)
+        past_parts.append(past_chunk)
+        chunk_stash = forward_layer(
+            hidden_chunk,
+            past_chunk,
+            second_history_weight,
+            second_current_weight,
+            second_residual_weight,
+        )
+        local_chunk, ahead_chunk, chunk_terms = backward_layer(
+            hidden_chunk,
+            past_chunk,
+            chunk_stash,
+            cotangent[:, rows, :],
+            second_history_weight,
+            second_current_weight,
+            second_residual_weight,
+        )
+        local_parts.append(local_chunk)
+        arrived_parts.append(shifted(ahead_chunk, "tm", -distant_offsets))
+        term_parts.append(chunk_terms)
+    local_two = jnp.concatenate(local_parts, axis=1)
+    arrived_back = jnp.concatenate(arrived_parts, axis=1)
+    second_layer_terms = tuple(first + second for first, second in zip(*term_parts))
     hidden_gradient = (local_two + arrived_back.astype(jnp.float32)).astype(jnp.bfloat16)
     local_one, forward_rows_first, first_layer_terms = backward_layer(
         signal,

time: 279 us -> 257 us (0.921)
  waiting for transfers between devices: 85.2 us -> 76 us
  starting transfers between devices: 145 us -> 136 us
    ppermute x15, starting transfers between devices: 128 us -> 111 us  [exchange(): lax.ppermute(value, axis, [(source, source ^ mask) for source in range(co...]
    ppermute x4 -> x6, waiting for transfers between devices: 31.1 us -> 20.8 us  [shifted(): lax.ppermute(value, axis, [(source, source + steps) for source in range(l...]
    ppermute x4 -> x6, starting transfers between devices: 16.8 us -> 25.3 us  [shifted(): lax.ppermute(value, axis, [(source, source + steps) for source in range(l...]
    unnamed x56 -> x54, local copies, waits for them, and re-layouts: 6.83 us -> 6.23 us
  transfers between devices with their start and end apart: 19 -> 21, of which waited for: 18 -> 18; matrix products, arithmetic and copies ran while one was open for 5% -> 8% of each run, Pallas kernels for 0% -> 0%
where the time goes in v4:
time: 257 us; the launch traced here: 256 us
  starting transfers between devices  136 us (53%)
  waiting for transfers between devices  76 us (30%)
  matrix products  19.5 us (8%)
  local copies, waits for them, and re-layouts  18.8 us (7%)
  other arithmetic  4.67 us (2%)
    ppermute x15, starting transfers between devices, exchange(): lax.ppermute(value, axis, [(source, source ^ mask) for source in range(co...  111 us
    ppermute x15, waiting for transfers between devices, exchange(): lax.ppermute(value, axis, [(source, source ^ mask) for source in range(co...  55.2 us
    ppermute x6, starting transfers between devices, shifted(): lax.ppermute(value, axis, [(source, source + steps) for source in range(l...  25.3 us
    ppermute x6, waiting for transfers between devices, shifted(): lax.ppermute(value, axis, [(source, source + steps) for source in range(l...  20.8 us
    unnamed x54, local copies, waits for them, and re-layouts  6.23 us
    reshape x6, local copies, waits for them, and re-layouts, reduce_grads(): flat = jnp.concatenate([member.reshape(-1, 128) for member in term_list])  5.52 us
  transfers between devices with their start and end apart: 21, of which 18 were waited for; matrix products, arithmetic and copies ran while one was open for 8% of the time, Pallas kernels for 0%

profile of v4, /device:TPU:1, one launch (start us, length us, event | category | flops | bytes accessed | tf_op | source)
XLA Modules:
  0.0 256.2 jit_solution(7965687565226491340)
XLA Ops:
  1.8 4.9 %collective-permute-start = (bf16[1,512,256]{2,1,0:T(8,128)(2,1)S(1)}, bf16[1,512,256]{2,1,0:T(8,128)(2,1)S(1)}, u32[]{:S(2)}, u32[]{:S(2)}) collective-permute-start(bf16[1,512,256]{2,1,0:T(8,128)(2,1)S(1)} %get-tuple-element.25), channel_id=1, source_target_pairs={{0,1},{1,2},{2,3},{3,4},{4,5},{5,6},{6,7},{7,8},{8,9},{9,10},{10,1... | collective-permute-start | bytes 786440 | tf_op jit(solution)/shard_map/ppermute | solution.py:15
  13.5 7.9 %collective-permute-start.1 = (bf16[1,512,256]{2,1,0:T(8,128)(2,1)S(1)}, bf16[1,512,256]{2,1,0:T(8,128)(2,1)S(1)}, u32[]{:S(2)}, u32[]{:S(2)}) collective-permute-start(bf16[1,512,256]{2,1,0:T(8,128)(2,1)S(1)} %get-tuple-element.23), channel_id=1, source_target_pairs={{0,8},{1,9},{2,10},{3,11},{4,12},{5,13},{6,14},{7,15},{8,16},{9,17... | collective-permute-start | bytes 786440 | tf_op jit(solution)/shard_map/ppermute | solution.py:15
  21.8 5.2 %collective-permute-done.1 = bf16[1,512,256]{2,1,0:T(8,128)(2,1)S(1)} collective-permute-done((bf16[1,512,256]{2,1,0:T(8,128)(2,1)S(1)}, bf16[1,512,256]{2,1,0:T(8,128)(2,1)S(1)}, u32[]{:S(2)}, u32[]{:S(2)}) %collective-permute-start.1) | collective-permute-done | bytes 262176 | tf_op jit(solution)/shard_map/ppermute | solution.py:15
  32.0 8.0 %collective-permute-start.2 = (bf16[1,512,256]{2,1,0:T(8,128)(2,1)S(1)}, bf16[1,512,256]{2,1,0:T(8,128)(2,1)S(1)}, u32[]{:S(2)}, u32[]{:S(2)}) collective-permute-start(bf16[1,512,256]{2,1,0:T(8,128)(2,1)S(1)} %get-tuple-element.8), channel_id=1, source_target_pairs={{0,8},{1,9},{2,10},{3,11},{4,12},{5,13},{6,14},{7,15},{8,16},{9,17... | collective-permute-start | bytes 786440 | tf_op jit(solution)/shard_map/ppermute | solution.py:15
  41.7 7.1 %collective-permute-done.2 = bf16[1,512,256]{2,1,0:T(8,128)(2,1)S(1)} collective-permute-done((bf16[1,512,256]{2,1,0:T(8,128)(2,1)S(1)}, bf16[1,512,256]{2,1,0:T(8,128)(2,1)S(1)}, u32[]{:S(2)}, u32[]{:S(2)}) %collective-permute-start.2) | collective-permute-done | bytes 262176 | tf_op jit(solution)/shard_map/ppermute | solution.py:15
  72.8 40.4 %collective-permute-start.6 = (f32[2560,128]{1,0:T(8,128)S(1)}, f32[2560,128]{1,0:T(8,128)}, u32[]{:S(2)}, u32[]{:S(2)}) collective-permute-start(f32[2560,128]{1,0:T(8,128)S(1)} %broadcast_select_fusion), channel_id=1, source_target_pairs={{0,1},{1,0},{2,3},{3,2},{4,5},{5,4},{6,7},{7,6},{8,9},{9,8},{10,11... | collective-permute-start | bytes 3932168 | tf_op jit(solution)/shard_map/ppermute | solution.py:66
  119.9 16.4 %collective-permute-done.7 = f32[1280,128]{1,0:T(8,128)S(1)} collective-permute-done((f32[1280,128]{1,0:T(8,128)S(1)}, f32[1280,128]{1,0:T(8,128)S(1)}, u32[]{:S(2)}, u32[]{:S(2)}) %collective-permute-start.7) | collective-permute-done | bytes 655392 | tf_op jit(solution)/shard_map/ppermute | solution.py:66
  136.4 3.2 %collective-permute-start.8 = (f32[640,128]{1,0:T(8,128)S(1)}, f32[640,128]{1,0:T(8,128)S(1)}, u32[]{:S(2)}, u32[]{:S(2)}) collective-permute-start(f32[640,128]{1,0:T(8,128)S(1)} %slice_select_fusion.1), channel_id=1, source_target_pairs={{0,64},{64,0},{128,192},{192,128},{256,320},{320,256},{384,448},{4... | collective-permute-start | bytes 983048 | tf_op jit(solution)/shard_map/ppermute | solution.py:66
  139.5 7.2 %collective-permute-done.8 = f32[640,128]{1,0:T(8,128)S(1)} collective-permute-done((f32[640,128]{1,0:T(8,128)S(1)}, f32[640,128]{1,0:T(8,128)S(1)}, u32[]{:S(2)}, u32[]{:S(2)}) %collective-permute-start.8) | collective-permute-done | bytes 327712 | tf_op jit(solution)/shard_map/ppermute | solution.py:66
  148.8 4.1 %collective-permute-done.9 = f32[320,128]{1,0:T(8,128)S(1)} collective-permute-done((f32[320,128]{1,0:T(8,128)S(1)}, f32[320,128]{1,0:T(8,128)S(1)}, u32[]{:S(2)}, u32[]{:S(2)}) %collective-permute-start.9) | collective-permute-done | bytes 163872 | tf_op jit(solution)/shard_map/ppermute | solution.py:66
  153.0 3.7 %collective-permute-start.10 = (f32[160,128]{1,0:T(8,128)S(1)}, f32[160,128]{1,0:T(8,128)S(1)}, u32[]{:S(2)}, u32[]{:S(2)}) collective-permute-start(f32[160,128]{1,0:T(8,128)S(1)} %slice_select_fusion.3), channel_id=1, source_target_pairs={{0,256},{64,320},{128,384},{192,448},{256,0},{320,64},{384,128},{4... | collective-permute-start | bytes 245768 | tf_op jit(solution)/shard_map/ppermute | solution.py:66
  156.7 3.1 %collective-permute-done.10 = f32[160,128]{1,0:T(8,128)S(1)} collective-permute-done((f32[160,128]{1,0:T(8,128)S(1)}, f32[160,128]{1,0:T(8,128)S(1)}, u32[]{:S(2)}, u32[]{:S(2)}) %collective-permute-start.10) | collective-permute-done | bytes 81952 | tf_op jit(solution)/shard_map/ppermute | solution.py:66
  159.8 4.8 %collective-permute-start.11 = (f32[80,128]{1,0:T(8,128)S(1)}, f32[80,128]{1,0:T(8,128)S(1)}, u32[]{:S(2)}, u32[]{:S(2)}) collective-permute-start(f32[80,128]{1,0:T(8,128)S(1)} %slice_select_fusion.4), channel_id=1, source_target_pairs={{0,128},{64,192},{128,0},{192,64},{256,384},{320,448},{384,256},{4... | collective-permute-start | bytes 122888 | tf_op jit(solution)/shard_map/ppermute | solution.py:66
  166.1 4.3 %collective-permute-start.12 = (f32[80,128]{1,0:T(8,128)S(1)}, f32[80,128]{1,0:T(8,128)S(1)}, u32[]{:S(2)}, u32[]{:S(2)}) collective-permute-start(f32[80,128]{1,0:T(8,128)S(1)} %select_add_fusion.5), channel_id=1, source_target_pairs={{0,4},{1,5},{2,6},{3,7},{4,0},{5,1},{6,2},{7,3},{8,12},{9,13},{10,... | collective-permute-start | bytes 122888 | tf_op jit(solution)/shard_map/ppermute | solution.py:66
  171.8 7.0 %collective-permute-start.13 = (f32[80,128]{1,0:T(8,128)S(1)}, f32[80,128]{1,0:T(8,128)S(1)}, u32[]{:S(2)}, u32[]{:S(2)}) collective-permute-start(f32[80,128]{1,0:T(8,128)S(1)} %add.97), channel_id=1, source_target_pairs={{0,8},{1,9},{2,10},{3,11},{4,12},{5,13},{6,14},{7,15},{8,0},{9,1},... | collective-permute-start | bytes 122888 | tf_op jit(solution)/shard_map/ppermute | solution.py:66
  180.4 9.1 %collective-permute-start.14 = (f32[80,128]{1,0:T(8,128)S(1)}, f32[80,128]{1,0:T(8,128)S(1)}, u32[]{:S(2)}, u32[]{:S(2)}) collective-permute-start(f32[80,128]{1,0:T(8,128)S(1)} %add.98), channel_id=1, source_target_pairs={{0,16},{1,17},{2,18},{3,19},{4,20},{5,21},{6,22},{7,23},{8,24},{9,... | collective-permute-start | bytes 122888 | tf_op jit(solution)/shard_map/ppermute | solution.py:66
  189.6 4.4 %collective-permute-done.14 = f32[80,128]{1,0:T(8,128)S(1)} collective-permute-done((f32[80,128]{1,0:T(8,128)S(1)}, f32[80,128]{1,0:T(8,128)S(1)}, u32[]{:S(2)}, u32[]{:S(2)}) %collective-permute-start.14) | collective-permute-done | bytes 40992 | tf_op jit(solution)/shard_map/ppermute | solution.py:66
  194.0 4.8 %collective-permute-start.15 = (bf16[80,128]{1,0:T(8,128)(2,1)S(1)}, bf16[80,128]{1,0:T(8,128)(2,1)S(1)}, u32[]{:S(2)}, u32[]{:S(2)}) collective-permute-start(bf16[80,128]{1,0:T(8,128)(2,1)S(1)} %multiply_convert_fusion.11), channel_id=1, source_target_pairs={{0,128},{64,192},{128,0},{192,64},{256,384},{320,448},{384,256},{4... | collective-permute-start | bytes 61448 | tf_op jit(solution)/shard_map/ppermute | solution.py:66
  200.3 4.6 %collective-permute-start.16 = (bf16[160,128]{1,0:T(8,128)(2,1)S(1)}, bf16[160,128]{1,0:T(8,128)(2,1)S(1)}, u32[]{:S(2)}, u32[]{:S(2)}) collective-permute-start(bf16[160,128]{1,0:T(8,128)(2,1)S(1)} %maximum_select_fusion.5), channel_id=1, source_target_pairs={{0,256},{64,320},{128,384},{192,448},{256,0},{320,64},{384,128},{4... | collective-permute-start | bytes 122888 | tf_op jit(solution)/shard_map/ppermute | solution.py:66
  206.6 3.5 %collective-permute-start.17 = (bf16[320,128]{1,0:T(8,128)(2,1)S(1)}, bf16[320,128]{1,0:T(8,128)(2,1)S(1)}, u32[]{:S(2)}, u32[]{:S(2)}) collective-permute-start(bf16[320,128]{1,0:T(8,128)(2,1)S(1)} %maximum_select_fusion.4), channel_id=1, source_target_pairs={{0,2},{1,3},{2,0},{3,1},{4,6},{5,7},{6,4},{7,5},{8,10},{9,11},{10,... | collective-permute-start | bytes 245768 | tf_op jit(solution)/shard_map/ppermute | solution.py:66
  212.0 3.2 %collective-permute-start.18 = (bf16[640,128]{1,0:T(8,128)(2,1)S(1)}, bf16[640,128]{1,0:T(8,128)(2,1)S(1)}, u32[]{:S(2)}, u32[]{:S(2)}) collective-permute-start(bf16[640,128]{1,0:T(8,128)(2,1)S(1)} %maximum_select_fusion.3), channel_id=1, source_target_pairs={{0,64},{64,0},{128,192},{192,128},{256,320},{320,256},{384,448},{4... | collective-permute-start | bytes 491528 | tf_op jit(solution)/shard_map/ppermute | solution.py:66
  221.1 4.9 %collective-permute-done.19 = bf16[1280,128]{1,0:T(8,128)(2,1)S(1)} collective-permute-done((bf16[1280,128]{1,0:T(8,128)(2,1)S(1)}, bf16[1280,128]{1,0:T(8,128)(2,1)S(1)}, u32[]{:S(2)}, u32[]{:S(2)}) %collective-permute-start.19) | collective-permute-done | bytes 327712 | tf_op jit(solution)/shard_map/ppermute | solution.py:66
  226.1 15.7 %collective-permute-start.20 = (bf16[2560,128]{1,0:T(8,128)(2,1)S(1)}, bf16[2560,128]{1,0:T(8,128)(2,1)S(1)}, u32[]{:S(2)}, u32[]{:S(2)}) collective-permute-start(bf16[2560,128]{1,0:T(8,128)(2,1)S(1)} %maximum_select_fusion.1), channel_id=1, source_target_pairs={{0,1},{1,0},{2,3},{3,2},{4,5},{5,4},{6,7},{7,6},{8,9},{9,8},{10,11... | collective-permute-start | bytes 1966088 | tf_op jit(solution)/shard_map/ppermute | solution.py:66
  243.8 5.8 %collective-permute-done.5 = bf16[1,512,256]{2,1,0:T(8,128)(2,1)S(1)} collective-permute-done((bf16[1,512,256]{2,1,0:T(8,128)(2,1)S(1)}, bf16[1,512,256]{2,1,0:T(8,128)(2,1)S(1)}, u32[]{:S(2)}, u32[]{:S(2)}) %collective-permute-start.5) | collective-permute-done | bytes 262176 | tf_op jit(solution)/shard_map/ppermute | solution.py:15
  (139 shorter events, 71.6 us)
Async XLA Ops:
  1.8 9.2 %collective-permute-start = (bf16[1,512,256]{2,1,0:T(8,128)(2,1)S(1)}, bf16[1,512,256]{2,1,0:T(8,128)(2,1)S(1)}, u32[]{:S(2)}, u32[]{:S(2)}) collective-permute-start(bf16[1,512,256]{2,1,0:T(8,128)(2,1)S(1)} %get-tuple-element.25), channel_id=1, source_target_pairs={{0,1},{1,2},{2,3},{3,4},{4,5},{5,6},{6,7},{7,8},{8,9},{9,10},{10,1... | collective-permute-start | bytes 786440 | tf_op jit(solution)/shard_map/ppermute | solution.py:15
  13.5 13.4 %collective-permute-start.1 = (bf16[1,512,256]{2,1,0:T(8,128)(2,1)S(1)}, bf16[1,512,256]{2,1,0:T(8,128)(2,1)S(1)}, u32[]{:S(2)}, u32[]{:S(2)}) collective-permute-start(bf16[1,512,256]{2,1,0:T(8,128)(2,1)S(1)} %get-tuple-element.23), channel_id=1, source_target_pairs={{0,8},{1,9},{2,10},{3,11},{4,12},{5,13},{6,14},{7,15},{8,16},{9,17... | collective-permute-start | bytes 786440 | tf_op jit(solution)/shard_map/ppermute | solution.py:15
  32.0 16.8 %collective-permute-start.2 = (bf16[1,512,256]{2,1,0:T(8,128)(2,1)S(1)}, bf16[1,512,256]{2,1,0:T(8,128)(2,1)S(1)}, u32[]{:S(2)}, u32[]{:S(2)}) collective-permute-start(bf16[1,512,256]{2,1,0:T(8,128)(2,1)S(1)} %get-tuple-element.8), channel_id=1, source_target_pairs={{0,8},{1,9},{2,10},{3,11},{4,12},{5,13},{6,14},{7,15},{8,16},{9,17... | collective-permute-start | bytes 786440 | tf_op jit(solution)/shard_map/ppermute | solution.py:15
  40.0 26.7 %collective-permute-start.3 = (bf16[1,512,256]{2,1,0:T(8,128)(2,1)}, bf16[1,512,256]{2,1,0:T(8,128)(2,1)}, u32[]{:S(2)}, u32[]{:S(2)}) collective-permute-start(bf16[1,512,256]{2,1,0:T(8,128)(2,1)} %fusion.3), channel_id=1, source_target_pairs={{8,0},{9,1},{10,2},{11,3},{12,4},{13,5},{14,6},{15,7},{16,8},{17,9... | collective-permute-start | bytes 786440 | tf_op jit(solution)/shard_map/ppermute | solution.py:15
  50.7 16.1 %collective-permute-start.4 = (bf16[1,512,256]{2,1,0:T(8,128)(2,1)}, bf16[1,512,256]{2,1,0:T(8,128)(2,1)}, u32[]{:S(2)}, u32[]{:S(2)}) collective-permute-start(bf16[1,512,256]{2,1,0:T(8,128)(2,1)} %fusion.4), channel_id=1, source_target_pairs={{8,0},{9,1},{10,2},{11,3},{12,4},{13,5},{14,6},{15,7},{16,8},{17,9... | collective-permute-start | bytes 786440 | tf_op jit(solution)/shard_map/ppermute | solution.py:15
  72.8 43.2 %collective-permute-start.6 = (f32[2560,128]{1,0:T(8,128)S(1)}, f32[2560,128]{1,0:T(8,128)}, u32[]{:S(2)}, u32[]{:S(2)}) collective-permute-start(f32[2560,128]{1,0:T(8,128)S(1)} %broadcast_select_fusion), channel_id=1, source_target_pairs={{0,1},{1,0},{2,3},{3,2},{4,5},{5,4},{6,7},{7,6},{8,9},{9,8},{10,11... | collective-permute-start | bytes 3932168 | tf_op jit(solution)/shard_map/ppermute | solution.py:66
  117.9 18.3 %collective-permute-start.7 = (f32[1280,128]{1,0:T(8,128)S(1)}, f32[1280,128]{1,0:T(8,128)S(1)}, u32[]{:S(2)}, u32[]{:S(2)}) collective-permute-start(f32[1280,128]{1,0:T(8,128)S(1)} %slice_select_fusion), channel_id=1, source_target_pairs={{0,32},{1,33},{2,34},{3,35},{4,36},{5,37},{6,38},{7,39},{8,40},{9,... | collective-permute-start | bytes 1966088 | tf_op jit(solution)/shard_map/ppermute | solution.py:66
  136.4 10.4 %collective-permute-start.8 = (f32[640,128]{1,0:T(8,128)S(1)}, f32[640,128]{1,0:T(8,128)S(1)}, u32[]{:S(2)}, u32[]{:S(2)}) collective-permute-start(f32[640,128]{1,0:T(8,128)S(1)} %slice_select_fusion.1), channel_id=1, source_target_pairs={{0,64},{64,0},{128,192},{192,128},{256,320},{320,256},{384,448},{4... | collective-permute-start | bytes 983048 | tf_op jit(solution)/shard_map/ppermute | solution.py:66
  146.8 6.1 %collective-permute-start.9 = (f32[320,128]{1,0:T(8,128)S(1)}, f32[320,128]{1,0:T(8,128)S(1)}, u32[]{:S(2)}, u32[]{:S(2)}) collective-permute-start(f32[320,128]{1,0:T(8,128)S(1)} %slice_select_fusion.2), channel_id=1, source_target_pairs={{0,2},{1,3},{2,0},{3,1},{4,6},{5,7},{6,4},{7,5},{8,10},{9,11},{10,... | collective-permute-start | bytes 491528 | tf_op jit(solution)/shard_map/ppermute | solution.py:66
  152.9 67.6 %copy-start.14 = (bf16[256,512]{1,0:T(8,128)(2,1)S(1)}, bf16[256,512]{1,0:T(8,128)(2,1)}, u32[]{:S(2)}) copy-start(bf16[256,512]{1,0:T(8,128)(2,1)} %param.10) | copy-start | bytes 786436
  152.9 67.6 %copy-start.22 = (bf16[1024,256]{0,1:T(8,128)(2,1)S(1)}, bf16[1024,256]{0,1:T(8,128)(2,1)}, u32[]{:S(2)}) copy-start(bf16[1024,256]{0,1:T(8,128)(2,1)} %copy-done.21) | copy-start | bytes 1572868
  152.9 67.6 %copy-start.24 = (bf16[1024,256]{0,1:T(8,128)(2,1)S(1)}, bf16[1024,256]{0,1:T(8,128)(2,1)}, u32[]{:S(2)}) copy-start(bf16[1024,256]{0,1:T(8,128)(2,1)} %copy-done.23) | copy-start | bytes 1572868
  153.0 6.8 %collective-permute-start.10 = (f32[160,128]{1,0:T(8,128)S(1)}, f32[160,128]{1,0:T(8,128)S(1)}, u32[]{:S(2)}, u32[]{:S(2)}) collective-permute-start(f32[160,128]{1,0:T(8,128)S(1)} %slice_select_fusion.3), channel_id=1, source_target_pairs={{0,256},{64,320},{128,384},{192,448},{256,0},{320,64},{384,128},{4... | collective-permute-start | bytes 245768 | tf_op jit(solution)/shard_map/ppermute | solution.py:66
  159.8 6.3 %collective-permute-start.11 = (f32[80,128]{1,0:T(8,128)S(1)}, f32[80,128]{1,0:T(8,128)S(1)}, u32[]{:S(2)}, u32[]{:S(2)}) collective-permute-start(f32[80,128]{1,0:T(8,128)S(1)} %slice_select_fusion.4), channel_id=1, source_target_pairs={{0,128},{64,192},{128,0},{192,64},{256,384},{320,448},{384,256},{4... | collective-permute-start | bytes 122888 | tf_op jit(solution)/shard_map/ppermute | solution.py:66
  166.1 5.7 %collective-permute-start.12 = (f32[80,128]{1,0:T(8,128)S(1)}, f32[80,128]{1,0:T(8,128)S(1)}, u32[]{:S(2)}, u32[]{:S(2)}) collective-permute-start(f32[80,128]{1,0:T(8,128)S(1)} %select_add_fusion.5), channel_id=1, source_target_pairs={{0,4},{1,5},{2,6},{3,7},{4,0},{5,1},{6,2},{7,3},{8,12},{9,13},{10,... | collective-permute-start | bytes 122888 | tf_op jit(solution)/shard_map/ppermute | solution.py:66
  171.8 8.6 %collective-permute-start.13 = (f32[80,128]{1,0:T(8,128)S(1)}, f32[80,128]{1,0:T(8,128)S(1)}, u32[]{:S(2)}, u32[]{:S(2)}) collective-permute-start(f32[80,128]{1,0:T(8,128)S(1)} %add.97), channel_id=1, source_target_pairs={{0,8},{1,9},{2,10},{3,11},{4,12},{5,13},{6,14},{7,15},{8,0},{9,1},... | collective-permute-start | bytes 122888 | tf_op jit(solution)/shard_map/ppermute | solution.py:66
  180.4 13.6 %collective-permute-start.14 = (f32[80,128]{1,0:T(8,128)S(1)}, f32[80,128]{1,0:T(8,128)S(1)}, u32[]{:S(2)}, u32[]{:S(2)}) collective-permute-start(f32[80,128]{1,0:T(8,128)S(1)} %add.98), channel_id=1, source_target_pairs={{0,16},{1,17},{2,18},{3,19},{4,20},{5,21},{6,22},{7,23},{8,24},{9,... | collective-permute-start | bytes 122888 | tf_op jit(solution)/shard_map/ppermute | solution.py:66
  194.0 6.3 %collective-permute-start.15 = (bf16[80,128]{1,0:T(8,128)(2,1)S(1)}, bf16[80,128]{1,0:T(8,128)(2,1)S(1)}, u32[]{:S(2)}, u32[]{:S(2)}) collective-permute-start(bf16[80,128]{1,0:T(8,128)(2,1)S(1)} %multiply_convert_fusion.11), channel_id=1, source_target_pairs={{0,128},{64,192},{128,0},{192,64},{256,384},{320,448},{384,256},{4... | collective-permute-start | bytes 61448 | tf_op jit(solution)/shard_map/ppermute | solution.py:66
  200.3 6.3 %collective-permute-start.16 = (bf16[160,128]{1,0:T(8,128)(2,1)S(1)}, bf16[160,128]{1,0:T(8,128)(2,1)S(1)}, u32[]{:S(2)}, u32[]{:S(2)}) collective-permute-start(bf16[160,128]{1,0:T(8,128)(2,1)S(1)} %maximum_select_fusion.5), channel_id=1, source_target_pairs={{0,256},{64,320},{128,384},{192,448},{256,0},{320,64},{384,128},{4... | collective-permute-start | bytes 122888 | tf_op jit(solution)/shard_map/ppermute | solution.py:66
  206.6 5.3 %collective-permute-start.17 = (bf16[320,128]{1,0:T(8,128)(2,1)S(1)}, bf16[320,128]{1,0:T(8,128)(2,1)S(1)}, u32[]{:S(2)}, u32[]{:S(2)}) collective-permute-start(bf16[320,128]{1,0:T(8,128)(2,1)S(1)} %maximum_select_fusion.4), channel_id=1, source_target_pairs={{0,2},{1,3},{2,0},{3,1},{4,6},{5,7},{6,4},{7,5},{8,10},{9,11},{10,... | collective-permute-start | bytes 245768 | tf_op jit(solution)/shard_map/ppermute | solution.py:66
  212.0 6.1 %collective-permute-start.18 = (bf16[640,128]{1,0:T(8,128)(2,1)S(1)}, bf16[640,128]{1,0:T(8,128)(2,1)S(1)}, u32[]{:S(2)}, u32[]{:S(2)}) collective-permute-start(bf16[640,128]{1,0:T(8,128)(2,1)S(1)} %maximum_select_fusion.3), channel_id=1, source_target_pairs={{0,64},{64,0},{128,192},{192,128},{256,320},{320,256},{384,448},{4... | collective-permute-start | bytes 491528 | tf_op jit(solution)/shard_map/ppermute | solution.py:66
  218.1 7.8 %collective-permute-start.19 = (bf16[1280,128]{1,0:T(8,128)(2,1)S(1)}, bf16[1280,128]{1,0:T(8,128)(2,1)S(1)}, u32[]{:S(2)}, u32[]{:S(2)}) collective-permute-start(bf16[1280,128]{1,0:T(8,128)(2,1)S(1)} %maximum_select_fusion.2), channel_id=1, source_target_pairs={{0,32},{1,33},{2,34},{3,35},{4,36},{5,37},{6,38},{7,39},{8,40},{9,... | collective-permute-start | bytes 983048 | tf_op jit(solution)/shard_map/ppermute | solution.py:66
  226.1 24.8 %collective-permute-start.20 = (bf16[2560,128]{1,0:T(8,128)(2,1)S(1)}, bf16[2560,128]{1,0:T(8,128)(2,1)S(1)}, u32[]{:S(2)}, u32[]{:S(2)}) collective-permute-start(bf16[2560,128]{1,0:T(8,128)(2,1)S(1)} %maximum_select_fusion.1), channel_id=1, source_target_pairs={{0,1},{1,0},{2,3},{3,2},{4,5},{5,4},{6,7},{7,6},{8,9},{9,8},{10,11... | collective-permute-start | bytes 1966088 | tf_op jit(solution)/shard_map/ppermute | solution.py:66
  241.9 7.7 %collective-permute-start.5 = (bf16[1,512,256]{2,1,0:T(8,128)(2,1)S(1)}, bf16[1,512,256]{2,1,0:T(8,128)(2,1)S(1)}, u32[]{:S(2)}, u32[]{:S(2)}) collective-permute-start(bf16[1,512,256]{2,1,0:T(8,128)(2,1)S(1)} %get-tuple-element.22), channel_id=1, source_target_pairs={{1,0},{2,1},{3,2},{4,3},{5,4},{6,5},{7,6},{8,7},{9,8},{10,9},{11,1... | collective-permute-start | bytes 786440 | tf_op jit(solution)/shard_map/ppermute | solution.py:15
  (22 other events, 163.9 us)

commit v5 on v4

--- a/solution.py
+++ b/solution.py
@@ -57,7 +57,8 @@
     return (local_grad, ahead_rows, (past_term, now_term, mix_term))
 
 
-HALVING_STEPS = (("tm", 1), ("tm", 32), ("dp", 1), ("tm", 2), ("dp", 4), ("dp", 2))
+EARLY_STEPS = (("tm", 1), ("tm", 32))
+HALVING_STEPS = (("dp", 1), ("tm", 2), ("dp", 4), ("dp", 2))
 BUTTERFLY_STEPS = (("tm", 4), ("tm", 8), ("tm", 16))
 
 
@@ -66,29 +67,47 @@
     return lax.ppermute(value, axis, [(source, source ^ mask) for source in range(count)])
 
 
-def reduce_grads(term_list, scale_factor):
-    shapes = [member.shape for member in term_list]
-    flat = jnp.concatenate([member.reshape(-1, 128) for member in term_list])
-    for axis, mask in HALVING_STEPS:
+def halve(flat, steps):
+    for axis, mask in steps:
         half = flat.shape[0] // 2
         upper = (lax.axis_index(axis) & mask) != 0
         first, second = flat[:half], flat[half:]
         kept = jnp.where(upper, second, first)
         sent = jnp.where(upper, first, second)
         flat = kept + exchange(sent, axis, mask)
-    for axis, mask in BUTTERFLY_STEPS:
-        flat = flat + exchange(flat, axis, mask)
-    flat = (flat * scale_factor).astype(jnp.bfloat16)
-    for axis, mask in reversed(HALVING_STEPS):
+    return flat
+
+
+def double(flat, steps):
+    for axis, mask in reversed(steps):
         upper = (lax.axis_index(axis) & mask) != 0
         other = exchange(flat, axis, mask)
         flat = jnp.where(upper, jnp.concatenate([other, flat]), jnp.concatenate([flat, other]))
-    out, start = [], 0
-    for shape in shapes:
-        rows = shape[0] * shape[1] // 128
-        out.append(flat[start:start + rows].reshape(shape))
-        start += rows
-    return tuple(out)
+    return flat
+
+
+def pack(term_list):
+    width = term_list[0].shape[1]
+    return jnp.concatenate([member.reshape(-1, width) for member in term_list])
+
+
+def reduce_packed(early_pieces, shapes, scale_factor):
+    joined = halve(jnp.concatenate(early_pieces), HALVING_STEPS)
+    for axis, mask in BUTTERFLY_STEPS:
+        joined = joined + exchange(joined, axis, mask)
+    joined = (joined * scale_factor).astype(jnp.bfloat16)
+    joined = double(joined, EARLY_STEPS + HALVING_STEPS)
+    layers, early = len(early_pieces), 1 << len(EARLY_STEPS)
+    block = joined.shape[0] // (layers * early)
+    outputs = []
+    for layer, layer_shapes in enumerate(shapes):
+        rows = jnp.concatenate([joined[(index * layers + layer) * block:(index * layers + layer + 1) * block] for index in range(early)])
+        start = 0
+        for shape in layer_shapes:
+            count = shape[0] * shape[1] // rows.shape[1]
+            outputs.append(rows[start:start + count].reshape(shape))
+            start += count
+    return tuple(outputs)
 
 
 def body(
@@ -126,6 +145,8 @@
         if chunk:
             hidden_chunk, _ = lax.optimization_barrier((hidden_chunk, past_parts[-1]))
         past_chunk = shifted(hidden_chunk, "tm", distant_offsets)
+        if chunk:
+            past_chunk, arrived_parts[-1] = lax.optimization_barrier((past_chunk, arrived_parts[-1]))
         past_parts.append(past_chunk)
         chunk_stash = forward_layer(
             hidden_chunk,
@@ -150,6 +171,8 @@
     arrived_back = jnp.concatenate(arrived_parts, axis=1)
     second_layer_terms = tuple(first + second for first, second in zip(*term_parts))
     hidden_gradient = (local_two + arrived_back.astype(jnp.float32)).astype(jnp.bfloat16)
+    early_two = halve(pack(second_layer_terms), EARLY_STEPS)
+    hidden_gradient, early_two = lax.optimization_barrier((hidden_gradient, early_two))
     local_one, forward_rows_first, first_layer_terms = backward_layer(
         signal,
         first_history_rows,
@@ -165,7 +188,9 @@
         [forward_rows_first[:, FIRST_DILATION:, :], received_head_rows], axis=1
     )
     grad_signal = (local_one + trailing_later_rows.astype(jnp.float32)).astype(jnp.bfloat16)
-    reduced = reduce_grads(tuple(first_layer_terms) + tuple(second_layer_terms), scale_factor)
+    early_one = halve(pack(first_layer_terms), EARLY_STEPS)
+    shapes = ([member.shape for member in first_layer_terms], [member.shape for member in second_layer_terms])
+    reduced = reduce_packed([early_one, early_two], shapes, scale_factor)
     reduced_one, reduced_two = reduced[:3], reduced[3:]
     return (
         grad_signal,

time: 257 us -> 266 us (1.035)
  local copies, waits for them, and re-layouts: 18.8 us -> 6.86 us
  waiting for transfers between devices: 76 us -> 86 us
  starting transfers between devices: 136 us -> 144 us
  other arithmetic: 4.67 us -> 8.51 us
    ppermute x6, waiting for transfers between devices: 20.8 us -> 33 us  [shifted(): lax.ppermute(value, axis, [(source, source + steps) for source in range(l...]
    ppermute x15 -> x17, starting transfers between devices: 111 us -> 119 us  [exchange(): lax.ppermute(value, axis, [(source, source ^ mask) for source in range(co...]
    reshape x12 -> x4, local copies, waits for them, and re-layouts: 10.4 us -> 3.21 us  [the longest x2 1.8 us: pack(): return jnp.concatenate([member.reshape(-1, width) for member in term_list])]
    unnamed x54 -> x64, local copies, waits for them, and re-layouts: 6.23 us -> 2.35 us
    ppermute x15 -> x17, waiting for transfers between devices: 55.2 us -> 52.9 us  [exchange(): lax.ppermute(value, axis, [(source, source ^ mask) for source in range(co...]
  transfers between devices with their start and end apart: 21 -> 23, of which waited for: 18 -> 19; matrix products, arithmetic and copies ran while one was open for 8% -> 3% of each run, Pallas kernels for 0% -> 0%
where the time goes in v5:
time: 266 us; the launch traced here: 265 us
  starting transfers between devices  144 us (54%)
  waiting for transfers between devices  86 us (32%)
  matrix products  17.9 us (7%)
  other arithmetic  8.51 us (3%)
  local copies, waits for them, and re-layouts  6.86 us (3%)
    ppermute x17, starting transfers between devices, exchange(): lax.ppermute(value, axis, [(source, source ^ mask) for source in range(co...  119 us
    ppermute x17, waiting for transfers between devices, exchange(): lax.ppermute(value, axis, [(source, source ^ mask) for source in range(co...  52.9 us
    ppermute x6, waiting for transfers between devices, shifted(): lax.ppermute(value, axis, [(source, source + steps) for source in range(l...  33 us
    ppermute x6, starting transfers between devices, shifted(): lax.ppermute(value, axis, [(source, source + steps) for source in range(l...  25.6 us
  transfers between devices with their start and end apart: 23, of which 19 were waited for; matrix products, arithmetic and copies ran while one was open for 3% of the time, Pallas kernels for 0%

profile of v5, /device:TPU:1, one launch (start us, length us, event | category | flops | bytes accessed | tf_op | source)
XLA Modules:
  0.0 265.0 jit_solution(17155326270240825251)
XLA Ops:
  1.8 4.9 %collective-permute-start = (bf16[1,512,256]{2,1,0:T(8,128)(2,1)S(1)}, bf16[1,512,256]{2,1,0:T(8,128)(2,1)S(1)}, u32[]{:S(2)}, u32[]{:S(2)}) collective-permute-start(bf16[1,512,256]{2,1,0:T(8,128)(2,1)S(1)} %get-tuple-element.39), channel_id=1, source_target_pairs={{0,1},{1,2},{2,3},{3,4},{4,5},{5,6},{6,7},{7,8},{8,9},{9,10},{10,1... | collective-permute-start | bytes 786440 | tf_op jit(solution)/shard_map/ppermute | solution.py:15
  13.2 8.0 %collective-permute-start.1 = (bf16[1,512,256]{2,1,0:T(8,128)(2,1)S(1)}, bf16[1,512,256]{2,1,0:T(8,128)(2,1)S(1)}, u32[]{:S(2)}, u32[]{:S(2)}) collective-permute-start(bf16[1,512,256]{2,1,0:T(8,128)(2,1)S(1)} %get-tuple-element.37), channel_id=1, source_target_pairs={{0,8},{1,9},{2,10},{3,11},{4,12},{5,13},{6,14},{7,15},{8,16},{9,17... | collective-permute-start | bytes 786440 | tf_op jit(solution)/shard_map/ppermute | solution.py:15
  21.6 5.2 %collective-permute-done.1 = bf16[1,512,256]{2,1,0:T(8,128)(2,1)S(1)} collective-permute-done((bf16[1,512,256]{2,1,0:T(8,128)(2,1)S(1)}, bf16[1,512,256]{2,1,0:T(8,128)(2,1)S(1)}, u32[]{:S(2)}, u32[]{:S(2)}) %collective-permute-start.1) | collective-permute-done | bytes 262176 | tf_op jit(solution)/shard_map/ppermute | solution.py:15
  29.2 8.0 %collective-permute-start.2 = (bf16[1,512,256]{2,1,0:T(8,128)(2,1)S(1)}, bf16[1,512,256]{2,1,0:T(8,128)(2,1)S(1)}, u32[]{:S(2)}, u32[]{:S(2)}) collective-permute-start(bf16[1,512,256]{2,1,0:T(8,128)(2,1)S(1)} %get-tuple-element.12), channel_id=1, source_target_pairs={{0,8},{1,9},{2,10},{3,11},{4,12},{5,13},{6,14},{7,15},{8,16},{9,17... | collective-permute-start | bytes 786440 | tf_op jit(solution)/shard_map/ppermute | solution.py:15
  38.9 9.7 %collective-permute-done.2 = bf16[1,512,256]{2,1,0:T(8,128)(2,1)S(1)} collective-permute-done((bf16[1,512,256]{2,1,0:T(8,128)(2,1)S(1)}, bf16[1,512,256]{2,1,0:T(8,128)(2,1)S(1)}, u32[]{:S(2)}, u32[]{:S(2)}) %collective-permute-start.2) | collective-permute-done | bytes 262176 | tf_op jit(solution)/shard_map/ppermute | solution.py:15
  58.0 30.6 %collective-permute-start.5 = (f32[320,512]{1,0:T(8,128)}, f32[320,512]{1,0:T(8,128)}, u32[]{:S(2)}, u32[]{:S(2)}) collective-permute-start(f32[320,512]{1,0:T(8,128)} %fusion.25), channel_id=1, source_target_pairs={{0,1},{1,0},{2,3},{3,2},{4,5},{5,4},{6,7},{7,6},{8,9},{9,8},{10,11... | collective-permute-start | bytes 1966088 | tf_op jit(solution)/shard_map/ppermute | solution.py:67
  93.1 6.0 %collective-permute-start.6 = (f32[160,512]{1,0:T(8,128)S(1)}, f32[160,512]{1,0:T(8,128)S(1)}, u32[]{:S(2)}, u32[]{:S(2)}) collective-permute-start(f32[160,512]{1,0:T(8,128)S(1)} %slice_select_fusion.1), channel_id=1, source_target_pairs={{0,32},{1,33},{2,34},{3,35},{4,36},{5,37},{6,38},{7,39},{8,40},{9,... | collective-permute-start | bytes 983048 | tf_op jit(solution)/shard_map/ppermute | solution.py:67
  99.9 9.7 %collective-permute-done.4 = bf16[1,512,256]{2,1,0:T(8,128)(2,1)S(1)} collective-permute-done((bf16[1,512,256]{2,1,0:T(8,128)(2,1)S(1)}, bf16[1,512,256]{2,1,0:T(8,128)(2,1)S(1)}, u32[]{:S(2)}, u32[]{:S(2)}) %collective-permute-start.4) | collective-permute-done | bytes 262176 | tf_op jit(solution)/shard_map/ppermute | solution.py:15
  120.9 4.2 %collective-permute-start.9 = (f32[160,512]{1,0:T(8,128)S(1)}, f32[160,512]{1,0:T(8,128)S(1)}, u32[]{:S(2)}, u32[]{:S(2)}) collective-permute-start(f32[160,512]{1,0:T(8,128)S(1)} %slice_select_fusion), channel_id=1, source_target_pairs={{0,32},{1,33},{2,34},{3,35},{4,36},{5,37},{6,38},{7,39},{8,40},{9,... | collective-permute-start | bytes 983048 | tf_op jit(solution)/shard_map/ppermute | solution.py:67
  125.1 7.8 %collective-permute-done.9 = f32[160,512]{1,0:T(8,128)S(1)} collective-permute-done((f32[160,512]{1,0:T(8,128)S(1)}, f32[160,512]{1,0:T(8,128)S(1)}, u32[]{:S(2)}, u32[]{:S(2)}) %collective-permute-start.9) | collective-permute-done | bytes 327712 | tf_op jit(solution)/shard_map/ppermute | solution.py:67
  136.3 6.9 %collective-permute-done.10 = f32[160,512]{1,0:T(8,128)S(1)} collective-permute-done((f32[160,512]{1,0:T(8,128)S(1)}, f32[160,512]{1,0:T(8,128)S(1)}, u32[]{:S(2)}, u32[]{:S(2)}) %collective-permute-start.10) | collective-permute-done | bytes 327712 | tf_op jit(solution)/shard_map/ppermute | solution.py:67
  145.4 4.1 %collective-permute-done.11 = f32[80,512]{1,0:T(8,128)S(1)} collective-permute-done((f32[80,512]{1,0:T(8,128)S(1)}, f32[80,512]{1,0:T(8,128)S(1)}, u32[]{:S(2)}, u32[]{:S(2)}) %collective-permute-start.11) | collective-permute-done | bytes 163872 | tf_op jit(solution)/shard_map/ppermute | solution.py:67
  149.6 11.8 %collective-permute-start.12 = (f32[40,512]{1,0:T(8,128)S(1)}, f32[40,512]{1,0:T(8,128)S(1)}, u32[]{:S(2)}, u32[]{:S(2)}) collective-permute-start(f32[40,512]{1,0:T(8,128)S(1)} %slice_select_fusion.3), channel_id=1, source_target_pairs={{0,256},{64,320},{128,384},{192,448},{256,0},{320,64},{384,128},{4... | collective-permute-start | bytes 245768 | tf_op jit(solution)/shard_map/ppermute | solution.py:67
  163.3 4.8 %collective-permute-start.13 = (f32[20,512]{1,0:T(8,128)S(1)}, f32[20,512]{1,0:T(8,128)S(1)}, u32[]{:S(2)}, u32[]{:S(2)}) collective-permute-start(f32[20,512]{1,0:T(8,128)S(1)} %slice_select_fusion.4), channel_id=1, source_target_pairs={{0,128},{64,192},{128,0},{192,64},{256,384},{320,448},{384,256},{4... | collective-permute-start | bytes 122888 | tf_op jit(solution)/shard_map/ppermute | solution.py:67
  169.7 10.3 %collective-permute-start.14 = (f32[20,512]{1,0:T(8,128)S(1)}, f32[20,512]{1,0:T(8,128)S(1)}, u32[]{:S(2)}, u32[]{:S(2)}) collective-permute-start(f32[20,512]{1,0:T(8,128)S(1)} %select_add_fusion.7), channel_id=1, source_target_pairs={{0,4},{1,5},{2,6},{3,7},{4,0},{5,1},{6,2},{7,3},{8,12},{9,13},{10,... | collective-permute-start | bytes 122888 | tf_op jit(solution)/shard_map/ppermute | solution.py:67
  181.4 6.7 %collective-permute-start.15 = (f32[20,512]{1,0:T(8,128)S(1)}, f32[20,512]{1,0:T(8,128)S(1)}, u32[]{:S(2)}, u32[]{:S(2)}) collective-permute-start(f32[20,512]{1,0:T(8,128)S(1)} %add.110), channel_id=1, source_target_pairs={{0,8},{1,9},{2,10},{3,11},{4,12},{5,13},{6,14},{7,15},{8,0},{9,1},... | collective-permute-start | bytes 122888 | tf_op jit(solution)/shard_map/ppermute | solution.py:67
  192.6 11.2 %collective-permute-done.16 = f32[20,512]{1,0:T(8,128)S(1)} collective-permute-done((f32[20,512]{1,0:T(8,128)S(1)}, f32[20,512]{1,0:T(8,128)S(1)}, u32[]{:S(2)}, u32[]{:S(2)}) %collective-permute-start.16) | collective-permute-done | bytes 40992 | tf_op jit(solution)/shard_map/ppermute | solution.py:67
  203.8 4.8 %collective-permute-start.17 = (bf16[20,512]{1,0:T(8,128)(2,1)S(1)}, bf16[20,512]{1,0:T(8,128)(2,1)S(1)}, u32[]{:S(2)}, u32[]{:S(2)}) collective-permute-start(bf16[20,512]{1,0:T(8,128)(2,1)S(1)} %multiply_convert_fusion.11), channel_id=1, source_target_pairs={{0,128},{64,192},{128,0},{192,64},{256,384},{320,448},{384,256},{4... | collective-permute-start | bytes 61448 | tf_op jit(solution)/shard_map/ppermute | solution.py:67
  212.2 4.3 %collective-permute-done.18 = bf16[40,512]{1,0:T(8,128)(2,1)S(1)} collective-permute-done((bf16[40,512]{1,0:T(8,128)(2,1)S(1)}, bf16[40,512]{1,0:T(8,128)(2,1)S(1)}, u32[]{:S(2)}, u32[]{:S(2)}) %collective-permute-start.18) | collective-permute-done | bytes 40992 | tf_op jit(solution)/shard_map/ppermute | solution.py:67
  216.5 4.4 %collective-permute-start.19 = (bf16[80,512]{1,0:T(8,128)(2,1)S(1)}, bf16[80,512]{1,0:T(8,128)(2,1)S(1)}, u32[]{:S(2)}, u32[]{:S(2)}) collective-permute-start(bf16[80,512]{1,0:T(8,128)(2,1)S(1)} %maximum_select_fusion.4), channel_id=1, source_target_pairs={{0,2},{1,3},{2,0},{3,1},{4,6},{5,7},{6,4},{7,5},{8,10},{9,11},{10,... | collective-permute-start | bytes 245768 | tf_op jit(solution)/shard_map/ppermute | solution.py:67
  228.9 3.5 %collective-permute-start.21 = (bf16[320,512]{1,0:T(8,128)(2,1)S(1)}, bf16[320,512]{1,0:T(8,128)(2,1)S(1)}, u32[]{:S(2)}, u32[]{:S(2)}) collective-permute-start(bf16[320,512]{1,0:T(8,128)(2,1)S(1)} %maximum_select_fusion.2), channel_id=1, source_target_pairs={{0,32},{1,33},{2,34},{3,35},{4,36},{5,37},{6,38},{7,39},{8,40},{9,... | collective-permute-start | bytes 983048 | tf_op jit(solution)/shard_map/ppermute | solution.py:67
  233.0 3.9 %collective-permute-done.21 = bf16[320,512]{1,0:T(8,128)(2,1)S(1)} collective-permute-done((bf16[320,512]{1,0:T(8,128)(2,1)S(1)}, bf16[320,512]{1,0:T(8,128)(2,1)S(1)}, u32[]{:S(2)}, u32[]{:S(2)}) %collective-permute-start.21) | collective-permute-done | bytes 327712 | tf_op jit(solution)/shard_map/ppermute | solution.py:67
  237.2 15.6 %collective-permute-start.22 = (bf16[640,512]{1,0:T(8,128)(2,1)S(1)}, bf16[640,512]{1,0:T(8,128)(2,1)S(1)}, u32[]{:S(2)}, u32[]{:S(2)}) collective-permute-start(bf16[640,512]{1,0:T(8,128)(2,1)S(1)} %maximum_select_fusion.1), channel_id=1, source_target_pairs={{0,1},{1,0},{2,3},{3,2},{4,5},{5,4},{6,7},{7,6},{8,9},{9,8},{10,11... | collective-permute-start | bytes 1966088 | tf_op jit(solution)/shard_map/ppermute | solution.py:67
  254.8 5.8 %collective-permute-done.7 = bf16[1,512,256]{2,1,0:T(8,128)(2,1)S(1)} collective-permute-done((bf16[1,512,256]{2,1,0:T(8,128)(2,1)S(1)}, bf16[1,512,256]{2,1,0:T(8,128)(2,1)S(1)}, u32[]{:S(2)}, u32[]{:S(2)}) %collective-permute-start.7) | collective-permute-done | bytes 262176 | tf_op jit(solution)/shard_map/ppermute | solution.py:15
  (147 shorter events, 70.9 us)
Async XLA Ops:
  1.8 9.2 %collective-permute-start = (bf16[1,512,256]{2,1,0:T(8,128)(2,1)S(1)}, bf16[1,512,256]{2,1,0:T(8,128)(2,1)S(1)}, u32[]{:S(2)}, u32[]{:S(2)}) collective-permute-start(bf16[1,512,256]{2,1,0:T(8,128)(2,1)S(1)} %get-tuple-element.39), channel_id=1, source_target_pairs={{0,1},{1,2},{2,3},{3,4},{4,5},{5,6},{6,7},{7,8},{8,9},{9,10},{10,1... | collective-permute-start | bytes 786440 | tf_op jit(solution)/shard_map/ppermute | solution.py:15
  13.2 13.6 %collective-permute-start.1 = (bf16[1,512,256]{2,1,0:T(8,128)(2,1)S(1)}, bf16[1,512,256]{2,1,0:T(8,128)(2,1)S(1)}, u32[]{:S(2)}, u32[]{:S(2)}) collective-permute-start(bf16[1,512,256]{2,1,0:T(8,128)(2,1)S(1)} %get-tuple-element.37), channel_id=1, source_target_pairs={{0,8},{1,9},{2,10},{3,11},{4,12},{5,13},{6,14},{7,15},{8,16},{9,17... | collective-permute-start | bytes 786440 | tf_op jit(solution)/shard_map/ppermute | solution.py:15
  29.2 19.4 %collective-permute-start.2 = (bf16[1,512,256]{2,1,0:T(8,128)(2,1)S(1)}, bf16[1,512,256]{2,1,0:T(8,128)(2,1)S(1)}, u32[]{:S(2)}, u32[]{:S(2)}) collective-permute-start(bf16[1,512,256]{2,1,0:T(8,128)(2,1)S(1)} %get-tuple-element.12), channel_id=1, source_target_pairs={{0,8},{1,9},{2,10},{3,11},{4,12},{5,13},{6,14},{7,15},{8,16},{9,17... | collective-permute-start | bytes 786440 | tf_op jit(solution)/shard_map/ppermute | solution.py:15
  37.2 11.3 %collective-permute-start.3 = (bf16[1,512,256]{2,1,0:T(8,128)(2,1)S(1)}, bf16[1,512,256]{2,1,0:T(8,128)(2,1)}, u32[]{:S(2)}, u32[]{:S(2)}) collective-permute-start(bf16[1,512,256]{2,1,0:T(8,128)(2,1)S(1)} %fusion.5), channel_id=1, source_target_pairs={{8,0},{9,1},{10,2},{11,3},{12,4},{13,5},{14,6},{15,7},{16,8},{17,9... | collective-permute-start | bytes 786440 | tf_op jit(solution)/shard_map/ppermute | solution.py:15
  58.0 33.5 %collective-permute-start.5 = (f32[320,512]{1,0:T(8,128)}, f32[320,512]{1,0:T(8,128)}, u32[]{:S(2)}, u32[]{:S(2)}) collective-permute-start(f32[320,512]{1,0:T(8,128)} %fusion.25), channel_id=1, source_target_pairs={{0,1},{1,0},{2,3},{3,2},{4,5},{5,4},{6,7},{7,6},{8,9},{9,8},{10,11... | collective-permute-start | bytes 1966088 | tf_op jit(solution)/shard_map/ppermute | solution.py:67
  90.1 19.5 %collective-permute-start.4 = (bf16[1,512,256]{2,1,0:T(8,128)(2,1)S(1)}, bf16[1,512,256]{2,1,0:T(8,128)(2,1)S(1)}, u32[]{:S(2)}, u32[]{:S(2)}) collective-permute-start(bf16[1,512,256]{2,1,0:T(8,128)(2,1)S(1)} %fusion.6), channel_id=1, source_target_pairs={{8,0},{9,1},{10,2},{11,3},{12,4},{13,5},{14,6},{15,7},{16,8},{17,9... | collective-permute-start | bytes 786440 | tf_op jit(solution)/shard_map/ppermute | solution.py:15
  93.1 17.6 %collective-permute-start.6 = (f32[160,512]{1,0:T(8,128)S(1)}, f32[160,512]{1,0:T(8,128)S(1)}, u32[]{:S(2)}, u32[]{:S(2)}) collective-permute-start(f32[160,512]{1,0:T(8,128)S(1)} %slice_select_fusion.1), channel_id=1, source_target_pairs={{0,32},{1,33},{2,34},{3,35},{4,36},{5,37},{6,38},{7,39},{8,40},{9,... | collective-permute-start | bytes 983048 | tf_op jit(solution)/shard_map/ppermute | solution.py:67
  116.1 4.5 %collective-permute-start.8 = (f32[320,512]{1,0:T(8,128)S(1)}, f32[320,512]{1,0:T(8,128)S(1)}, u32[]{:S(2)}, u32[]{:S(2)}) collective-permute-start(f32[320,512]{1,0:T(8,128)S(1)} %fusion.26), channel_id=1, source_target_pairs={{0,1},{1,0},{2,3},{3,2},{4,5},{5,4},{6,7},{7,6},{8,9},{9,8},{10,11... | collective-permute-start | bytes 1966088 | tf_op jit(solution)/shard_map/ppermute | solution.py:67
  120.9 12.0 %collective-permute-start.9 = (f32[160,512]{1,0:T(8,128)S(1)}, f32[160,512]{1,0:T(8,128)S(1)}, u32[]{:S(2)}, u32[]{:S(2)}) collective-permute-start(f32[160,512]{1,0:T(8,128)S(1)} %slice_select_fusion), channel_id=1, source_target_pairs={{0,32},{1,33},{2,34},{3,35},{4,36},{5,37},{6,38},{7,39},{8,40},{9,... | collective-permute-start | bytes 983048 | tf_op jit(solution)/shard_map/ppermute | solution.py:67
  133.0 10.2 %collective-permute-start.10 = (f32[160,512]{1,0:T(8,128)S(1)}, f32[160,512]{1,0:T(8,128)S(1)}, u32[]{:S(2)}, u32[]{:S(2)}) collective-permute-start(f32[160,512]{1,0:T(8,128)S(1)} %get-tuple-element.17), channel_id=1, source_target_pairs={{0,64},{64,0},{128,192},{192,128},{256,320},{320,256},{384,448},{4... | collective-permute-start | bytes 983048 | tf_op jit(solution)/shard_map/ppermute | solution.py:67
  143.3 89.2 %copy-start.17 = (bf16[256,512]{1,0:T(8,128)(2,1)S(1)}, bf16[256,512]{1,0:T(8,128)(2,1)}, u32[]{:S(2)}) copy-start(bf16[256,512]{1,0:T(8,128)(2,1)} %param.10) | copy-start | bytes 786436
  143.4 6.2 %collective-permute-start.11 = (f32[80,512]{1,0:T(8,128)S(1)}, f32[80,512]{1,0:T(8,128)S(1)}, u32[]{:S(2)}, u32[]{:S(2)}) collective-permute-start(f32[80,512]{1,0:T(8,128)S(1)} %slice_select_fusion.2), channel_id=1, source_target_pairs={{0,2},{1,3},{2,0},{3,1},{4,6},{5,7},{6,4},{7,5},{8,10},{9,11},{10,... | collective-permute-start | bytes 491528 | tf_op jit(solution)/shard_map/ppermute | solution.py:67
  149.6 13.7 %collective-permute-start.12 = (f32[40,512]{1,0:T(8,128)S(1)}, f32[40,512]{1,0:T(8,128)S(1)}, u32[]{:S(2)}, u32[]{:S(2)}) collective-permute-start(f32[40,512]{1,0:T(8,128)S(1)} %slice_select_fusion.3), channel_id=1, source_target_pairs={{0,256},{64,320},{128,384},{192,448},{256,0},{320,64},{384,128},{4... | collective-permute-start | bytes 245768 | tf_op jit(solution)/shard_map/ppermute | solution.py:67
  163.3 6.3 %collective-permute-start.13 = (f32[20,512]{1,0:T(8,128)S(1)}, f32[20,512]{1,0:T(8,128)S(1)}, u32[]{:S(2)}, u32[]{:S(2)}) collective-permute-start(f32[20,512]{1,0:T(8,128)S(1)} %slice_select_fusion.4), channel_id=1, source_target_pairs={{0,128},{64,192},{128,0},{192,64},{256,384},{320,448},{384,256},{4... | collective-permute-start | bytes 122888 | tf_op jit(solution)/shard_map/ppermute | solution.py:67
  169.7 11.7 %collective-permute-start.14 = (f32[20,512]{1,0:T(8,128)S(1)}, f32[20,512]{1,0:T(8,128)S(1)}, u32[]{:S(2)}, u32[]{:S(2)}) collective-permute-start(f32[20,512]{1,0:T(8,128)S(1)} %select_add_fusion.7), channel_id=1, source_target_pairs={{0,4},{1,5},{2,6},{3,7},{4,0},{5,1},{6,2},{7,3},{8,12},{9,13},{10,... | collective-permute-start | bytes 122888 | tf_op jit(solution)/shard_map/ppermute | solution.py:67
  181.4 8.7 %collective-permute-start.15 = (f32[20,512]{1,0:T(8,128)S(1)}, f32[20,512]{1,0:T(8,128)S(1)}, u32[]{:S(2)}, u32[]{:S(2)}) collective-permute-start(f32[20,512]{1,0:T(8,128)S(1)} %add.110), channel_id=1, source_target_pairs={{0,8},{1,9},{2,10},{3,11},{4,12},{5,13},{6,14},{7,15},{8,0},{9,1},... | collective-permute-start | bytes 122888 | tf_op jit(solution)/shard_map/ppermute | solution.py:67
  190.2 13.7 %collective-permute-start.16 = (f32[20,512]{1,0:T(8,128)S(1)}, f32[20,512]{1,0:T(8,128)S(1)}, u32[]{:S(2)}, u32[]{:S(2)}) collective-permute-start(f32[20,512]{1,0:T(8,128)S(1)} %add.111), channel_id=1, source_target_pairs={{0,16},{1,17},{2,18},{3,19},{4,20},{5,21},{6,22},{7,23},{8,24},{9,... | collective-permute-start | bytes 122888 | tf_op jit(solution)/shard_map/ppermute | solution.py:67
  203.8 6.4 %collective-permute-start.17 = (bf16[20,512]{1,0:T(8,128)(2,1)S(1)}, bf16[20,512]{1,0:T(8,128)(2,1)S(1)}, u32[]{:S(2)}, u32[]{:S(2)}) collective-permute-start(bf16[20,512]{1,0:T(8,128)(2,1)S(1)} %multiply_convert_fusion.11), channel_id=1, source_target_pairs={{0,128},{64,192},{128,0},{192,64},{256,384},{320,448},{384,256},{4... | collective-permute-start | bytes 61448 | tf_op jit(solution)/shard_map/ppermute | solution.py:67
  210.2 6.3 %collective-permute-start.18 = (bf16[40,512]{1,0:T(8,128)(2,1)S(1)}, bf16[40,512]{1,0:T(8,128)(2,1)S(1)}, u32[]{:S(2)}, u32[]{:S(2)}) collective-permute-start(bf16[40,512]{1,0:T(8,128)(2,1)S(1)} %maximum_select_fusion.5), channel_id=1, source_target_pairs={{0,256},{64,320},{128,384},{192,448},{256,0},{320,64},{384,128},{4... | collective-permute-start | bytes 122888 | tf_op jit(solution)/shard_map/ppermute | solution.py:67
  216.5 6.2 %collective-permute-start.19 = (bf16[80,512]{1,0:T(8,128)(2,1)S(1)}, bf16[80,512]{1,0:T(8,128)(2,1)S(1)}, u32[]{:S(2)}, u32[]{:S(2)}) collective-permute-start(bf16[80,512]{1,0:T(8,128)(2,1)S(1)} %maximum_select_fusion.4), channel_id=1, source_target_pairs={{0,2},{1,3},{2,0},{3,1},{4,6},{5,7},{6,4},{7,5},{8,10},{9,11},{10,... | collective-permute-start | bytes 245768 | tf_op jit(solution)/shard_map/ppermute | solution.py:67
  222.8 6.1 %collective-permute-start.20 = (bf16[160,512]{1,0:T(8,128)(2,1)S(1)}, bf16[160,512]{1,0:T(8,128)(2,1)S(1)}, u32[]{:S(2)}, u32[]{:S(2)}) collective-permute-start(bf16[160,512]{1,0:T(8,128)(2,1)S(1)} %maximum_select_fusion.3), channel_id=1, source_target_pairs={{0,64},{64,0},{128,192},{192,128},{256,320},{320,256},{384,448},{4... | collective-permute-start | bytes 491528 | tf_op jit(solution)/shard_map/ppermute | solution.py:67
  228.9 8.0 %collective-permute-start.21 = (bf16[320,512]{1,0:T(8,128)(2,1)S(1)}, bf16[320,512]{1,0:T(8,128)(2,1)S(1)}, u32[]{:S(2)}, u32[]{:S(2)}) collective-permute-start(bf16[320,512]{1,0:T(8,128)(2,1)S(1)} %maximum_select_fusion.2), channel_id=1, source_target_pairs={{0,32},{1,33},{2,34},{3,35},{4,36},{5,37},{6,38},{7,39},{8,40},{9,... | collective-permute-start | bytes 983048 | tf_op jit(solution)/shard_map/ppermute | solution.py:67
  237.2 24.7 %collective-permute-start.22 = (bf16[640,512]{1,0:T(8,128)(2,1)S(1)}, bf16[640,512]{1,0:T(8,128)(2,1)S(1)}, u32[]{:S(2)}, u32[]{:S(2)}) collective-permute-start(bf16[640,512]{1,0:T(8,128)(2,1)S(1)} %maximum_select_fusion.1), channel_id=1, source_target_pairs={{0,1},{1,0},{2,3},{3,2},{4,5},{5,4},{6,7},{7,6},{8,9},{9,8},{10,11... | collective-permute-start | bytes 1966088 | tf_op jit(solution)/shard_map/ppermute | solution.py:67
  252.9 7.7 %collective-permute-start.7 = (bf16[1,512,256]{2,1,0:T(8,128)(2,1)S(1)}, bf16[1,512,256]{2,1,0:T(8,128)(2,1)S(1)}, u32[]{:S(2)}, u32[]{:S(2)}) collective-permute-start(bf16[1,512,256]{2,1,0:T(8,128)(2,1)S(1)} %get-tuple-element.36), channel_id=1, source_target_pairs={{1,0},{2,1},{3,2},{4,3},{5,4},{6,5},{7,6},{8,7},{9,8},{10,9},{11,1... | collective-permute-start | bytes 786440 | tf_op jit(solution)/shard_map/ppermute | solution.py:15
  (31 other events, 334.0 us)

commit v6 on v4

--- a/solution.py
+++ b/solution.py
@@ -58,6 +58,7 @@
 
 
 HALVING_STEPS = (("tm", 1), ("tm", 32), ("dp", 1), ("tm", 2), ("dp", 4), ("dp", 2))
+PACKED_WIDTH = 512
 BUTTERFLY_STEPS = (("tm", 4), ("tm", 8), ("tm", 16))
 
 
@@ -68,7 +69,7 @@
 
 def reduce_grads(term_list, scale_factor):
     shapes = [member.shape for member in term_list]
-    flat = jnp.concatenate([member.reshape(-1, 128) for member in term_list])
+    flat = jnp.concatenate([member.reshape(-1, PACKED_WIDTH) for member in term_list])
     for axis, mask in HALVING_STEPS:
         half = flat.shape[0] // 2
         upper = (lax.axis_index(axis) & mask) != 0
@@ -85,7 +86,7 @@
         flat = jnp.where(upper, jnp.concatenate([other, flat]), jnp.concatenate([flat, other]))
     out, start = [], 0
     for shape in shapes:
-        rows = shape[0] * shape[1] // 128
+        rows = shape[0] * shape[1] // PACKED_WIDTH
         out.append(flat[start:start + rows].reshape(shape))
         start += rows
     return tuple(out)

time: 257 us -> 256 us (level)
  waiting for transfers between devices: 76 us -> 128 us
  starting transfers between devices: 136 us -> 90.7 us
  local copies, waits for them, and re-layouts: 18.8 us -> 8.89 us
    ppermute x15, starting transfers between devices: 111 us -> 65.4 us  [exchange(): lax.ppermute(value, axis, [(source, source ^ mask) for source in range(co...]
    ppermute x6, waiting for transfers between devices: 20.8 us -> 62.2 us  [shifted(): lax.ppermute(value, axis, [(source, source + steps) for source in range(l...]
    ppermute x15, waiting for transfers between devices: 55.2 us -> 65.5 us  [exchange(): lax.ppermute(value, axis, [(source, source ^ mask) for source in range(co...]
    reshape x6 -> x2, local copies, waits for them, and re-layouts: 5.52 us -> 1.79 us  [reduce_grads(): member.reshape(-1, PACKED_WIDTH)]
    reshape x6 -> x2, local copies, waits for them, and re-layouts: 4.86 us -> 1.4 us  [reduce_grads(): out.append(flat[start:start + rows].reshape(shape))]
    unnamed x54 -> x62, local copies, waits for them, and re-layouts: 6.23 us -> 3.49 us
  transfers between devices with their start and end apart: 21 -> 21, of which waited for: 18 -> 19; matrix products, arithmetic and copies ran while one was open for 8% -> 6% of each run, Pallas kernels for 0% -> 0%
where the time goes in v6:
time: 256 us; the launch traced here: 255 us
  waiting for transfers between devices  128 us (50%)
  starting transfers between devices  90.7 us (35%)
  matrix products  20.1 us (8%)
  local copies, waits for them, and re-layouts  8.89 us (3%)
  other arithmetic  6.51 us (3%)
    ppermute x15, waiting for transfers between devices, exchange(): lax.ppermute(value, axis, [(source, source ^ mask) for source in range(co...  65.5 us
    ppermute x15, starting transfers between devices, exchange(): lax.ppermute(value, axis, [(source, source ^ mask) for source in range(co...  65.4 us
    ppermute x6, waiting for transfers between devices, shifted(): lax.ppermute(value, axis, [(source, source + steps) for source in range(l...  62.2 us
    ppermute x6, starting transfers between devices, shifted(): lax.ppermute(value, axis, [(source, source + steps) for source in range(l...  25.3 us
  transfers between devices with their start and end apart: 21, of which 19 were waited for; matrix products, arithmetic and copies ran while one was open for 6% of the time, Pallas kernels for 0%

profile of v6, /device:TPU:1, one launch (start us, length us, event | category | flops | bytes accessed | tf_op | source)
XLA Modules:
  0.0 255.3 jit_solution(6511204348201866120)
XLA Ops:
  1.8 4.9 %collective-permute-start = (bf16[1,512,256]{2,1,0:T(8,128)(2,1)S(1)}, bf16[1,512,256]{2,1,0:T(8,128)(2,1)S(1)}, u32[]{:S(2)}, u32[]{:S(2)}) collective-permute-start(bf16[1,512,256]{2,1,0:T(8,128)(2,1)S(1)} %get-tuple-element.25), channel_id=1, source_target_pairs={{0,1},{1,2},{2,3},{3,4},{4,5},{5,6},{6,7},{7,8},{8,9},{9,10},{10,1... | collective-permute-start | bytes 786440 | tf_op jit(solution)/shard_map/ppermute | solution.py:15
  13.5 7.9 %collective-permute-start.1 = (bf16[1,512,256]{2,1,0:T(8,128)(2,1)S(1)}, bf16[1,512,256]{2,1,0:T(8,128)(2,1)S(1)}, u32[]{:S(2)}, u32[]{:S(2)}) collective-permute-start(bf16[1,512,256]{2,1,0:T(8,128)(2,1)S(1)} %get-tuple-element.23), channel_id=1, source_target_pairs={{0,8},{1,9},{2,10},{3,11},{4,12},{5,13},{6,14},{7,15},{8,16},{9,17... | collective-permute-start | bytes 786440 | tf_op jit(solution)/shard_map/ppermute | solution.py:15
  21.8 5.2 %collective-permute-done.1 = bf16[1,512,256]{2,1,0:T(8,128)(2,1)S(1)} collective-permute-done((bf16[1,512,256]{2,1,0:T(8,128)(2,1)S(1)}, bf16[1,512,256]{2,1,0:T(8,128)(2,1)S(1)}, u32[]{:S(2)}, u32[]{:S(2)}) %collective-permute-start.1) | collective-permute-done | bytes 262176 | tf_op jit(solution)/shard_map/ppermute | solution.py:15
  31.0 8.0 %collective-permute-start.2 = (bf16[1,512,256]{2,1,0:T(8,128)(2,1)S(1)}, bf16[1,512,256]{2,1,0:T(8,128)(2,1)S(1)}, u32[]{:S(2)}, u32[]{:S(2)}) collective-permute-start(bf16[1,512,256]{2,1,0:T(8,128)(2,1)S(1)} %get-tuple-element.8), channel_id=1, source_target_pairs={{0,8},{1,9},{2,10},{3,11},{4,12},{5,13},{6,14},{7,15},{8,16},{9,17... | collective-permute-start | bytes 786440 | tf_op jit(solution)/shard_map/ppermute | solution.py:15
  40.7 8.1 %collective-permute-done.2 = bf16[1,512,256]{2,1,0:T(8,128)(2,1)S(1)} collective-permute-done((bf16[1,512,256]{2,1,0:T(8,128)(2,1)S(1)}, bf16[1,512,256]{2,1,0:T(8,128)(2,1)S(1)}, u32[]{:S(2)}, u32[]{:S(2)}) %collective-permute-start.2) | collective-permute-done | bytes 262176 | tf_op jit(solution)/shard_map/ppermute | solution.py:15
  60.6 40.5 %collective-permute-done.4 = bf16[1,512,256]{2,1,0:T(8,128)(2,1)} collective-permute-done((bf16[1,512,256]{2,1,0:T(8,128)(2,1)}, bf16[1,512,256]{2,1,0:T(8,128)(2,1)}, u32[]{:S(2)}, u32[]{:S(2)}) %collective-permute-start.4) | collective-permute-done | bytes 262176 | tf_op jit(solution)/shard_map/ppermute | solution.py:15
  108.6 5.2 %collective-permute-start.6 = (f32[640,512]{1,0:T(8,128)}, f32[640,512]{1,0:T(8,128)}, u32[]{:S(2)}, u32[]{:S(2)}) collective-permute-start(f32[640,512]{1,0:T(8,128)} %fusion.9), channel_id=1, source_target_pairs={{0,1},{1,0},{2,3},{3,2},{4,5},{5,4},{6,7},{7,6},{8,9},{9,8},{10,11... | collective-permute-start | bytes 3932168 | tf_op jit(solution)/shard_map/ppermute | solution.py:67
  120.8 15.9 %collective-permute-done.7 = f32[320,512]{1,0:T(8,128)S(1)} collective-permute-done((f32[320,512]{1,0:T(8,128)S(1)}, f32[320,512]{1,0:T(8,128)S(1)}, u32[]{:S(2)}, u32[]{:S(2)}) %collective-permute-start.7) | collective-permute-done | bytes 655392 | tf_op jit(solution)/shard_map/ppermute | solution.py:67
  139.8 7.1 %collective-permute-done.8 = f32[160,512]{1,0:T(8,128)S(1)} collective-permute-done((f32[160,512]{1,0:T(8,128)S(1)}, f32[160,512]{1,0:T(8,128)S(1)}, u32[]{:S(2)}, u32[]{:S(2)}) %collective-permute-start.8) | collective-permute-done | bytes 327712 | tf_op jit(solution)/shard_map/ppermute | solution.py:67
  148.9 4.1 %collective-permute-done.9 = f32[80,512]{1,0:T(8,128)S(1)} collective-permute-done((f32[80,512]{1,0:T(8,128)S(1)}, f32[80,512]{1,0:T(8,128)S(1)}, u32[]{:S(2)}, u32[]{:S(2)}) %collective-permute-start.9) | collective-permute-done | bytes 163872 | tf_op jit(solution)/shard_map/ppermute | solution.py:67
  153.2 4.0 %collective-permute-start.10 = (f32[40,512]{1,0:T(8,128)S(1)}, f32[40,512]{1,0:T(8,128)S(1)}, u32[]{:S(2)}, u32[]{:S(2)}) collective-permute-start(f32[40,512]{1,0:T(8,128)S(1)} %slice_select_fusion.3), channel_id=1, source_target_pairs={{0,256},{64,320},{128,384},{192,448},{256,0},{320,64},{384,128},{4... | collective-permute-start | bytes 245768 | tf_op jit(solution)/shard_map/ppermute | solution.py:67
  160.0 4.8 %collective-permute-start.11 = (f32[20,512]{1,0:T(8,128)S(1)}, f32[20,512]{1,0:T(8,128)S(1)}, u32[]{:S(2)}, u32[]{:S(2)}) collective-permute-start(f32[20,512]{1,0:T(8,128)S(1)} %slice_select_fusion.4), channel_id=1, source_target_pairs={{0,128},{64,192},{128,0},{192,64},{256,384},{320,448},{384,256},{4... | collective-permute-start | bytes 122888 | tf_op jit(solution)/shard_map/ppermute | solution.py:67
  166.4 3.7 %collective-permute-start.12 = (f32[20,512]{1,0:T(8,128)S(1)}, f32[20,512]{1,0:T(8,128)S(1)}, u32[]{:S(2)}, u32[]{:S(2)}) collective-permute-start(f32[20,512]{1,0:T(8,128)S(1)} %select_add_fusion.5), channel_id=1, source_target_pairs={{0,4},{1,5},{2,6},{3,7},{4,0},{5,1},{6,2},{7,3},{8,12},{9,13},{10,... | collective-permute-start | bytes 122888 | tf_op jit(solution)/shard_map/ppermute | solution.py:67
  172.7 5.3 %collective-permute-start.13 = (f32[20,512]{1,0:T(8,128)S(1)}, f32[20,512]{1,0:T(8,128)S(1)}, u32[]{:S(2)}, u32[]{:S(2)}) collective-permute-start(f32[20,512]{1,0:T(8,128)S(1)} %add.97), channel_id=1, source_target_pairs={{0,8},{1,9},{2,10},{3,11},{4,12},{5,13},{6,14},{7,15},{8,0},{9,1},... | collective-permute-start | bytes 122888 | tf_op jit(solution)/shard_map/ppermute | solution.py:67
  178.0 4.4 %collective-permute-done.13 = f32[20,512]{1,0:T(8,128)S(1)} collective-permute-done((f32[20,512]{1,0:T(8,128)S(1)}, f32[20,512]{1,0:T(8,128)S(1)}, u32[]{:S(2)}, u32[]{:S(2)}) %collective-permute-start.13) | collective-permute-done | bytes 40992 | tf_op jit(solution)/shard_map/ppermute | solution.py:67
  182.5 6.7 %collective-permute-start.14 = (f32[20,512]{1,0:T(8,128)S(1)}, f32[20,512]{1,0:T(8,128)S(1)}, u32[]{:S(2)}, u32[]{:S(2)}) collective-permute-start(f32[20,512]{1,0:T(8,128)S(1)} %add.98), channel_id=1, source_target_pairs={{0,16},{1,17},{2,18},{3,19},{4,20},{5,21},{6,22},{7,23},{8,24},{9,... | collective-permute-start | bytes 122888 | tf_op jit(solution)/shard_map/ppermute | solution.py:67
  189.1 6.9 %collective-permute-done.14 = f32[20,512]{1,0:T(8,128)S(1)} collective-permute-done((f32[20,512]{1,0:T(8,128)S(1)}, f32[20,512]{1,0:T(8,128)S(1)}, u32[]{:S(2)}, u32[]{:S(2)}) %collective-permute-start.14) | collective-permute-done | bytes 40992 | tf_op jit(solution)/shard_map/ppermute | solution.py:67
  196.0 4.8 %collective-permute-start.15 = (bf16[20,512]{1,0:T(8,128)(2,1)S(1)}, bf16[20,512]{1,0:T(8,128)(2,1)S(1)}, u32[]{:S(2)}, u32[]{:S(2)}) collective-permute-start(bf16[20,512]{1,0:T(8,128)(2,1)S(1)} %multiply_convert_fusion.11), channel_id=1, source_target_pairs={{0,128},{64,192},{128,0},{192,64},{256,384},{320,448},{384,256},{4... | collective-permute-start | bytes 61448 | tf_op jit(solution)/shard_map/ppermute | solution.py:67
  205.2 3.5 %collective-permute-done.16 = bf16[40,512]{1,0:T(8,128)(2,1)S(1)} collective-permute-done((bf16[40,512]{1,0:T(8,128)(2,1)S(1)}, bf16[40,512]{1,0:T(8,128)(2,1)S(1)}, u32[]{:S(2)}, u32[]{:S(2)}) %collective-permute-start.16) | collective-permute-done | bytes 40992 | tf_op jit(solution)/shard_map/ppermute | solution.py:67
  210.6 3.3 %collective-permute-done.17 = bf16[80,512]{1,0:T(8,128)(2,1)S(1)} collective-permute-done((bf16[80,512]{1,0:T(8,128)(2,1)S(1)}, bf16[80,512]{1,0:T(8,128)(2,1)S(1)}, u32[]{:S(2)}, u32[]{:S(2)}) %collective-permute-start.17) | collective-permute-done | bytes 81952 | tf_op jit(solution)/shard_map/ppermute | solution.py:67
  216.2 3.8 %collective-permute-done.18 = bf16[160,512]{1,0:T(8,128)(2,1)S(1)} collective-permute-done((bf16[160,512]{1,0:T(8,128)(2,1)S(1)}, bf16[160,512]{1,0:T(8,128)(2,1)S(1)}, u32[]{:S(2)}, u32[]{:S(2)}) %collective-permute-start.18) | collective-permute-done | bytes 163872 | tf_op jit(solution)/shard_map/ppermute | solution.py:67
  222.7 5.1 %collective-permute-done.19 = bf16[320,512]{1,0:T(8,128)(2,1)S(1)} collective-permute-done((bf16[320,512]{1,0:T(8,128)(2,1)S(1)}, bf16[320,512]{1,0:T(8,128)(2,1)S(1)}, u32[]{:S(2)}, u32[]{:S(2)}) %collective-permute-start.19) | collective-permute-done | bytes 327712 | tf_op jit(solution)/shard_map/ppermute | solution.py:67
  228.1 15.2 %collective-permute-start.20 = (bf16[640,512]{1,0:T(8,128)(2,1)S(1)}, bf16[640,512]{1,0:T(8,128)(2,1)S(1)}, u32[]{:S(2)}, u32[]{:S(2)}) collective-permute-start(bf16[640,512]{1,0:T(8,128)(2,1)S(1)} %maximum_select_fusion.1), channel_id=1, source_target_pairs={{0,1},{1,0},{2,3},{3,2},{4,5},{5,4},{6,7},{7,6},{8,9},{9,8},{10,11... | collective-permute-start | bytes 1966088 | tf_op jit(solution)/shard_map/ppermute | solution.py:67
  245.3 5.8 %collective-permute-done.5 = bf16[1,512,256]{2,1,0:T(8,128)(2,1)S(1)} collective-permute-done((bf16[1,512,256]{2,1,0:T(8,128)(2,1)S(1)}, bf16[1,512,256]{2,1,0:T(8,128)(2,1)S(1)}, u32[]{:S(2)}, u32[]{:S(2)}) %collective-permute-start.5) | collective-permute-done | bytes 262176 | tf_op jit(solution)/shard_map/ppermute | solution.py:15
  (137 shorter events, 69.9 us)
Async XLA Ops:
  1.8 9.2 %collective-permute-start = (bf16[1,512,256]{2,1,0:T(8,128)(2,1)S(1)}, bf16[1,512,256]{2,1,0:T(8,128)(2,1)S(1)}, u32[]{:S(2)}, u32[]{:S(2)}) collective-permute-start(bf16[1,512,256]{2,1,0:T(8,128)(2,1)S(1)} %get-tuple-element.25), channel_id=1, source_target_pairs={{0,1},{1,2},{2,3},{3,4},{4,5},{5,6},{6,7},{7,8},{8,9},{9,10},{10,1... | collective-permute-start | bytes 786440 | tf_op jit(solution)/shard_map/ppermute | solution.py:15
  13.5 13.4 %collective-permute-start.1 = (bf16[1,512,256]{2,1,0:T(8,128)(2,1)S(1)}, bf16[1,512,256]{2,1,0:T(8,128)(2,1)S(1)}, u32[]{:S(2)}, u32[]{:S(2)}) collective-permute-start(bf16[1,512,256]{2,1,0:T(8,128)(2,1)S(1)} %get-tuple-element.23), channel_id=1, source_target_pairs={{0,8},{1,9},{2,10},{3,11},{4,12},{5,13},{6,14},{7,15},{8,16},{9,17... | collective-permute-start | bytes 786440 | tf_op jit(solution)/shard_map/ppermute | solution.py:15
  31.0 17.8 %collective-permute-start.2 = (bf16[1,512,256]{2,1,0:T(8,128)(2,1)S(1)}, bf16[1,512,256]{2,1,0:T(8,128)(2,1)S(1)}, u32[]{:S(2)}, u32[]{:S(2)}) collective-permute-start(bf16[1,512,256]{2,1,0:T(8,128)(2,1)S(1)} %get-tuple-element.8), channel_id=1, source_target_pairs={{0,8},{1,9},{2,10},{3,11},{4,12},{5,13},{6,14},{7,15},{8,16},{9,17... | collective-permute-start | bytes 786440 | tf_op jit(solution)/shard_map/ppermute | solution.py:15
  39.1 21.5 %collective-permute-start.3 = (bf16[1,512,256]{2,1,0:T(8,128)(2,1)}, bf16[1,512,256]{2,1,0:T(8,128)(2,1)}, u32[]{:S(2)}, u32[]{:S(2)}) collective-permute-start(bf16[1,512,256]{2,1,0:T(8,128)(2,1)} %fusion.3), channel_id=1, source_target_pairs={{8,0},{9,1},{10,2},{11,3},{12,4},{13,5},{14,6},{15,7},{16,8},{17,9... | collective-permute-start | bytes 786440 | tf_op jit(solution)/shard_map/ppermute | solution.py:15
  52.9 48.2 %collective-permute-start.4 = (bf16[1,512,256]{2,1,0:T(8,128)(2,1)}, bf16[1,512,256]{2,1,0:T(8,128)(2,1)}, u32[]{:S(2)}, u32[]{:S(2)}) collective-permute-start(bf16[1,512,256]{2,1,0:T(8,128)(2,1)} %fusion.4), channel_id=1, source_target_pairs={{8,0},{9,1},{10,2},{11,3},{12,4},{13,5},{14,6},{15,7},{16,8},{17,9... | collective-permute-start | bytes 786440 | tf_op jit(solution)/shard_map/ppermute | solution.py:15
  108.6 8.2 %collective-permute-start.6 = (f32[640,512]{1,0:T(8,128)}, f32[640,512]{1,0:T(8,128)}, u32[]{:S(2)}, u32[]{:S(2)}) collective-permute-start(f32[640,512]{1,0:T(8,128)} %fusion.9), channel_id=1, source_target_pairs={{0,1},{1,0},{2,3},{3,2},{4,5},{5,4},{6,7},{7,6},{8,9},{9,8},{10,11... | collective-permute-start | bytes 3932168 | tf_op jit(solution)/shard_map/ppermute | solution.py:67
  118.9 17.8 %collective-permute-start.7 = (f32[320,512]{1,0:T(8,128)S(1)}, f32[320,512]{1,0:T(8,128)S(1)}, u32[]{:S(2)}, u32[]{:S(2)}) collective-permute-start(f32[320,512]{1,0:T(8,128)S(1)} %slice_select_fusion), channel_id=1, source_target_pairs={{0,32},{1,33},{2,34},{3,35},{4,36},{5,37},{6,38},{7,39},{8,40},{9,... | collective-permute-start | bytes 1966088 | tf_op jit(solution)/shard_map/ppermute | solution.py:67
  137.0 9.9 %collective-permute-start.8 = (f32[160,512]{1,0:T(8,128)S(1)}, f32[160,512]{1,0:T(8,128)S(1)}, u32[]{:S(2)}, u32[]{:S(2)}) collective-permute-start(f32[160,512]{1,0:T(8,128)S(1)} %slice_select_fusion.1), channel_id=1, source_target_pairs={{0,64},{64,0},{128,192},{192,128},{256,320},{320,256},{384,448},{4... | collective-permute-start | bytes 983048 | tf_op jit(solution)/shard_map/ppermute | solution.py:67
  147.0 6.1 %collective-permute-start.9 = (f32[80,512]{1,0:T(8,128)S(1)}, f32[80,512]{1,0:T(8,128)S(1)}, u32[]{:S(2)}, u32[]{:S(2)}) collective-permute-start(f32[80,512]{1,0:T(8,128)S(1)} %slice_select_fusion.2), channel_id=1, source_target_pairs={{0,2},{1,3},{2,0},{3,1},{4,6},{5,7},{6,4},{7,5},{8,10},{9,11},{10,... | collective-permute-start | bytes 491528 | tf_op jit(solution)/shard_map/ppermute | solution.py:67
  153.1 69.1 %copy-start.16 = (bf16[256,512]{1,0:T(8,128)(2,1)S(1)}, bf16[256,512]{1,0:T(8,128)(2,1)}, u32[]{:S(2)}) copy-start(bf16[256,512]{1,0:T(8,128)(2,1)} %param.10) | copy-start | bytes 786436
  153.1 69.1 %copy-start.27 = (bf16[1024,256]{0,1:T(8,128)(2,1)S(1)}, bf16[1024,256]{0,1:T(8,128)(2,1)}, u32[]{:S(2)}) copy-start(bf16[1024,256]{0,1:T(8,128)(2,1)} %get-tuple-element.9) | copy-start | bytes 1572868
  153.1 69.1 %copy-start.30 = (bf16[1024,256]{0,1:T(8,128)(2,1)S(1)}, bf16[1024,256]{0,1:T(8,128)(2,1)}, u32[]{:S(2)}) copy-start(bf16[1024,256]{0,1:T(8,128)(2,1)} %get-tuple-element.10) | copy-start | bytes 1572868
  153.2 6.8 %collective-permute-start.10 = (f32[40,512]{1,0:T(8,128)S(1)}, f32[40,512]{1,0:T(8,128)S(1)}, u32[]{:S(2)}, u32[]{:S(2)}) collective-permute-start(f32[40,512]{1,0:T(8,128)S(1)} %slice_select_fusion.3), channel_id=1, source_target_pairs={{0,256},{64,320},{128,384},{192,448},{256,0},{320,64},{384,128},{4... | collective-permute-start | bytes 245768 | tf_op jit(solution)/shard_map/ppermute | solution.py:67
  160.0 6.3 %collective-permute-start.11 = (f32[20,512]{1,0:T(8,128)S(1)}, f32[20,512]{1,0:T(8,128)S(1)}, u32[]{:S(2)}, u32[]{:S(2)}) collective-permute-start(f32[20,512]{1,0:T(8,128)S(1)} %slice_select_fusion.4), channel_id=1, source_target_pairs={{0,128},{64,192},{128,0},{192,64},{256,384},{320,448},{384,256},{4... | collective-permute-start | bytes 122888 | tf_op jit(solution)/shard_map/ppermute | solution.py:67
  166.4 6.3 %collective-permute-start.12 = (f32[20,512]{1,0:T(8,128)S(1)}, f32[20,512]{1,0:T(8,128)S(1)}, u32[]{:S(2)}, u32[]{:S(2)}) collective-permute-start(f32[20,512]{1,0:T(8,128)S(1)} %select_add_fusion.5), channel_id=1, source_target_pairs={{0,4},{1,5},{2,6},{3,7},{4,0},{5,1},{6,2},{7,3},{8,12},{9,13},{10,... | collective-permute-start | bytes 122888 | tf_op jit(solution)/shard_map/ppermute | solution.py:67
  172.7 9.8 %collective-permute-start.13 = (f32[20,512]{1,0:T(8,128)S(1)}, f32[20,512]{1,0:T(8,128)S(1)}, u32[]{:S(2)}, u32[]{:S(2)}) collective-permute-start(f32[20,512]{1,0:T(8,128)S(1)} %add.97), channel_id=1, source_target_pairs={{0,8},{1,9},{2,10},{3,11},{4,12},{5,13},{6,14},{7,15},{8,0},{9,1},... | collective-permute-start | bytes 122888 | tf_op jit(solution)/shard_map/ppermute | solution.py:67
  182.5 13.5 %collective-permute-start.14 = (f32[20,512]{1,0:T(8,128)S(1)}, f32[20,512]{1,0:T(8,128)S(1)}, u32[]{:S(2)}, u32[]{:S(2)}) collective-permute-start(f32[20,512]{1,0:T(8,128)S(1)} %add.98), channel_id=1, source_target_pairs={{0,16},{1,17},{2,18},{3,19},{4,20},{5,21},{6,22},{7,23},{8,24},{9,... | collective-permute-start | bytes 122888 | tf_op jit(solution)/shard_map/ppermute | solution.py:67
  196.0 6.4 %collective-permute-start.15 = (bf16[20,512]{1,0:T(8,128)(2,1)S(1)}, bf16[20,512]{1,0:T(8,128)(2,1)S(1)}, u32[]{:S(2)}, u32[]{:S(2)}) collective-permute-start(bf16[20,512]{1,0:T(8,128)(2,1)S(1)} %multiply_convert_fusion.11), channel_id=1, source_target_pairs={{0,128},{64,192},{128,0},{192,64},{256,384},{320,448},{384,256},{4... | collective-permute-start | bytes 61448 | tf_op jit(solution)/shard_map/ppermute | solution.py:67
  202.4 6.3 %collective-permute-start.16 = (bf16[40,512]{1,0:T(8,128)(2,1)S(1)}, bf16[40,512]{1,0:T(8,128)(2,1)S(1)}, u32[]{:S(2)}, u32[]{:S(2)}) collective-permute-start(bf16[40,512]{1,0:T(8,128)(2,1)S(1)} %maximum_select_fusion.5), channel_id=1, source_target_pairs={{0,256},{64,320},{128,384},{192,448},{256,0},{320,64},{384,128},{4... | collective-permute-start | bytes 122888 | tf_op jit(solution)/shard_map/ppermute | solution.py:67
  208.7 5.2 %collective-permute-start.17 = (bf16[80,512]{1,0:T(8,128)(2,1)S(1)}, bf16[80,512]{1,0:T(8,128)(2,1)S(1)}, u32[]{:S(2)}, u32[]{:S(2)}) collective-permute-start(bf16[80,512]{1,0:T(8,128)(2,1)S(1)} %maximum_select_fusion.4), channel_id=1, source_target_pairs={{0,2},{1,3},{2,0},{3,1},{4,6},{5,7},{6,4},{7,5},{8,10},{9,11},{10,... | collective-permute-start | bytes 245768 | tf_op jit(solution)/shard_map/ppermute | solution.py:67
  213.9 6.1 %collective-permute-start.18 = (bf16[160,512]{1,0:T(8,128)(2,1)S(1)}, bf16[160,512]{1,0:T(8,128)(2,1)S(1)}, u32[]{:S(2)}, u32[]{:S(2)}) collective-permute-start(bf16[160,512]{1,0:T(8,128)(2,1)S(1)} %maximum_select_fusion.3), channel_id=1, source_target_pairs={{0,64},{64,0},{128,192},{192,128},{256,320},{320,256},{384,448},{4... | collective-permute-start | bytes 491528 | tf_op jit(solution)/shard_map/ppermute | solution.py:67
  220.1 7.8 %collective-permute-start.19 = (bf16[320,512]{1,0:T(8,128)(2,1)S(1)}, bf16[320,512]{1,0:T(8,128)(2,1)S(1)}, u32[]{:S(2)}, u32[]{:S(2)}) collective-permute-start(bf16[320,512]{1,0:T(8,128)(2,1)S(1)} %maximum_select_fusion.2), channel_id=1, source_target_pairs={{0,32},{1,33},{2,34},{3,35},{4,36},{5,37},{6,38},{7,39},{8,40},{9,... | collective-permute-start | bytes 983048 | tf_op jit(solution)/shard_map/ppermute | solution.py:67
  228.1 24.2 %collective-permute-start.20 = (bf16[640,512]{1,0:T(8,128)(2,1)S(1)}, bf16[640,512]{1,0:T(8,128)(2,1)S(1)}, u32[]{:S(2)}, u32[]{:S(2)}) collective-permute-start(bf16[640,512]{1,0:T(8,128)(2,1)S(1)} %maximum_select_fusion.1), channel_id=1, source_target_pairs={{0,1},{1,0},{2,3},{3,2},{4,5},{5,4},{6,7},{7,6},{8,9},{9,8},{10,11... | collective-permute-start | bytes 1966088 | tf_op jit(solution)/shard_map/ppermute | solution.py:67
  243.3 7.7 %collective-permute-start.5 = (bf16[1,512,256]{2,1,0:T(8,128)(2,1)S(1)}, bf16[1,512,256]{2,1,0:T(8,128)(2,1)S(1)}, u32[]{:S(2)}, u32[]{:S(2)}) collective-permute-start(bf16[1,512,256]{2,1,0:T(8,128)(2,1)S(1)} %get-tuple-element.22), channel_id=1, source_target_pairs={{1,0},{2,1},{3,2},{4,3},{5,4},{6,5},{7,6},{8,7},{9,8},{10,9},{11,1... | collective-permute-start | bytes 786440 | tf_op jit(solution)/shard_map/ppermute | solution.py:15
  (28 other events, 229.9 us)

commit v7 on v6

--- a/solution.py
+++ b/solution.py
@@ -67,7 +67,7 @@
     return lax.ppermute(value, axis, [(source, source ^ mask) for source in range(count)])
 
 
-def reduce_grads(term_list, scale_factor):
+def reduce_grads(term_list, scale_factor, companion):
     shapes = [member.shape for member in term_list]
     flat = jnp.concatenate([member.reshape(-1, PACKED_WIDTH) for member in term_list])
     for axis, mask in HALVING_STEPS:
@@ -77,6 +77,8 @@
         kept = jnp.where(upper, second, first)
         sent = jnp.where(upper, first, second)
         flat = kept + exchange(sent, axis, mask)
+        if mask == 32:
+            flat, companion = lax.optimization_barrier((flat, companion))
     for axis, mask in BUTTERFLY_STEPS:
         flat = flat + exchange(flat, axis, mask)
     flat = (flat * scale_factor).astype(jnp.bfloat16)
@@ -89,7 +91,7 @@
         rows = shape[0] * shape[1] // PACKED_WIDTH
         out.append(flat[start:start + rows].reshape(shape))
         start += rows
-    return tuple(out)
+    return tuple(out), companion
 
 
 def body(
@@ -166,7 +168,7 @@
         [forward_rows_first[:, FIRST_DILATION:, :], received_head_rows], axis=1
     )
     grad_signal = (local_one + trailing_later_rows.astype(jnp.float32)).astype(jnp.bfloat16)
-    reduced = reduce_grads(tuple(first_layer_terms) + tuple(second_layer_terms), scale_factor)
+    reduced, grad_signal = reduce_grads(tuple(first_layer_terms) + tuple(second_layer_terms), scale_factor, grad_signal)
     reduced_one, reduced_two = reduced[:3], reduced[3:]
     return (
         grad_signal,

time: 256 us -> 249 us (0.973)
  waiting for transfers between devices: 128 us -> 80.8 us
  starting transfers between devices: 90.7 us -> 127 us
  matrix products: 20.1 us -> 22.7 us
    ppermute x15, starting transfers between devices: 65.4 us -> 101 us  [exchange(): lax.ppermute(value, axis, [(source, source ^ mask) for source in range(co...]
    ppermute x6, waiting for transfers between devices: 62.2 us -> 28.4 us  [shifted(): lax.ppermute(value, axis, [(source, source + steps) for source in range(l...]
    ppermute x15, waiting for transfers between devices: 65.5 us -> 52.5 us  [exchange(): lax.ppermute(value, axis, [(source, source ^ mask) for source in range(co...]
  transfers between devices with their start and end apart: 21 -> 21, of which waited for: 19 -> 20; matrix products, arithmetic and copies ran while one was open for 6% -> 7% of each run, Pallas kernels for 0% -> 0%
where the time goes in v7:
time: 249 us; the launch traced here: 248 us
  starting transfers between devices  127 us (51%)
  waiting for transfers between devices  80.8 us (32%)
  matrix products  22.7 us (9%)
  local copies, waits for them, and re-layouts  10.3 us (4%)
  other arithmetic  6.22 us (2%)
    ppermute x15, starting transfers between devices, exchange(): lax.ppermute(value, axis, [(source, source ^ mask) for source in range(co...  101 us
    ppermute x15, waiting for transfers between devices, exchange(): lax.ppermute(value, axis, [(source, source ^ mask) for source in range(co...  52.5 us
    ppermute x6, waiting for transfers between devices, shifted(): lax.ppermute(value, axis, [(source, source + steps) for source in range(l...  28.4 us
    ppermute x6, starting transfers between devices, shifted(): lax.ppermute(value, axis, [(source, source + steps) for source in range(l...  25.7 us
    dot_general x3, matrix products, backward_layer(): jnp.dot(pre_grad, tap_now.T, preferred_element_type=jnp.float32)  4.99 us
  transfers between devices with their start and end apart: 21, of which 20 were waited for; matrix products, arithmetic and copies ran while one was open for 7% of the time, Pallas kernels for 0%

profile of v7, /device:TPU:1, one launch (start us, length us, event | category | flops | bytes accessed | tf_op | source)
XLA Modules:
  0.0 248.0 jit_solution(16910817566430243592)
XLA Ops:
  1.8 4.9 %collective-permute-start = (bf16[1,512,256]{2,1,0:T(8,128)(2,1)S(1)}, bf16[1,512,256]{2,1,0:T(8,128)(2,1)S(1)}, u32[]{:S(2)}, u32[]{:S(2)}) collective-permute-start(bf16[1,512,256]{2,1,0:T(8,128)(2,1)S(1)} %get-tuple-element.29), channel_id=1, source_target_pairs={{0,1},{1,2},{2,3},{3,4},{4,5},{5,6},{6,7},{7,8},{8,9},{9,10},{10,1... | collective-permute-start | bytes 786440 | tf_op jit(solution)/shard_map/ppermute | solution.py:15
  13.5 7.9 %collective-permute-start.1 = (bf16[1,512,256]{2,1,0:T(8,128)(2,1)S(1)}, bf16[1,512,256]{2,1,0:T(8,128)(2,1)S(1)}, u32[]{:S(2)}, u32[]{:S(2)}) collective-permute-start(bf16[1,512,256]{2,1,0:T(8,128)(2,1)S(1)} %get-tuple-element.27), channel_id=1, source_target_pairs={{0,8},{1,9},{2,10},{3,11},{4,12},{5,13},{6,14},{7,15},{8,16},{9,17... | collective-permute-start | bytes 786440 | tf_op jit(solution)/shard_map/ppermute | solution.py:15
  21.8 5.2 %collective-permute-done.1 = bf16[1,512,256]{2,1,0:T(8,128)(2,1)S(1)} collective-permute-done((bf16[1,512,256]{2,1,0:T(8,128)(2,1)S(1)}, bf16[1,512,256]{2,1,0:T(8,128)(2,1)S(1)}, u32[]{:S(2)}, u32[]{:S(2)}) %collective-permute-start.1) | collective-permute-done | bytes 262176 | tf_op jit(solution)/shard_map/ppermute | solution.py:15
  31.6 8.0 %collective-permute-start.2 = (bf16[1,512,256]{2,1,0:T(8,128)(2,1)S(1)}, bf16[1,512,256]{2,1,0:T(8,128)(2,1)S(1)}, u32[]{:S(2)}, u32[]{:S(2)}) collective-permute-start(bf16[1,512,256]{2,1,0:T(8,128)(2,1)S(1)} %get-tuple-element.10), channel_id=1, source_target_pairs={{0,8},{1,9},{2,10},{3,11},{4,12},{5,13},{6,14},{7,15},{8,16},{9,17... | collective-permute-start | bytes 786440 | tf_op jit(solution)/shard_map/ppermute | solution.py:15
  41.3 7.5 %collective-permute-done.2 = bf16[1,512,256]{2,1,0:T(8,128)(2,1)S(1)} collective-permute-done((bf16[1,512,256]{2,1,0:T(8,128)(2,1)S(1)}, bf16[1,512,256]{2,1,0:T(8,128)(2,1)S(1)}, u32[]{:S(2)}, u32[]{:S(2)}) %collective-permute-start.2) | collective-permute-done | bytes 262176 | tf_op jit(solution)/shard_map/ppermute | solution.py:15
  60.6 7.0 %collective-permute-done.4 = bf16[1,512,256]{2,1,0:T(8,128)(2,1)} collective-permute-done((bf16[1,512,256]{2,1,0:T(8,128)(2,1)}, bf16[1,512,256]{2,1,0:T(8,128)(2,1)}, u32[]{:S(2)}, u32[]{:S(2)}) %collective-permute-start.4) | collective-permute-done | bytes 262176 | tf_op jit(solution)/shard_map/ppermute | solution.py:15
  75.2 37.7 %collective-permute-start.5 = (f32[640,512]{1,0:T(8,128)}, f32[640,512]{1,0:T(8,128)}, u32[]{:S(2)}, u32[]{:S(2)}) collective-permute-start(f32[640,512]{1,0:T(8,128)} %fusion.9), channel_id=1, source_target_pairs={{0,1},{1,0},{2,3},{3,2},{4,5},{5,4},{6,7},{7,6},{8,9},{9,8},{10,11... | collective-permute-start | bytes 3932168 | tf_op jit(solution)/shard_map/ppermute | solution.py:67
  123.0 5.9 %collective-permute-done.7 = bf16[1,512,256]{2,1,0:T(8,128)(2,1)} collective-permute-done((bf16[1,512,256]{2,1,0:T(8,128)(2,1)}, bf16[1,512,256]{2,1,0:T(8,128)(2,1)}, u32[]{:S(2)}, u32[]{:S(2)}) %collective-permute-start.7) | collective-permute-done | bytes 262176 | tf_op jit(solution)/shard_map/ppermute | solution.py:15
  131.6 4.2 %collective-permute-done.6 = f32[320,512]{1,0:T(8,128)S(1)} collective-permute-done((f32[320,512]{1,0:T(8,128)S(1)}, f32[320,512]{1,0:T(8,128)S(1)}, u32[]{:S(2)}, u32[]{:S(2)}) %collective-permute-start.6) | collective-permute-done | bytes 655392 | tf_op jit(solution)/shard_map/ppermute | solution.py:67
  139.0 6.9 %collective-permute-done.8 = f32[160,512]{1,0:T(8,128)S(1)} collective-permute-done((f32[160,512]{1,0:T(8,128)S(1)}, f32[160,512]{1,0:T(8,128)S(1)}, u32[]{:S(2)}, u32[]{:S(2)}) %collective-permute-start.8) | collective-permute-done | bytes 327712 | tf_op jit(solution)/shard_map/ppermute | solution.py:67
  148.0 4.1 %collective-permute-done.9 = f32[80,512]{1,0:T(8,128)S(1)} collective-permute-done((f32[80,512]{1,0:T(8,128)S(1)}, f32[80,512]{1,0:T(8,128)S(1)}, u32[]{:S(2)}, u32[]{:S(2)}) %collective-permute-start.9) | collective-permute-done | bytes 163872 | tf_op jit(solution)/shard_map/ppermute | solution.py:67
  152.2 3.8 %collective-permute-start.10 = (f32[40,512]{1,0:T(8,128)S(1)}, f32[40,512]{1,0:T(8,128)S(1)}, u32[]{:S(2)}, u32[]{:S(2)}) collective-permute-start(f32[40,512]{1,0:T(8,128)S(1)} %slice_select_fusion.3), channel_id=1, source_target_pairs={{0,256},{64,320},{128,384},{192,448},{256,0},{320,64},{384,128},{4... | collective-permute-start | bytes 245768 | tf_op jit(solution)/shard_map/ppermute | solution.py:67
  158.9 4.8 %collective-permute-start.11 = (f32[20,512]{1,0:T(8,128)S(1)}, f32[20,512]{1,0:T(8,128)S(1)}, u32[]{:S(2)}, u32[]{:S(2)}) collective-permute-start(f32[20,512]{1,0:T(8,128)S(1)} %slice_select_fusion.4), channel_id=1, source_target_pairs={{0,128},{64,192},{128,0},{192,64},{256,384},{320,448},{384,256},{4... | collective-permute-start | bytes 122888 | tf_op jit(solution)/shard_map/ppermute | solution.py:67
  165.3 5.1 %collective-permute-start.12 = (f32[20,512]{1,0:T(8,128)S(1)}, f32[20,512]{1,0:T(8,128)S(1)}, u32[]{:S(2)}, u32[]{:S(2)}) collective-permute-start(f32[20,512]{1,0:T(8,128)S(1)} %select_add_fusion.5), channel_id=1, source_target_pairs={{0,4},{1,5},{2,6},{3,7},{4,0},{5,1},{6,2},{7,3},{8,12},{9,13},{10,... | collective-permute-start | bytes 122888 | tf_op jit(solution)/shard_map/ppermute | solution.py:67
  172.4 5.9 %collective-permute-start.13 = (f32[20,512]{1,0:T(8,128)S(1)}, f32[20,512]{1,0:T(8,128)S(1)}, u32[]{:S(2)}, u32[]{:S(2)}) collective-permute-start(f32[20,512]{1,0:T(8,128)S(1)} %add.97), channel_id=1, source_target_pairs={{0,8},{1,9},{2,10},{3,11},{4,12},{5,13},{6,14},{7,15},{8,0},{9,1},... | collective-permute-start | bytes 122888 | tf_op jit(solution)/shard_map/ppermute | solution.py:67
  178.4 3.2 %collective-permute-done.13 = f32[20,512]{1,0:T(8,128)S(1)} collective-permute-done((f32[20,512]{1,0:T(8,128)S(1)}, f32[20,512]{1,0:T(8,128)S(1)}, u32[]{:S(2)}, u32[]{:S(2)}) %collective-permute-start.13) | collective-permute-done | bytes 40992 | tf_op jit(solution)/shard_map/ppermute | solution.py:67
  181.6 8.4 %collective-permute-start.14 = (f32[20,512]{1,0:T(8,128)S(1)}, f32[20,512]{1,0:T(8,128)S(1)}, u32[]{:S(2)}, u32[]{:S(2)}) collective-permute-start(f32[20,512]{1,0:T(8,128)S(1)} %add.98), channel_id=1, source_target_pairs={{0,16},{1,17},{2,18},{3,19},{4,20},{5,21},{6,22},{7,23},{8,24},{9,... | collective-permute-start | bytes 122888 | tf_op jit(solution)/shard_map/ppermute | solution.py:67
  190.0 5.2 %collective-permute-done.14 = f32[20,512]{1,0:T(8,128)S(1)} collective-permute-done((f32[20,512]{1,0:T(8,128)S(1)}, f32[20,512]{1,0:T(8,128)S(1)}, u32[]{:S(2)}, u32[]{:S(2)}) %collective-permute-start.14) | collective-permute-done | bytes 40992 | tf_op jit(solution)/shard_map/ppermute | solution.py:67
  198.2 3.4 %collective-permute-done.15 = bf16[20,512]{1,0:T(8,128)(2,1)S(1)} collective-permute-done((bf16[20,512]{1,0:T(8,128)(2,1)S(1)}, bf16[20,512]{1,0:T(8,128)(2,1)S(1)}, u32[]{:S(2)}, u32[]{:S(2)}) %collective-permute-start.15) | collective-permute-done | bytes 20512 | tf_op jit(solution)/shard_map/ppermute | solution.py:67
  204.7 3.2 %collective-permute-done.16 = bf16[40,512]{1,0:T(8,128)(2,1)S(1)} collective-permute-done((bf16[40,512]{1,0:T(8,128)(2,1)S(1)}, bf16[40,512]{1,0:T(8,128)(2,1)S(1)}, u32[]{:S(2)}, u32[]{:S(2)}) %collective-permute-start.16) | collective-permute-done | bytes 40992 | tf_op jit(solution)/shard_map/ppermute | solution.py:67
  209.9 3.3 %collective-permute-done.17 = bf16[80,512]{1,0:T(8,128)(2,1)S(1)} collective-permute-done((bf16[80,512]{1,0:T(8,128)(2,1)S(1)}, bf16[80,512]{1,0:T(8,128)(2,1)S(1)}, u32[]{:S(2)}, u32[]{:S(2)}) %collective-permute-start.17) | collective-permute-done | bytes 81952 | tf_op jit(solution)/shard_map/ppermute | solution.py:67
  215.3 3.9 %collective-permute-done.18 = bf16[160,512]{1,0:T(8,128)(2,1)S(1)} collective-permute-done((bf16[160,512]{1,0:T(8,128)(2,1)S(1)}, bf16[160,512]{1,0:T(8,128)(2,1)S(1)}, u32[]{:S(2)}, u32[]{:S(2)}) %collective-permute-start.18) | collective-permute-done | bytes 163872 | tf_op jit(solution)/shard_map/ppermute | solution.py:67
  221.6 5.6 %collective-permute-done.19 = bf16[320,512]{1,0:T(8,128)(2,1)S(1)} collective-permute-done((bf16[320,512]{1,0:T(8,128)(2,1)S(1)}, bf16[320,512]{1,0:T(8,128)(2,1)S(1)}, u32[]{:S(2)}, u32[]{:S(2)}) %collective-permute-start.19) | collective-permute-done | bytes 327712 | tf_op jit(solution)/shard_map/ppermute | solution.py:67
  227.4 15.9 %collective-permute-start.20 = (bf16[640,512]{1,0:T(8,128)(2,1)S(1)}, bf16[640,512]{1,0:T(8,128)(2,1)S(1)}, u32[]{:S(2)}, u32[]{:S(2)}) collective-permute-start(bf16[640,512]{1,0:T(8,128)(2,1)S(1)} %maximum_select_fusion.1), channel_id=1, source_target_pairs={{0,1},{1,0},{2,3},{3,2},{4,5},{5,4},{6,7},{7,6},{8,9},{9,8},{10,11... | collective-permute-start | bytes 1966088 | tf_op jit(solution)/shard_map/ppermute | solution.py:67
  (141 shorter events, 75.4 us)
Async XLA Ops:
  1.8 9.2 %collective-permute-start = (bf16[1,512,256]{2,1,0:T(8,128)(2,1)S(1)}, bf16[1,512,256]{2,1,0:T(8,128)(2,1)S(1)}, u32[]{:S(2)}, u32[]{:S(2)}) collective-permute-start(bf16[1,512,256]{2,1,0:T(8,128)(2,1)S(1)} %get-tuple-element.29), channel_id=1, source_target_pairs={{0,1},{1,2},{2,3},{3,4},{4,5},{5,6},{6,7},{7,8},{8,9},{9,10},{10,1... | collective-permute-start | bytes 786440 | tf_op jit(solution)/shard_map/ppermute | solution.py:15
  13.5 13.4 %collective-permute-start.1 = (bf16[1,512,256]{2,1,0:T(8,128)(2,1)S(1)}, bf16[1,512,256]{2,1,0:T(8,128)(2,1)S(1)}, u32[]{:S(2)}, u32[]{:S(2)}) collective-permute-start(bf16[1,512,256]{2,1,0:T(8,128)(2,1)S(1)} %get-tuple-element.27), channel_id=1, source_target_pairs={{0,8},{1,9},{2,10},{3,11},{4,12},{5,13},{6,14},{7,15},{8,16},{9,17... | collective-permute-start | bytes 786440 | tf_op jit(solution)/shard_map/ppermute | solution.py:15
  31.6 17.2 %collective-permute-start.2 = (bf16[1,512,256]{2,1,0:T(8,128)(2,1)S(1)}, bf16[1,512,256]{2,1,0:T(8,128)(2,1)S(1)}, u32[]{:S(2)}, u32[]{:S(2)}) collective-permute-start(bf16[1,512,256]{2,1,0:T(8,128)(2,1)S(1)} %get-tuple-element.10), channel_id=1, source_target_pairs={{0,8},{1,9},{2,10},{3,11},{4,12},{5,13},{6,14},{7,15},{8,16},{9,17... | collective-permute-start | bytes 786440 | tf_op jit(solution)/shard_map/ppermute | solution.py:15
  39.6 21.0 %collective-permute-start.3 = (bf16[1,512,256]{2,1,0:T(8,128)(2,1)}, bf16[1,512,256]{2,1,0:T(8,128)(2,1)}, u32[]{:S(2)}, u32[]{:S(2)}) collective-permute-start(bf16[1,512,256]{2,1,0:T(8,128)(2,1)} %fusion.3), channel_id=1, source_target_pairs={{8,0},{9,1},{10,2},{11,3},{12,4},{13,5},{14,6},{15,7},{16,8},{17,9... | collective-permute-start | bytes 786440 | tf_op jit(solution)/shard_map/ppermute | solution.py:15
  51.7 15.9 %collective-permute-start.4 = (bf16[1,512,256]{2,1,0:T(8,128)(2,1)}, bf16[1,512,256]{2,1,0:T(8,128)(2,1)}, u32[]{:S(2)}, u32[]{:S(2)}) collective-permute-start(bf16[1,512,256]{2,1,0:T(8,128)(2,1)} %fusion.4), channel_id=1, source_target_pairs={{8,0},{9,1},{10,2},{11,3},{12,4},{13,5},{14,6},{15,7},{16,8},{17,9... | collective-permute-start | bytes 786440 | tf_op jit(solution)/shard_map/ppermute | solution.py:15
  73.9 39.1 %copy-start.20 = (bf16[256,512]{1,0:T(8,128)(2,1)S(1)}, bf16[256,512]{1,0:T(8,128)(2,1)}, u32[]{:S(2)}) copy-start(bf16[256,512]{1,0:T(8,128)(2,1)} %param.10) | copy-start | bytes 786436
  73.9 39.1 %copy-start.30 = (bf16[1024,256]{0,1:T(8,128)(2,1)S(1)}, bf16[1024,256]{0,1:T(8,128)(2,1)}, u32[]{:S(2)}) copy-start(bf16[1024,256]{0,1:T(8,128)(2,1)} %get-tuple-element.13) | copy-start | bytes 1572868
  75.2 40.7 %copy-start.6 = (f32[128,512]{1,0:T(8,128)S(1)}, f32[128,512]{1,0:T(8,128)}, u32[]{:S(2)}) copy-start(f32[128,512]{1,0:T(8,128)} %copy-done.5) | copy-start | bytes 786436
  75.2 40.7 %collective-permute-start.5 = (f32[640,512]{1,0:T(8,128)}, f32[640,512]{1,0:T(8,128)}, u32[]{:S(2)}, u32[]{:S(2)}) collective-permute-start(f32[640,512]{1,0:T(8,128)} %fusion.9), channel_id=1, source_target_pairs={{0,1},{1,0},{2,3},{3,2},{4,5},{5,4},{6,7},{7,6},{8,9},{9,8},{10,11... | collective-permute-start | bytes 3932168 | tf_op jit(solution)/shard_map/ppermute | solution.py:67
  117.9 18.0 %collective-permute-start.6 = (f32[320,512]{1,0:T(8,128)S(1)}, f32[320,512]{1,0:T(8,128)S(1)}, u32[]{:S(2)}, u32[]{:S(2)}) collective-permute-start(f32[320,512]{1,0:T(8,128)S(1)} %slice_select_fusion), channel_id=1, source_target_pairs={{0,32},{1,33},{2,34},{3,35},{4,36},{5,37},{6,38},{7,39},{8,40},{9,... | collective-permute-start | bytes 1966088 | tf_op jit(solution)/shard_map/ppermute | solution.py:67
  120.7 8.2 %collective-permute-start.7 = (bf16[1,512,256]{2,1,0:T(8,128)(2,1)}, bf16[1,512,256]{2,1,0:T(8,128)(2,1)}, u32[]{:S(2)}, u32[]{:S(2)}) collective-permute-start(bf16[1,512,256]{2,1,0:T(8,128)(2,1)} %get-tuple-element.26), channel_id=1, source_target_pairs={{1,0},{2,1},{3,2},{4,3},{5,4},{6,5},{7,6},{8,7},{9,8},{10,9},{11,1... | collective-permute-start | bytes 786440 | tf_op jit(solution)/shard_map/ppermute | solution.py:15
  136.1 9.9 %collective-permute-start.8 = (f32[160,512]{1,0:T(8,128)S(1)}, f32[160,512]{1,0:T(8,128)S(1)}, u32[]{:S(2)}, u32[]{:S(2)}) collective-permute-start(f32[160,512]{1,0:T(8,128)S(1)} %slice_select_fusion.1), channel_id=1, source_target_pairs={{0,64},{64,0},{128,192},{192,128},{256,320},{320,256},{384,448},{4... | collective-permute-start | bytes 983048 | tf_op jit(solution)/shard_map/ppermute | solution.py:67
  146.1 6.1 %collective-permute-start.9 = (f32[80,512]{1,0:T(8,128)S(1)}, f32[80,512]{1,0:T(8,128)S(1)}, u32[]{:S(2)}, u32[]{:S(2)}) collective-permute-start(f32[80,512]{1,0:T(8,128)S(1)} %slice_select_fusion.2), channel_id=1, source_target_pairs={{0,2},{1,3},{2,0},{3,1},{4,6},{5,7},{6,4},{7,5},{8,10},{9,11},{10,... | collective-permute-start | bytes 491528 | tf_op jit(solution)/shard_map/ppermute | solution.py:67
  152.2 6.7 %collective-permute-start.10 = (f32[40,512]{1,0:T(8,128)S(1)}, f32[40,512]{1,0:T(8,128)S(1)}, u32[]{:S(2)}, u32[]{:S(2)}) collective-permute-start(f32[40,512]{1,0:T(8,128)S(1)} %slice_select_fusion.3), channel_id=1, source_target_pairs={{0,256},{64,320},{128,384},{192,448},{256,0},{320,64},{384,128},{4... | collective-permute-start | bytes 245768 | tf_op jit(solution)/shard_map/ppermute | solution.py:67
  158.9 6.3 %collective-permute-start.11 = (f32[20,512]{1,0:T(8,128)S(1)}, f32[20,512]{1,0:T(8,128)S(1)}, u32[]{:S(2)}, u32[]{:S(2)}) collective-permute-start(f32[20,512]{1,0:T(8,128)S(1)} %slice_select_fusion.4), channel_id=1, source_target_pairs={{0,128},{64,192},{128,0},{192,64},{256,384},{320,448},{384,256},{4... | collective-permute-start | bytes 122888 | tf_op jit(solution)/shard_map/ppermute | solution.py:67
  165.3 7.1 %collective-permute-start.12 = (f32[20,512]{1,0:T(8,128)S(1)}, f32[20,512]{1,0:T(8,128)S(1)}, u32[]{:S(2)}, u32[]{:S(2)}) collective-permute-start(f32[20,512]{1,0:T(8,128)S(1)} %select_add_fusion.5), channel_id=1, source_target_pairs={{0,4},{1,5},{2,6},{3,7},{4,0},{5,1},{6,2},{7,3},{8,12},{9,13},{10,... | collective-permute-start | bytes 122888 | tf_op jit(solution)/shard_map/ppermute | solution.py:67
  172.4 9.1 %collective-permute-start.13 = (f32[20,512]{1,0:T(8,128)S(1)}, f32[20,512]{1,0:T(8,128)S(1)}, u32[]{:S(2)}, u32[]{:S(2)}) collective-permute-start(f32[20,512]{1,0:T(8,128)S(1)} %add.97), channel_id=1, source_target_pairs={{0,8},{1,9},{2,10},{3,11},{4,12},{5,13},{6,14},{7,15},{8,0},{9,1},... | collective-permute-start | bytes 122888 | tf_op jit(solution)/shard_map/ppermute | solution.py:67
  181.6 13.7 %collective-permute-start.14 = (f32[20,512]{1,0:T(8,128)S(1)}, f32[20,512]{1,0:T(8,128)S(1)}, u32[]{:S(2)}, u32[]{:S(2)}) collective-permute-start(f32[20,512]{1,0:T(8,128)S(1)} %add.98), channel_id=1, source_target_pairs={{0,16},{1,17},{2,18},{3,19},{4,20},{5,21},{6,22},{7,23},{8,24},{9,... | collective-permute-start | bytes 122888 | tf_op jit(solution)/shard_map/ppermute | solution.py:67
  195.3 6.4 %collective-permute-start.15 = (bf16[20,512]{1,0:T(8,128)(2,1)S(1)}, bf16[20,512]{1,0:T(8,128)(2,1)S(1)}, u32[]{:S(2)}, u32[]{:S(2)}) collective-permute-start(bf16[20,512]{1,0:T(8,128)(2,1)S(1)} %multiply_convert_fusion.11), channel_id=1, source_target_pairs={{0,128},{64,192},{128,0},{192,64},{256,384},{320,448},{384,256},{4... | collective-permute-start | bytes 61448 | tf_op jit(solution)/shard_map/ppermute | solution.py:67
  201.7 6.3 %collective-permute-start.16 = (bf16[40,512]{1,0:T(8,128)(2,1)S(1)}, bf16[40,512]{1,0:T(8,128)(2,1)S(1)}, u32[]{:S(2)}, u32[]{:S(2)}) collective-permute-start(bf16[40,512]{1,0:T(8,128)(2,1)S(1)} %maximum_select_fusion.5), channel_id=1, source_target_pairs={{0,256},{64,320},{128,384},{192,448},{256,0},{320,64},{384,128},{4... | collective-permute-start | bytes 122888 | tf_op jit(solution)/shard_map/ppermute | solution.py:67
  207.9 5.2 %collective-permute-start.17 = (bf16[80,512]{1,0:T(8,128)(2,1)S(1)}, bf16[80,512]{1,0:T(8,128)(2,1)S(1)}, u32[]{:S(2)}, u32[]{:S(2)}) collective-permute-start(bf16[80,512]{1,0:T(8,128)(2,1)S(1)} %maximum_select_fusion.4), channel_id=1, source_target_pairs={{0,2},{1,3},{2,0},{3,1},{4,6},{5,7},{6,4},{7,5},{8,10},{9,11},{10,... | collective-permute-start | bytes 245768 | tf_op jit(solution)/shard_map/ppermute | solution.py:67
  213.1 6.1 %collective-permute-start.18 = (bf16[160,512]{1,0:T(8,128)(2,1)S(1)}, bf16[160,512]{1,0:T(8,128)(2,1)S(1)}, u32[]{:S(2)}, u32[]{:S(2)}) collective-permute-start(bf16[160,512]{1,0:T(8,128)(2,1)S(1)} %maximum_select_fusion.3), channel_id=1, source_target_pairs={{0,64},{64,0},{128,192},{192,128},{256,320},{320,256},{384,448},{4... | collective-permute-start | bytes 491528 | tf_op jit(solution)/shard_map/ppermute | solution.py:67
  219.3 7.8 %collective-permute-start.19 = (bf16[320,512]{1,0:T(8,128)(2,1)S(1)}, bf16[320,512]{1,0:T(8,128)(2,1)S(1)}, u32[]{:S(2)}, u32[]{:S(2)}) collective-permute-start(bf16[320,512]{1,0:T(8,128)(2,1)S(1)} %maximum_select_fusion.2), channel_id=1, source_target_pairs={{0,32},{1,33},{2,34},{3,35},{4,36},{5,37},{6,38},{7,39},{8,40},{9,... | collective-permute-start | bytes 983048 | tf_op jit(solution)/shard_map/ppermute | solution.py:67
  227.4 17.6 %collective-permute-start.20 = (bf16[640,512]{1,0:T(8,128)(2,1)S(1)}, bf16[640,512]{1,0:T(8,128)(2,1)S(1)}, u32[]{:S(2)}, u32[]{:S(2)}) collective-permute-start(bf16[640,512]{1,0:T(8,128)(2,1)S(1)} %maximum_select_fusion.1), channel_id=1, source_target_pairs={{0,1},{1,0},{2,3},{3,2},{4,5},{5,4},{6,7},{7,6},{8,9},{9,8},{10,11... | collective-permute-start | bytes 1966088 | tf_op jit(solution)/shard_map/ppermute | solution.py:67
  (30 other events, 120.7 us)

commit v8 on v7

--- a/solution.py
+++ b/solution.py
@@ -58,7 +58,6 @@
 
 
 HALVING_STEPS = (("tm", 1), ("tm", 32), ("dp", 1), ("tm", 2), ("dp", 4), ("dp", 2))
-PACKED_WIDTH = 512
 BUTTERFLY_STEPS = (("tm", 4), ("tm", 8), ("tm", 16))
 
 
@@ -68,8 +67,9 @@
 
 
 def reduce_grads(term_list, scale_factor, companion):
-    shapes = [member.shape for member in term_list]
-    flat = jnp.concatenate([member.reshape(-1, PACKED_WIDTH) for member in term_list])
+    past_one, now_one, mix_one, past_two, now_two, mix_two = term_list
+    blocks = (past_one, now_one, past_two, now_two, jnp.concatenate([mix_one, mix_two], axis=1))
+    flat = jnp.concatenate(blocks)
     for axis, mask in HALVING_STEPS:
         half = flat.shape[0] // 2
         upper = (lax.axis_index(axis) & mask) != 0
@@ -86,12 +86,11 @@
         upper = (lax.axis_index(axis) & mask) != 0
         other = exchange(flat, axis, mask)
         flat = jnp.where(upper, jnp.concatenate([other, flat]), jnp.concatenate([flat, other]))
-    out, start = [], 0
-    for shape in shapes:
-        rows = shape[0] * shape[1] // PACKED_WIDTH
-        out.append(flat[start:start + rows].reshape(shape))
-        start += rows
-    return tuple(out), companion
+    rows = past_one.shape[0]
+    parts = [flat[index * rows:(index + 1) * rows] for index in range(len(blocks))]
+    mix_width = mix_one.shape[1]
+    out = (parts[0], parts[1], parts[4][:, :mix_width], parts[2], parts[3], parts[4][:, mix_width:])
+    return out, companion
 
 
 def body(

time: 249 us -> 242 us (0.972)
  matrix products: 22.7 us -> 14.4 us
  local copies, waits for them, and re-layouts: 10.3 us -> 5.84 us
  waiting for transfers between devices: 80.8 us -> 84.1 us
  starting transfers between devices: 127 us -> 130 us
    ppermute x6, waiting for transfers between devices: 28.4 us -> 39.7 us  [shifted(): lax.ppermute(value, axis, [(source, source + steps) for source in range(l...]
    ppermute x15, waiting for transfers between devices: 52.5 us -> 44.4 us  [exchange(): lax.ppermute(value, axis, [(source, source ^ mask) for source in range(co...]
    ppermute x15, starting transfers between devices: 101 us -> 104 us  [exchange(): lax.ppermute(value, axis, [(source, source ^ mask) for source in range(co...]
    reshape x4 -> x0, local copies, waits for them, and re-layouts: 3.2 us -> none  [the longest x2 1.79 us: reduce_grads(): member.reshape(-1, PACKED_WIDTH)]
    dot_general x3, matrix products: 4.15 us -> 1.18 us  [backward_layer(): jnp.einsum('rc,rg->cg', flat_past, pre_grad, preferred_element_type=jnp.f...]
  transfers between devices with their start and end apart: 21 -> 21, of which waited for: 20 -> 20; matrix products, arithmetic and copies ran while one was open for 7% -> 4% of each run, Pallas kernels for 0% -> 0%
where the time goes in v8:
time: 242 us; the launch traced here: 241 us
  starting transfers between devices  130 us (54%)
  waiting for transfers between devices  84.1 us (35%)
  matrix products  14.4 us (6%)
  local copies, waits for them, and re-layouts  5.84 us (2%)
  other arithmetic  5.15 us (2%)
    ppermute x15, starting transfers between devices, exchange(): lax.ppermute(value, axis, [(source, source ^ mask) for source in range(co...  104 us
    ppermute x15, waiting for transfers between devices, exchange(): lax.ppermute(value, axis, [(source, source ^ mask) for source in range(co...  44.4 us
    ppermute x6, waiting for transfers between devices, shifted(): lax.ppermute(value, axis, [(source, source + steps) for source in range(l...  39.7 us
    ppermute x6, starting transfers between devices, shifted(): lax.ppermute(value, axis, [(source, source + steps) for source in range(l...  25.7 us
  transfers between devices with their start and end apart: 21, of which 20 were waited for; matrix products, arithmetic and copies ran while one was open for 4% of the time, Pallas kernels for 0%

profile of v8, /device:TPU:1, one launch (start us, length us, event | category | flops | bytes accessed | tf_op | source)
XLA Modules:
  0.0 240.9 jit_solution(2436107139047104512)
XLA Ops:
  1.8 4.9 %collective-permute-start = (bf16[1,512,256]{2,1,0:T(8,128)(2,1)S(1)}, bf16[1,512,256]{2,1,0:T(8,128)(2,1)S(1)}, u32[]{:S(2)}, u32[]{:S(2)}) collective-permute-start(bf16[1,512,256]{2,1,0:T(8,128)(2,1)S(1)} %get-tuple-element.29), channel_id=1, source_target_pairs={{0,1},{1,2},{2,3},{3,4},{4,5},{5,6},{6,7},{7,8},{8,9},{9,10},{10,1... | collective-permute-start | bytes 786440 | tf_op jit(solution)/shard_map/ppermute | solution.py:15
  13.0 7.9 %collective-permute-start.1 = (bf16[1,512,256]{2,1,0:T(8,128)(2,1)S(1)}, bf16[1,512,256]{2,1,0:T(8,128)(2,1)S(1)}, u32[]{:S(2)}, u32[]{:S(2)}) collective-permute-start(bf16[1,512,256]{2,1,0:T(8,128)(2,1)S(1)} %get-tuple-element.27), channel_id=1, source_target_pairs={{0,8},{1,9},{2,10},{3,11},{4,12},{5,13},{6,14},{7,15},{8,16},{9,17... | collective-permute-start | bytes 786440 | tf_op jit(solution)/shard_map/ppermute | solution.py:15
  21.3 5.2 %collective-permute-done.1 = bf16[1,512,256]{2,1,0:T(8,128)(2,1)S(1)} collective-permute-done((bf16[1,512,256]{2,1,0:T(8,128)(2,1)S(1)}, bf16[1,512,256]{2,1,0:T(8,128)(2,1)S(1)}, u32[]{:S(2)}, u32[]{:S(2)}) %collective-permute-start.1) | collective-permute-done | bytes 262176 | tf_op jit(solution)/shard_map/ppermute | solution.py:15
  29.2 8.0 %collective-permute-start.2 = (bf16[1,512,256]{2,1,0:T(8,128)(2,1)S(1)}, bf16[1,512,256]{2,1,0:T(8,128)(2,1)S(1)}, u32[]{:S(2)}, u32[]{:S(2)}) collective-permute-start(bf16[1,512,256]{2,1,0:T(8,128)(2,1)S(1)} %get-tuple-element.10), channel_id=1, source_target_pairs={{0,8},{1,9},{2,10},{3,11},{4,12},{5,13},{6,14},{7,15},{8,16},{9,17... | collective-permute-start | bytes 786440 | tf_op jit(solution)/shard_map/ppermute | solution.py:15
  38.9 9.4 %collective-permute-done.2 = bf16[1,512,256]{2,1,0:T(8,128)(2,1)S(1)} collective-permute-done((bf16[1,512,256]{2,1,0:T(8,128)(2,1)S(1)}, bf16[1,512,256]{2,1,0:T(8,128)(2,1)S(1)}, u32[]{:S(2)}, u32[]{:S(2)}) %collective-permute-start.2) | collective-permute-done | bytes 262176 | tf_op jit(solution)/shard_map/ppermute | solution.py:15
  52.5 16.5 %collective-permute-done.4 = bf16[1,512,256]{2,1,0:T(8,128)(2,1)S(1)} collective-permute-done((bf16[1,512,256]{2,1,0:T(8,128)(2,1)S(1)}, bf16[1,512,256]{2,1,0:T(8,128)(2,1)S(1)}, u32[]{:S(2)}, u32[]{:S(2)}) %collective-permute-start.4) | collective-permute-done | bytes 262176 | tf_op jit(solution)/shard_map/ppermute | solution.py:15
  73.4 33.7 %collective-permute-start.5 = (f32[640,512]{1,0:T(8,128)}, f32[640,512]{1,0:T(8,128)}, u32[]{:S(2)}, u32[]{:S(2)}) collective-permute-start(f32[640,512]{1,0:T(8,128)} %fusion.10), channel_id=1, source_target_pairs={{0,1},{1,0},{2,3},{3,2},{4,5},{5,4},{6,7},{7,6},{8,9},{9,8},{10,11... | collective-permute-start | bytes 3932168 | tf_op jit(solution)/shard_map/ppermute | solution.py:66
  117.0 5.9 %collective-permute-done.7 = bf16[1,512,256]{2,1,0:T(8,128)(2,1)} collective-permute-done((bf16[1,512,256]{2,1,0:T(8,128)(2,1)}, bf16[1,512,256]{2,1,0:T(8,128)(2,1)}, u32[]{:S(2)}, u32[]{:S(2)}) %collective-permute-start.7) | collective-permute-done | bytes 262176 | tf_op jit(solution)/shard_map/ppermute | solution.py:15
  125.6 4.2 %collective-permute-done.6 = f32[320,512]{1,0:T(8,128)S(1)} collective-permute-done((f32[320,512]{1,0:T(8,128)S(1)}, f32[320,512]{1,0:T(8,128)S(1)}, u32[]{:S(2)}, u32[]{:S(2)}) %collective-permute-start.6) | collective-permute-done | bytes 655392 | tf_op jit(solution)/shard_map/ppermute | solution.py:66
  130.0 3.2 %collective-permute-start.8 = (f32[160,512]{1,0:T(8,128)S(1)}, f32[160,512]{1,0:T(8,128)S(1)}, u32[]{:S(2)}, u32[]{:S(2)}) collective-permute-start(f32[160,512]{1,0:T(8,128)S(1)} %slice_select_fusion.1), channel_id=1, source_target_pairs={{0,64},{64,0},{128,192},{192,128},{256,320},{320,256},{384,448},{4... | collective-permute-start | bytes 983048 | tf_op jit(solution)/shard_map/ppermute | solution.py:66
  133.2 6.7 %collective-permute-done.8 = f32[160,512]{1,0:T(8,128)S(1)} collective-permute-done((f32[160,512]{1,0:T(8,128)S(1)}, f32[160,512]{1,0:T(8,128)S(1)}, u32[]{:S(2)}, u32[]{:S(2)}) %collective-permute-start.8) | collective-permute-done | bytes 327712 | tf_op jit(solution)/shard_map/ppermute | solution.py:66
  142.0 4.1 %collective-permute-done.9 = f32[80,512]{1,0:T(8,128)S(1)} collective-permute-done((f32[80,512]{1,0:T(8,128)S(1)}, f32[80,512]{1,0:T(8,128)S(1)}, u32[]{:S(2)}, u32[]{:S(2)}) %collective-permute-start.9) | collective-permute-done | bytes 163872 | tf_op jit(solution)/shard_map/ppermute | solution.py:66
  146.2 4.8 %collective-permute-start.10 = (f32[40,512]{1,0:T(8,128)S(1)}, f32[40,512]{1,0:T(8,128)S(1)}, u32[]{:S(2)}, u32[]{:S(2)}) collective-permute-start(f32[40,512]{1,0:T(8,128)S(1)} %slice_select_fusion.3), channel_id=1, source_target_pairs={{0,256},{64,320},{128,384},{192,448},{256,0},{320,64},{384,128},{4... | collective-permute-start | bytes 245768 | tf_op jit(solution)/shard_map/ppermute | solution.py:66
  152.9 4.9 %collective-permute-start.11 = (f32[20,512]{1,0:T(8,128)S(1)}, f32[20,512]{1,0:T(8,128)S(1)}, u32[]{:S(2)}, u32[]{:S(2)}) collective-permute-start(f32[20,512]{1,0:T(8,128)S(1)} %slice_select_fusion.4), channel_id=1, source_target_pairs={{0,128},{64,192},{128,0},{192,64},{256,384},{320,448},{384,256},{4... | collective-permute-start | bytes 122888 | tf_op jit(solution)/shard_map/ppermute | solution.py:66
  159.2 5.3 %collective-permute-start.12 = (f32[20,512]{1,0:T(8,128)S(1)}, f32[20,512]{1,0:T(8,128)S(1)}, u32[]{:S(2)}, u32[]{:S(2)}) collective-permute-start(f32[20,512]{1,0:T(8,128)S(1)} %select_add_fusion.5), channel_id=1, source_target_pairs={{0,4},{1,5},{2,6},{3,7},{4,0},{5,1},{6,2},{7,3},{8,12},{9,13},{10,... | collective-permute-start | bytes 122888 | tf_op jit(solution)/shard_map/ppermute | solution.py:66
  166.5 6.7 %collective-permute-start.13 = (f32[20,512]{1,0:T(8,128)S(1)}, f32[20,512]{1,0:T(8,128)S(1)}, u32[]{:S(2)}, u32[]{:S(2)}) collective-permute-start(f32[20,512]{1,0:T(8,128)S(1)} %add.97), channel_id=1, source_target_pairs={{0,8},{1,9},{2,10},{3,11},{4,12},{5,13},{6,14},{7,15},{8,0},{9,1},... | collective-permute-start | bytes 122888 | tf_op jit(solution)/shard_map/ppermute | solution.py:66
  175.3 8.6 %collective-permute-start.14 = (f32[20,512]{1,0:T(8,128)S(1)}, f32[20,512]{1,0:T(8,128)S(1)}, u32[]{:S(2)}, u32[]{:S(2)}) collective-permute-start(f32[20,512]{1,0:T(8,128)S(1)} %add.98), channel_id=1, source_target_pairs={{0,16},{1,17},{2,18},{3,19},{4,20},{5,21},{6,22},{7,23},{8,24},{9,... | collective-permute-start | bytes 122888 | tf_op jit(solution)/shard_map/ppermute | solution.py:66
  183.9 5.2 %collective-permute-done.14 = f32[20,512]{1,0:T(8,128)S(1)} collective-permute-done((f32[20,512]{1,0:T(8,128)S(1)}, f32[20,512]{1,0:T(8,128)S(1)}, u32[]{:S(2)}, u32[]{:S(2)}) %collective-permute-start.14) | collective-permute-done | bytes 40992 | tf_op jit(solution)/shard_map/ppermute | solution.py:66
  189.0 4.8 %collective-permute-start.15 = (bf16[20,512]{1,0:T(8,128)(2,1)S(1)}, bf16[20,512]{1,0:T(8,128)(2,1)S(1)}, u32[]{:S(2)}, u32[]{:S(2)}) collective-permute-start(bf16[20,512]{1,0:T(8,128)(2,1)S(1)} %multiply_convert_fusion.11), channel_id=1, source_target_pairs={{0,128},{64,192},{128,0},{192,64},{256,384},{320,448},{384,256},{4... | collective-permute-start | bytes 61448 | tf_op jit(solution)/shard_map/ppermute | solution.py:66
  195.4 4.9 %collective-permute-start.16 = (bf16[40,512]{1,0:T(8,128)(2,1)S(1)}, bf16[40,512]{1,0:T(8,128)(2,1)S(1)}, u32[]{:S(2)}, u32[]{:S(2)}) collective-permute-start(bf16[40,512]{1,0:T(8,128)(2,1)S(1)} %maximum_select_fusion.5), channel_id=1, source_target_pairs={{0,256},{64,320},{128,384},{192,448},{256,0},{320,64},{384,128},{4... | collective-permute-start | bytes 122888 | tf_op jit(solution)/shard_map/ppermute | solution.py:66
  203.6 3.3 %collective-permute-done.17 = bf16[80,512]{1,0:T(8,128)(2,1)S(1)} collective-permute-done((bf16[80,512]{1,0:T(8,128)(2,1)S(1)}, bf16[80,512]{1,0:T(8,128)(2,1)S(1)}, u32[]{:S(2)}, u32[]{:S(2)}) %collective-permute-start.17) | collective-permute-done | bytes 81952 | tf_op jit(solution)/shard_map/ppermute | solution.py:66
  206.9 3.1 %collective-permute-start.18 = (bf16[160,512]{1,0:T(8,128)(2,1)S(1)}, bf16[160,512]{1,0:T(8,128)(2,1)S(1)}, u32[]{:S(2)}, u32[]{:S(2)}) collective-permute-start(bf16[160,512]{1,0:T(8,128)(2,1)S(1)} %maximum_select_fusion.3), channel_id=1, source_target_pairs={{0,64},{64,0},{128,192},{192,128},{256,320},{320,256},{384,448},{4... | collective-permute-start | bytes 491528 | tf_op jit(solution)/shard_map/ppermute | solution.py:66
  216.0 4.9 %collective-permute-done.19 = bf16[320,512]{1,0:T(8,128)(2,1)S(1)} collective-permute-done((bf16[320,512]{1,0:T(8,128)(2,1)S(1)}, bf16[320,512]{1,0:T(8,128)(2,1)S(1)}, u32[]{:S(2)}, u32[]{:S(2)}) %collective-permute-start.19) | collective-permute-done | bytes 327712 | tf_op jit(solution)/shard_map/ppermute | solution.py:66
  221.2 15.8 %collective-permute-start.20 = (bf16[640,512]{1,0:T(8,128)(2,1)S(1)}, bf16[640,512]{1,0:T(8,128)(2,1)S(1)}, u32[]{:S(2)}, u32[]{:S(2)}) collective-permute-start(bf16[640,512]{1,0:T(8,128)(2,1)S(1)} %maximum_select_fusion.1), channel_id=1, source_target_pairs={{0,1},{1,0},{2,3},{3,2},{4,5},{5,4},{6,7},{7,6},{8,9},{9,8},{10,11... | collective-permute-start | bytes 1966088 | tf_op jit(solution)/shard_map/ppermute | solution.py:66
  (111 shorter events, 57.7 us)
Async XLA Ops:
  0.6 25.8 %copy-start = (bf16[256,512]{1,0:T(8,128)(2,1)S(1)}, bf16[256,512]{1,0:T(8,128)(2,1)}, u32[]{:S(2)}) copy-start(bf16[256,512]{1,0:T(8,128)(2,1)} %param.13) | copy-start | bytes 786436
  1.8 9.2 %collective-permute-start = (bf16[1,512,256]{2,1,0:T(8,128)(2,1)S(1)}, bf16[1,512,256]{2,1,0:T(8,128)(2,1)S(1)}, u32[]{:S(2)}, u32[]{:S(2)}) collective-permute-start(bf16[1,512,256]{2,1,0:T(8,128)(2,1)S(1)} %get-tuple-element.29), channel_id=1, source_target_pairs={{0,1},{1,2},{2,3},{3,4},{4,5},{5,6},{6,7},{7,8},{8,9},{9,10},{10,1... | collective-permute-start | bytes 786440 | tf_op jit(solution)/shard_map/ppermute | solution.py:15
  13.0 13.5 %collective-permute-start.1 = (bf16[1,512,256]{2,1,0:T(8,128)(2,1)S(1)}, bf16[1,512,256]{2,1,0:T(8,128)(2,1)S(1)}, u32[]{:S(2)}, u32[]{:S(2)}) collective-permute-start(bf16[1,512,256]{2,1,0:T(8,128)(2,1)S(1)} %get-tuple-element.27), channel_id=1, source_target_pairs={{0,8},{1,9},{2,10},{3,11},{4,12},{5,13},{6,14},{7,15},{8,16},{9,17... | collective-permute-start | bytes 786440 | tf_op jit(solution)/shard_map/ppermute | solution.py:15
  29.2 19.1 %collective-permute-start.2 = (bf16[1,512,256]{2,1,0:T(8,128)(2,1)S(1)}, bf16[1,512,256]{2,1,0:T(8,128)(2,1)S(1)}, u32[]{:S(2)}, u32[]{:S(2)}) collective-permute-start(bf16[1,512,256]{2,1,0:T(8,128)(2,1)S(1)} %get-tuple-element.10), channel_id=1, source_target_pairs={{0,8},{1,9},{2,10},{3,11},{4,12},{5,13},{6,14},{7,15},{8,16},{9,17... | collective-permute-start | bytes 786440 | tf_op jit(solution)/shard_map/ppermute | solution.py:15
  37.2 15.2 %collective-permute-start.3 = (bf16[1,512,256]{2,1,0:T(8,128)(2,1)S(1)}, bf16[1,512,256]{2,1,0:T(8,128)(2,1)S(1)}, u32[]{:S(2)}, u32[]{:S(2)}) collective-permute-start(bf16[1,512,256]{2,1,0:T(8,128)(2,1)S(1)} %fusion.4), channel_id=1, source_target_pairs={{8,0},{9,1},{10,2},{11,3},{12,4},{13,5},{14,6},{15,7},{16,8},{17,9... | collective-permute-start | bytes 786440 | tf_op jit(solution)/shard_map/ppermute | solution.py:15
  49.8 19.2 %collective-permute-start.4 = (bf16[1,512,256]{2,1,0:T(8,128)(2,1)S(1)}, bf16[1,512,256]{2,1,0:T(8,128)(2,1)S(1)}, u32[]{:S(2)}, u32[]{:S(2)}) collective-permute-start(bf16[1,512,256]{2,1,0:T(8,128)(2,1)S(1)} %fusion.5), channel_id=1, source_target_pairs={{8,0},{9,1},{10,2},{11,3},{12,4},{13,5},{14,6},{15,7},{16,8},{17,9... | collective-permute-start | bytes 786440 | tf_op jit(solution)/shard_map/ppermute | solution.py:15
  51.4 20.3 %copy-start.9 = (f32[256,256]{1,0:T(8,128)}, f32[256,256]{1,0:T(8,128)S(1)}, u32[]{:S(2)}) copy-start(f32[256,256]{1,0:T(8,128)S(1)} %convolution_add_fusion.9) | copy-start | bytes 786436
  72.0 35.1 %copy-start.12 = (bf16[256,512]{1,0:T(8,128)(2,1)S(1)}, bf16[256,512]{1,0:T(8,128)(2,1)}, u32[]{:S(2)}) copy-start(bf16[256,512]{1,0:T(8,128)(2,1)} %param.10) | copy-start | bytes 786436
  73.4 36.7 %collective-permute-start.5 = (f32[640,512]{1,0:T(8,128)}, f32[640,512]{1,0:T(8,128)}, u32[]{:S(2)}, u32[]{:S(2)}) collective-permute-start(f32[640,512]{1,0:T(8,128)} %fusion.10), channel_id=1, source_target_pairs={{0,1},{1,0},{2,3},{3,2},{4,5},{5,4},{6,7},{7,6},{8,9},{9,8},{10,11... | collective-permute-start | bytes 3932168 | tf_op jit(solution)/shard_map/ppermute | solution.py:66
  112.0 17.8 %collective-permute-start.6 = (f32[320,512]{1,0:T(8,128)S(1)}, f32[320,512]{1,0:T(8,128)S(1)}, u32[]{:S(2)}, u32[]{:S(2)}) collective-permute-start(f32[320,512]{1,0:T(8,128)S(1)} %slice_select_fusion), channel_id=1, source_target_pairs={{0,32},{1,33},{2,34},{3,35},{4,36},{5,37},{6,38},{7,39},{8,40},{9,... | collective-permute-start | bytes 1966088 | tf_op jit(solution)/shard_map/ppermute | solution.py:66
  114.7 8.2 %collective-permute-start.7 = (bf16[1,512,256]{2,1,0:T(8,128)(2,1)}, bf16[1,512,256]{2,1,0:T(8,128)(2,1)}, u32[]{:S(2)}, u32[]{:S(2)}) collective-permute-start(bf16[1,512,256]{2,1,0:T(8,128)(2,1)} %get-tuple-element.26), channel_id=1, source_target_pairs={{1,0},{2,1},{3,2},{4,3},{5,4},{6,5},{7,6},{8,7},{9,8},{10,9},{11,1... | collective-permute-start | bytes 786440 | tf_op jit(solution)/shard_map/ppermute | solution.py:15
  130.0 9.9 %collective-permute-start.8 = (f32[160,512]{1,0:T(8,128)S(1)}, f32[160,512]{1,0:T(8,128)S(1)}, u32[]{:S(2)}, u32[]{:S(2)}) collective-permute-start(f32[160,512]{1,0:T(8,128)S(1)} %slice_select_fusion.1), channel_id=1, source_target_pairs={{0,64},{64,0},{128,192},{192,128},{256,320},{320,256},{384,448},{4... | collective-permute-start | bytes 983048 | tf_op jit(solution)/shard_map/ppermute | solution.py:66
  140.0 6.1 %collective-permute-start.9 = (f32[80,512]{1,0:T(8,128)S(1)}, f32[80,512]{1,0:T(8,128)S(1)}, u32[]{:S(2)}, u32[]{:S(2)}) collective-permute-start(f32[80,512]{1,0:T(8,128)S(1)} %slice_select_fusion.2), channel_id=1, source_target_pairs={{0,2},{1,3},{2,0},{3,1},{4,6},{5,7},{6,4},{7,5},{8,10},{9,11},{10,... | collective-permute-start | bytes 491528 | tf_op jit(solution)/shard_map/ppermute | solution.py:66
  146.2 6.7 %collective-permute-start.10 = (f32[40,512]{1,0:T(8,128)S(1)}, f32[40,512]{1,0:T(8,128)S(1)}, u32[]{:S(2)}, u32[]{:S(2)}) collective-permute-start(f32[40,512]{1,0:T(8,128)S(1)} %slice_select_fusion.3), channel_id=1, source_target_pairs={{0,256},{64,320},{128,384},{192,448},{256,0},{320,64},{384,128},{4... | collective-permute-start | bytes 245768 | tf_op jit(solution)/shard_map/ppermute | solution.py:66
  152.9 6.3 %collective-permute-start.11 = (f32[20,512]{1,0:T(8,128)S(1)}, f32[20,512]{1,0:T(8,128)S(1)}, u32[]{:S(2)}, u32[]{:S(2)}) collective-permute-start(f32[20,512]{1,0:T(8,128)S(1)} %slice_select_fusion.4), channel_id=1, source_target_pairs={{0,128},{64,192},{128,0},{192,64},{256,384},{320,448},{384,256},{4... | collective-permute-start | bytes 122888 | tf_op jit(solution)/shard_map/ppermute | solution.py:66
  159.2 7.2 %collective-permute-start.12 = (f32[20,512]{1,0:T(8,128)S(1)}, f32[20,512]{1,0:T(8,128)S(1)}, u32[]{:S(2)}, u32[]{:S(2)}) collective-permute-start(f32[20,512]{1,0:T(8,128)S(1)} %select_add_fusion.5), channel_id=1, source_target_pairs={{0,4},{1,5},{2,6},{3,7},{4,0},{5,1},{6,2},{7,3},{8,12},{9,13},{10,... | collective-permute-start | bytes 122888 | tf_op jit(solution)/shard_map/ppermute | solution.py:66
  166.5 8.8 %collective-permute-start.13 = (f32[20,512]{1,0:T(8,128)S(1)}, f32[20,512]{1,0:T(8,128)S(1)}, u32[]{:S(2)}, u32[]{:S(2)}) collective-permute-start(f32[20,512]{1,0:T(8,128)S(1)} %add.97), channel_id=1, source_target_pairs={{0,8},{1,9},{2,10},{3,11},{4,12},{5,13},{6,14},{7,15},{8,0},{9,1},... | collective-permute-start | bytes 122888 | tf_op jit(solution)/shard_map/ppermute | solution.py:66
  175.3 13.7 %collective-permute-start.14 = (f32[20,512]{1,0:T(8,128)S(1)}, f32[20,512]{1,0:T(8,128)S(1)}, u32[]{:S(2)}, u32[]{:S(2)}) collective-permute-start(f32[20,512]{1,0:T(8,128)S(1)} %add.98), channel_id=1, source_target_pairs={{0,16},{1,17},{2,18},{3,19},{4,20},{5,21},{6,22},{7,23},{8,24},{9,... | collective-permute-start | bytes 122888 | tf_op jit(solution)/shard_map/ppermute | solution.py:66
  189.0 6.4 %collective-permute-start.15 = (bf16[20,512]{1,0:T(8,128)(2,1)S(1)}, bf16[20,512]{1,0:T(8,128)(2,1)S(1)}, u32[]{:S(2)}, u32[]{:S(2)}) collective-permute-start(bf16[20,512]{1,0:T(8,128)(2,1)S(1)} %multiply_convert_fusion.11), channel_id=1, source_target_pairs={{0,128},{64,192},{128,0},{192,64},{256,384},{320,448},{384,256},{4... | collective-permute-start | bytes 61448 | tf_op jit(solution)/shard_map/ppermute | solution.py:66
  195.4 6.3 %collective-permute-start.16 = (bf16[40,512]{1,0:T(8,128)(2,1)S(1)}, bf16[40,512]{1,0:T(8,128)(2,1)S(1)}, u32[]{:S(2)}, u32[]{:S(2)}) collective-permute-start(bf16[40,512]{1,0:T(8,128)(2,1)S(1)} %maximum_select_fusion.5), channel_id=1, source_target_pairs={{0,256},{64,320},{128,384},{192,448},{256,0},{320,64},{384,128},{4... | collective-permute-start | bytes 122888 | tf_op jit(solution)/shard_map/ppermute | solution.py:66
  201.7 5.2 %collective-permute-start.17 = (bf16[80,512]{1,0:T(8,128)(2,1)S(1)}, bf16[80,512]{1,0:T(8,128)(2,1)S(1)}, u32[]{:S(2)}, u32[]{:S(2)}) collective-permute-start(bf16[80,512]{1,0:T(8,128)(2,1)S(1)} %maximum_select_fusion.4), channel_id=1, source_target_pairs={{0,2},{1,3},{2,0},{3,1},{4,6},{5,7},{6,4},{7,5},{8,10},{9,11},{10,... | collective-permute-start | bytes 245768 | tf_op jit(solution)/shard_map/ppermute | solution.py:66
  206.9 6.1 %collective-permute-start.18 = (bf16[160,512]{1,0:T(8,128)(2,1)S(1)}, bf16[160,512]{1,0:T(8,128)(2,1)S(1)}, u32[]{:S(2)}, u32[]{:S(2)}) collective-permute-start(bf16[160,512]{1,0:T(8,128)(2,1)S(1)} %maximum_select_fusion.3), channel_id=1, source_target_pairs={{0,64},{64,0},{128,192},{192,128},{256,320},{320,256},{384,448},{4... | collective-permute-start | bytes 491528 | tf_op jit(solution)/shard_map/ppermute | solution.py:66
  213.1 7.8 %collective-permute-start.19 = (bf16[320,512]{1,0:T(8,128)(2,1)S(1)}, bf16[320,512]{1,0:T(8,128)(2,1)S(1)}, u32[]{:S(2)}, u32[]{:S(2)}) collective-permute-start(bf16[320,512]{1,0:T(8,128)(2,1)S(1)} %maximum_select_fusion.2), channel_id=1, source_target_pairs={{0,32},{1,33},{2,34},{3,35},{4,36},{5,37},{6,38},{7,39},{8,40},{9,... | collective-permute-start | bytes 983048 | tf_op jit(solution)/shard_map/ppermute | solution.py:66
  221.2 17.6 %collective-permute-start.20 = (bf16[640,512]{1,0:T(8,128)(2,1)S(1)}, bf16[640,512]{1,0:T(8,128)(2,1)S(1)}, u32[]{:S(2)}, u32[]{:S(2)}) collective-permute-start(bf16[640,512]{1,0:T(8,128)(2,1)S(1)} %maximum_select_fusion.1), channel_id=1, source_target_pairs={{0,1},{1,0},{2,3},{3,2},{4,5},{5,4},{6,7},{7,6},{8,9},{9,8},{10,11... | collective-permute-start | bytes 1966088 | tf_op jit(solution)/shard_map/ppermute | solution.py:66
  (17 other events, 50.8 us)

commit v9 on v8

--- a/solution.py
+++ b/solution.py
@@ -57,8 +57,20 @@
     return (local_grad, ahead_rows, (past_term, now_term, mix_term))
 
 
-HALVING_STEPS = (("tm", 1), ("tm", 32), ("dp", 1), ("tm", 2), ("dp", 4), ("dp", 2))
+HALVING_STEPS = ((1, 1), (32, 64), (64, 32), (2, 2), (256, 256), (128, 128))
+AXES = ("dp", "tm")
 BUTTERFLY_STEPS = (("tm", 4), ("tm", 8), ("tm", 16))
+
+
+def paired(value, masks):
+    count = lax.axis_size(AXES)
+    pairs = [(source, source ^ masks[source & 1]) for source in range(count)]
+    return lax.ppermute(value, AXES, pairs)
+
+
+def upper_of(masks):
+    index = lax.axis_index(AXES)
+    return (index & jnp.where((index & 1) != 0, masks[1], masks[0])) != 0
 
 
 def exchange(value, axis, mask):
@@ -70,21 +82,21 @@
     past_one, now_one, mix_one, past_two, now_two, mix_two = term_list
     blocks = (past_one, now_one, past_two, now_two, jnp.concatenate([mix_one, mix_two], axis=1))
     flat = jnp.concatenate(blocks)
-    for axis, mask in HALVING_STEPS:
+    for step, masks in enumerate(HALVING_STEPS):
         half = flat.shape[0] // 2
-        upper = (lax.axis_index(axis) & mask) != 0
+        upper = upper_of(masks)
         first, second = flat[:half], flat[half:]
         kept = jnp.where(upper, second, first)
         sent = jnp.where(upper, first, second)
-        flat = kept + exchange(sent, axis, mask)
-        if mask == 32:
+        flat = kept + paired(sent, masks)
+        if step == 1:
             flat, companion = lax.optimization_barrier((flat, companion))
     for axis, mask in BUTTERFLY_STEPS:
         flat = flat + exchange(flat, axis, mask)
     flat = (flat * scale_factor).astype(jnp.bfloat16)
-    for axis, mask in reversed(HALVING_STEPS):
-        upper = (lax.axis_index(axis) & mask) != 0
-        other = exchange(flat, axis, mask)
+    for masks in reversed(HALVING_STEPS):
+        upper = upper_of(masks)
+        other = paired(flat, masks)
         flat = jnp.where(upper, jnp.concatenate([other, flat]), jnp.concatenate([flat, other]))
     rows = past_one.shape[0]
     parts = [flat[index * rows:(index + 1) * rows] for index in range(len(blocks))]

time: 242 us -> 236 us (0.975)
  waiting for transfers between devices: 84.1 us -> 80.9 us
  starting transfers between devices: 130 us -> 127 us
    ppermute x15 -> x3, starting transfers between devices: 104 us -> 19.7 us  [exchange(): lax.ppermute(value, axis, [(source, source ^ mask) for source in range(co...]
    ppermute x0 -> x12, starting transfers between devices: none -> 82.4 us  [paired(): return lax.ppermute(value, AXES, pairs)]
    ppermute x15 -> x3, waiting for transfers between devices: 44.4 us -> 9.85 us  [exchange(): lax.ppermute(value, axis, [(source, source ^ mask) for source in range(co...]
    ppermute x0 -> x12, waiting for transfers between devices: none -> 31 us  [paired(): return lax.ppermute(value, AXES, pairs)]
  transfers between devices with their start and end apart: 21 -> 21, of which waited for: 20 -> 19; matrix products, arithmetic and copies ran while one was open for 4% -> 4% of each run, Pallas kernels for 0% -> 0%
where the time goes in v9:
time: 236 us; the launch traced here: 235 us
  starting transfers between devices  127 us (54%)
  waiting for transfers between devices  80.9 us (34%)
  matrix products  14.5 us (6%)
  local copies, waits for them, and re-layouts  5.84 us (2%)
  other arithmetic  5.15 us (2%)
    ppermute x12, starting transfers between devices, paired(): return lax.ppermute(value, AXES, pairs)  82.4 us
    ppermute x6, waiting for transfers between devices, shifted(): lax.ppermute(value, axis, [(source, source + steps) for source in range(l...  40 us
    ppermute x12, waiting for transfers between devices, paired(): return lax.ppermute(value, AXES, pairs)  31 us
    ppermute x6, starting transfers between devices, shifted(): lax.ppermute(value, axis, [(source, source + steps) for source in range(l...  25.3 us
    ppermute x3, starting transfers between devices, exchange(): lax.ppermute(value, axis, [(source, source ^ mask) for source in range(co...  19.7 us
    ppermute x3, waiting for transfers between devices, exchange(): lax.ppermute(value, axis, [(source, source ^ mask) for source in range(co...  9.85 us
  transfers between devices with their start and end apart: 21, of which 19 were waited for; matrix products, arithmetic and copies ran while one was open for 4% of the time, Pallas kernels for 0%

profile of v9, /device:TPU:1, one launch (start us, length us, event | category | flops | bytes accessed | tf_op | source)
XLA Modules:
  0.0 235.1 jit_solution(6957170368192184588)
XLA Ops:
  1.8 4.9 %collective-permute-start = (bf16[1,512,256]{2,1,0:T(8,128)(2,1)S(1)}, bf16[1,512,256]{2,1,0:T(8,128)(2,1)S(1)}, u32[]{:S(2)}, u32[]{:S(2)}) collective-permute-start(bf16[1,512,256]{2,1,0:T(8,128)(2,1)S(1)} %get-tuple-element.29), channel_id=1, source_target_pairs={{0,1},{1,2},{2,3},{3,4},{4,5},{5,6},{6,7},{7,8},{8,9},{9,10},{10,1... | collective-permute-start | bytes 786440 | tf_op jit(solution)/shard_map/ppermute | solution.py:15
  13.0 7.9 %collective-permute-start.1 = (bf16[1,512,256]{2,1,0:T(8,128)(2,1)S(1)}, bf16[1,512,256]{2,1,0:T(8,128)(2,1)S(1)}, u32[]{:S(2)}, u32[]{:S(2)}) collective-permute-start(bf16[1,512,256]{2,1,0:T(8,128)(2,1)S(1)} %get-tuple-element.27), channel_id=1, source_target_pairs={{0,8},{1,9},{2,10},{3,11},{4,12},{5,13},{6,14},{7,15},{8,16},{9,17... | collective-permute-start | bytes 786440 | tf_op jit(solution)/shard_map/ppermute | solution.py:15
  21.3 5.2 %collective-permute-done.1 = bf16[1,512,256]{2,1,0:T(8,128)(2,1)S(1)} collective-permute-done((bf16[1,512,256]{2,1,0:T(8,128)(2,1)S(1)}, bf16[1,512,256]{2,1,0:T(8,128)(2,1)S(1)}, u32[]{:S(2)}, u32[]{:S(2)}) %collective-permute-start.1) | collective-permute-done | bytes 262176 | tf_op jit(solution)/shard_map/ppermute | solution.py:15
  29.2 8.0 %collective-permute-start.2 = (bf16[1,512,256]{2,1,0:T(8,128)(2,1)S(1)}, bf16[1,512,256]{2,1,0:T(8,128)(2,1)S(1)}, u32[]{:S(2)}, u32[]{:S(2)}) collective-permute-start(bf16[1,512,256]{2,1,0:T(8,128)(2,1)S(1)} %get-tuple-element.10), channel_id=1, source_target_pairs={{0,8},{1,9},{2,10},{3,11},{4,12},{5,13},{6,14},{7,15},{8,16},{9,17... | collective-permute-start | bytes 786440 | tf_op jit(solution)/shard_map/ppermute | solution.py:15
  38.9 9.4 %collective-permute-done.2 = bf16[1,512,256]{2,1,0:T(8,128)(2,1)S(1)} collective-permute-done((bf16[1,512,256]{2,1,0:T(8,128)(2,1)S(1)}, bf16[1,512,256]{2,1,0:T(8,128)(2,1)S(1)}, u32[]{:S(2)}, u32[]{:S(2)}) %collective-permute-start.2) | collective-permute-done | bytes 262176 | tf_op jit(solution)/shard_map/ppermute | solution.py:15
  52.5 16.5 %collective-permute-done.4 = bf16[1,512,256]{2,1,0:T(8,128)(2,1)S(1)} collective-permute-done((bf16[1,512,256]{2,1,0:T(8,128)(2,1)S(1)}, bf16[1,512,256]{2,1,0:T(8,128)(2,1)S(1)}, u32[]{:S(2)}, u32[]{:S(2)}) %collective-permute-start.4) | collective-permute-done | bytes 262176 | tf_op jit(solution)/shard_map/ppermute | solution.py:15
  73.4 33.7 %collective-permute-start.5 = (f32[640,512]{1,0:T(8,128)}, f32[640,512]{1,0:T(8,128)}, u32[]{:S(2)}, u32[]{:S(2)}) collective-permute-start(f32[640,512]{1,0:T(8,128)} %fusion.10), channel_id=1, source_target_pairs={{0,1},{1,0},{2,3},{3,2},{4,5},{5,4},{6,7},{7,6},{8,9},{9,8},{10,11... | collective-permute-start | bytes 3932168 | tf_op jit(solution)/shard_map/ppermute | solution.py:68
  112.0 3.2 %collective-permute-start.6 = (f32[320,512]{1,0:T(8,128)S(1)}, f32[320,512]{1,0:T(8,128)S(1)}, u32[]{:S(2)}, u32[]{:S(2)}) collective-permute-start(f32[320,512]{1,0:T(8,128)S(1)} %slice_select_fusion), channel_id=1, source_target_pairs={{0,32},{1,65},{2,34},{3,67},{4,36},{5,69},{6,38},{7,71},{8,40},{9,... | collective-permute-start | bytes 1966088 | tf_op jit(solution)/shard_map/ppermute | solution.py:68
  117.9 6.3 %collective-permute-done.7 = bf16[1,512,256]{2,1,0:T(8,128)(2,1)} collective-permute-done((bf16[1,512,256]{2,1,0:T(8,128)(2,1)}, bf16[1,512,256]{2,1,0:T(8,128)(2,1)}, u32[]{:S(2)}, u32[]{:S(2)}) %collective-permute-start.7) | collective-permute-done | bytes 262176 | tf_op jit(solution)/shard_map/ppermute | solution.py:15
  129.7 5.2 %collective-permute-done.8 = f32[160,512]{1,0:T(8,128)S(1)} collective-permute-done((f32[160,512]{1,0:T(8,128)S(1)}, f32[160,512]{1,0:T(8,128)S(1)}, u32[]{:S(2)}, u32[]{:S(2)}) %collective-permute-start.8) | collective-permute-done | bytes 327712 | tf_op jit(solution)/shard_map/ppermute | solution.py:68
  137.7 4.9 %collective-permute-done.9 = f32[80,512]{1,0:T(8,128)S(1)} collective-permute-done((f32[80,512]{1,0:T(8,128)S(1)}, f32[80,512]{1,0:T(8,128)S(1)}, u32[]{:S(2)}, u32[]{:S(2)}) %collective-permute-start.9) | collective-permute-done | bytes 163872 | tf_op jit(solution)/shard_map/ppermute | solution.py:68
  142.6 4.8 %collective-permute-start.10 = (f32[40,512]{1,0:T(8,128)S(1)}, f32[40,512]{1,0:T(8,128)S(1)}, u32[]{:S(2)}, u32[]{:S(2)}) collective-permute-start(f32[40,512]{1,0:T(8,128)S(1)} %slice_select_fusion.3), channel_id=1, source_target_pairs={{0,256},{1,257},{2,258},{3,259},{4,260},{5,261},{6,262},{7,263},{8... | collective-permute-start | bytes 245768 | tf_op jit(solution)/shard_map/ppermute | solution.py:68
  149.7 4.9 %collective-permute-start.11 = (f32[20,512]{1,0:T(8,128)S(1)}, f32[20,512]{1,0:T(8,128)S(1)}, u32[]{:S(2)}, u32[]{:S(2)}) collective-permute-start(f32[20,512]{1,0:T(8,128)S(1)} %slice_select_fusion.4), channel_id=1, source_target_pairs={{0,128},{1,129},{2,130},{3,131},{4,132},{5,133},{6,134},{7,135},{8... | collective-permute-start | bytes 122888 | tf_op jit(solution)/shard_map/ppermute | solution.py:68
  156.0 5.6 %collective-permute-start.12 = (f32[20,512]{1,0:T(8,128)S(1)}, f32[20,512]{1,0:T(8,128)S(1)}, u32[]{:S(2)}, u32[]{:S(2)}) collective-permute-start(f32[20,512]{1,0:T(8,128)S(1)} %select_add_fusion.5), channel_id=1, source_target_pairs={{0,4},{1,5},{2,6},{3,7},{4,0},{5,1},{6,2},{7,3},{8,12},{9,13},{10,... | collective-permute-start | bytes 122888 | tf_op jit(solution)/shard_map/ppermute | solution.py:78
  163.1 6.5 %collective-permute-start.13 = (f32[20,512]{1,0:T(8,128)S(1)}, f32[20,512]{1,0:T(8,128)S(1)}, u32[]{:S(2)}, u32[]{:S(2)}) collective-permute-start(f32[20,512]{1,0:T(8,128)S(1)} %add.112), channel_id=1, source_target_pairs={{0,8},{1,9},{2,10},{3,11},{4,12},{5,13},{6,14},{7,15},{8,0},{9,1},... | collective-permute-start | bytes 122888 | tf_op jit(solution)/shard_map/ppermute | solution.py:78
  171.9 7.6 %collective-permute-start.14 = (f32[20,512]{1,0:T(8,128)S(1)}, f32[20,512]{1,0:T(8,128)S(1)}, u32[]{:S(2)}, u32[]{:S(2)}) collective-permute-start(f32[20,512]{1,0:T(8,128)S(1)} %add.113), channel_id=1, source_target_pairs={{0,16},{1,17},{2,18},{3,19},{4,20},{5,21},{6,22},{7,23},{8,24},{9,... | collective-permute-start | bytes 122888 | tf_op jit(solution)/shard_map/ppermute | solution.py:78
  179.5 6.1 %collective-permute-done.14 = f32[20,512]{1,0:T(8,128)S(1)} collective-permute-done((f32[20,512]{1,0:T(8,128)S(1)}, f32[20,512]{1,0:T(8,128)S(1)}, u32[]{:S(2)}, u32[]{:S(2)}) %collective-permute-start.14) | collective-permute-done | bytes 40992 | tf_op jit(solution)/shard_map/ppermute | solution.py:78
  185.6 4.7 %collective-permute-start.15 = (bf16[20,512]{1,0:T(8,128)(2,1)S(1)}, bf16[20,512]{1,0:T(8,128)(2,1)S(1)}, u32[]{:S(2)}, u32[]{:S(2)}) collective-permute-start(bf16[20,512]{1,0:T(8,128)(2,1)S(1)} %multiply_convert_fusion.11), channel_id=1, source_target_pairs={{0,128},{1,129},{2,130},{3,131},{4,132},{5,133},{6,134},{7,135},{8... | collective-permute-start | bytes 61448 | tf_op jit(solution)/shard_map/ppermute | solution.py:68
  191.7 4.5 %collective-permute-start.16 = (bf16[40,512]{1,0:T(8,128)(2,1)S(1)}, bf16[40,512]{1,0:T(8,128)(2,1)S(1)}, u32[]{:S(2)}, u32[]{:S(2)}) collective-permute-start(bf16[40,512]{1,0:T(8,128)(2,1)S(1)} %maximum_select_fusion.5), channel_id=1, source_target_pairs={{0,256},{1,257},{2,258},{3,259},{4,260},{5,261},{6,262},{7,263},{8... | collective-permute-start | bytes 122888 | tf_op jit(solution)/shard_map/ppermute | solution.py:68
  198.3 3.1 %collective-permute-start.17 = (bf16[80,512]{1,0:T(8,128)(2,1)S(1)}, bf16[80,512]{1,0:T(8,128)(2,1)S(1)}, u32[]{:S(2)}, u32[]{:S(2)}) collective-permute-start(bf16[80,512]{1,0:T(8,128)(2,1)S(1)} %maximum_select_fusion.4), channel_id=1, source_target_pairs={{0,2},{1,3},{2,0},{3,1},{4,6},{5,7},{6,4},{7,5},{8,10},{9,11},{10,... | collective-permute-start | bytes 245768 | tf_op jit(solution)/shard_map/ppermute | solution.py:68
  203.5 2.9 %collective-permute-start.18 = (bf16[160,512]{1,0:T(8,128)(2,1)S(1)}, bf16[160,512]{1,0:T(8,128)(2,1)S(1)}, u32[]{:S(2)}, u32[]{:S(2)}) collective-permute-start(bf16[160,512]{1,0:T(8,128)(2,1)S(1)} %maximum_select_fusion.3), channel_id=1, source_target_pairs={{0,64},{1,33},{2,66},{3,35},{4,68},{5,37},{6,70},{7,39},{8,72},{9,... | collective-permute-start | bytes 491528 | tf_op jit(solution)/shard_map/ppermute | solution.py:68
  206.4 3.2 %collective-permute-done.18 = bf16[160,512]{1,0:T(8,128)(2,1)S(1)} collective-permute-done((bf16[160,512]{1,0:T(8,128)(2,1)S(1)}, bf16[160,512]{1,0:T(8,128)(2,1)S(1)}, u32[]{:S(2)}, u32[]{:S(2)}) %collective-permute-start.18) | collective-permute-done | bytes 163872 | tf_op jit(solution)/shard_map/ppermute | solution.py:68
  211.7 5.7 %collective-permute-done.19 = bf16[320,512]{1,0:T(8,128)(2,1)S(1)} collective-permute-done((bf16[320,512]{1,0:T(8,128)(2,1)S(1)}, bf16[320,512]{1,0:T(8,128)(2,1)S(1)}, u32[]{:S(2)}, u32[]{:S(2)}) %collective-permute-start.19) | collective-permute-done | bytes 327712 | tf_op jit(solution)/shard_map/ppermute | solution.py:68
  217.7 13.4 %collective-permute-start.20 = (bf16[640,512]{1,0:T(8,128)(2,1)S(1)}, bf16[640,512]{1,0:T(8,128)(2,1)S(1)}, u32[]{:S(2)}, u32[]{:S(2)}) collective-permute-start(bf16[640,512]{1,0:T(8,128)(2,1)S(1)} %maximum_select_fusion.1), channel_id=1, source_target_pairs={{0,1},{1,0},{2,3},{3,2},{4,5},{5,4},{6,7},{7,6},{8,9},{9,8},{10,11... | collective-permute-start | bytes 1966088 | tf_op jit(solution)/shard_map/ppermute | solution.py:68
  (111 shorter events, 55.7 us)
Async XLA Ops:
  0.6 25.8 %copy-start = (bf16[256,512]{1,0:T(8,128)(2,1)S(1)}, bf16[256,512]{1,0:T(8,128)(2,1)}, u32[]{:S(2)}) copy-start(bf16[256,512]{1,0:T(8,128)(2,1)} %param.13) | copy-start | bytes 786436
  1.8 9.2 %collective-permute-start = (bf16[1,512,256]{2,1,0:T(8,128)(2,1)S(1)}, bf16[1,512,256]{2,1,0:T(8,128)(2,1)S(1)}, u32[]{:S(2)}, u32[]{:S(2)}) collective-permute-start(bf16[1,512,256]{2,1,0:T(8,128)(2,1)S(1)} %get-tuple-element.29), channel_id=1, source_target_pairs={{0,1},{1,2},{2,3},{3,4},{4,5},{5,6},{6,7},{7,8},{8,9},{9,10},{10,1... | collective-permute-start | bytes 786440 | tf_op jit(solution)/shard_map/ppermute | solution.py:15
  13.0 13.5 %collective-permute-start.1 = (bf16[1,512,256]{2,1,0:T(8,128)(2,1)S(1)}, bf16[1,512,256]{2,1,0:T(8,128)(2,1)S(1)}, u32[]{:S(2)}, u32[]{:S(2)}) collective-permute-start(bf16[1,512,256]{2,1,0:T(8,128)(2,1)S(1)} %get-tuple-element.27), channel_id=1, source_target_pairs={{0,8},{1,9},{2,10},{3,11},{4,12},{5,13},{6,14},{7,15},{8,16},{9,17... | collective-permute-start | bytes 786440 | tf_op jit(solution)/shard_map/ppermute | solution.py:15
  29.2 19.1 %collective-permute-start.2 = (bf16[1,512,256]{2,1,0:T(8,128)(2,1)S(1)}, bf16[1,512,256]{2,1,0:T(8,128)(2,1)S(1)}, u32[]{:S(2)}, u32[]{:S(2)}) collective-permute-start(bf16[1,512,256]{2,1,0:T(8,128)(2,1)S(1)} %get-tuple-element.10), channel_id=1, source_target_pairs={{0,8},{1,9},{2,10},{3,11},{4,12},{5,13},{6,14},{7,15},{8,16},{9,17... | collective-permute-start | bytes 786440 | tf_op jit(solution)/shard_map/ppermute | solution.py:15
  37.2 15.2 %collective-permute-start.3 = (bf16[1,512,256]{2,1,0:T(8,128)(2,1)S(1)}, bf16[1,512,256]{2,1,0:T(8,128)(2,1)S(1)}, u32[]{:S(2)}, u32[]{:S(2)}) collective-permute-start(bf16[1,512,256]{2,1,0:T(8,128)(2,1)S(1)} %fusion.4), channel_id=1, source_target_pairs={{8,0},{9,1},{10,2},{11,3},{12,4},{13,5},{14,6},{15,7},{16,8},{17,9... | collective-permute-start | bytes 786440 | tf_op jit(solution)/shard_map/ppermute | solution.py:15
  49.8 19.2 %collective-permute-start.4 = (bf16[1,512,256]{2,1,0:T(8,128)(2,1)S(1)}, bf16[1,512,256]{2,1,0:T(8,128)(2,1)S(1)}, u32[]{:S(2)}, u32[]{:S(2)}) collective-permute-start(bf16[1,512,256]{2,1,0:T(8,128)(2,1)S(1)} %fusion.5), channel_id=1, source_target_pairs={{8,0},{9,1},{10,2},{11,3},{12,4},{13,5},{14,6},{15,7},{16,8},{17,9... | collective-permute-start | bytes 786440 | tf_op jit(solution)/shard_map/ppermute | solution.py:15
  51.4 20.3 %copy-start.9 = (f32[256,256]{1,0:T(8,128)}, f32[256,256]{1,0:T(8,128)S(1)}, u32[]{:S(2)}) copy-start(f32[256,256]{1,0:T(8,128)S(1)} %convolution_add_fusion.9) | copy-start | bytes 786436
  72.0 35.1 %copy-start.12 = (bf16[256,512]{1,0:T(8,128)(2,1)S(1)}, bf16[256,512]{1,0:T(8,128)(2,1)}, u32[]{:S(2)}) copy-start(bf16[256,512]{1,0:T(8,128)(2,1)} %param.10) | copy-start | bytes 786436
  73.4 36.7 %collective-permute-start.5 = (f32[640,512]{1,0:T(8,128)}, f32[640,512]{1,0:T(8,128)}, u32[]{:S(2)}, u32[]{:S(2)}) collective-permute-start(f32[640,512]{1,0:T(8,128)} %fusion.10), channel_id=1, source_target_pairs={{0,1},{1,0},{2,3},{3,2},{4,5},{5,4},{6,7},{7,6},{8,9},{9,8},{10,11... | collective-permute-start | bytes 3932168 | tf_op jit(solution)/shard_map/ppermute | solution.py:68
  112.0 14.9 %collective-permute-start.6 = (f32[320,512]{1,0:T(8,128)S(1)}, f32[320,512]{1,0:T(8,128)S(1)}, u32[]{:S(2)}, u32[]{:S(2)}) collective-permute-start(f32[320,512]{1,0:T(8,128)S(1)} %slice_select_fusion), channel_id=1, source_target_pairs={{0,32},{1,65},{2,34},{3,67},{4,36},{5,69},{6,38},{7,71},{8,40},{9,... | collective-permute-start | bytes 1966088 | tf_op jit(solution)/shard_map/ppermute | solution.py:68
  116.0 8.2 %collective-permute-start.7 = (bf16[1,512,256]{2,1,0:T(8,128)(2,1)}, bf16[1,512,256]{2,1,0:T(8,128)(2,1)}, u32[]{:S(2)}, u32[]{:S(2)}) collective-permute-start(bf16[1,512,256]{2,1,0:T(8,128)(2,1)} %get-tuple-element.26), channel_id=1, source_target_pairs={{1,0},{2,1},{3,2},{4,3},{5,4},{6,5},{7,6},{8,7},{9,8},{10,9},{11,1... | collective-permute-start | bytes 786440 | tf_op jit(solution)/shard_map/ppermute | solution.py:15
  127.1 7.8 %collective-permute-start.8 = (f32[160,512]{1,0:T(8,128)S(1)}, f32[160,512]{1,0:T(8,128)S(1)}, u32[]{:S(2)}, u32[]{:S(2)}) collective-permute-start(f32[160,512]{1,0:T(8,128)S(1)} %slice_select_fusion.1), channel_id=1, source_target_pairs={{0,64},{1,33},{2,66},{3,35},{4,68},{5,37},{6,70},{7,39},{8,72},{9,... | collective-permute-start | bytes 983048 | tf_op jit(solution)/shard_map/ppermute | solution.py:68
  135.0 7.5 %collective-permute-start.9 = (f32[80,512]{1,0:T(8,128)S(1)}, f32[80,512]{1,0:T(8,128)S(1)}, u32[]{:S(2)}, u32[]{:S(2)}) collective-permute-start(f32[80,512]{1,0:T(8,128)S(1)} %slice_select_fusion.2), channel_id=1, source_target_pairs={{0,2},{1,3},{2,0},{3,1},{4,6},{5,7},{6,4},{7,5},{8,10},{9,11},{10,... | collective-permute-start | bytes 491528 | tf_op jit(solution)/shard_map/ppermute | solution.py:68
  142.6 7.0 %collective-permute-start.10 = (f32[40,512]{1,0:T(8,128)S(1)}, f32[40,512]{1,0:T(8,128)S(1)}, u32[]{:S(2)}, u32[]{:S(2)}) collective-permute-start(f32[40,512]{1,0:T(8,128)S(1)} %slice_select_fusion.3), channel_id=1, source_target_pairs={{0,256},{1,257},{2,258},{3,259},{4,260},{5,261},{6,262},{7,263},{8... | collective-permute-start | bytes 245768 | tf_op jit(solution)/shard_map/ppermute | solution.py:68
  149.7 6.3 %collective-permute-start.11 = (f32[20,512]{1,0:T(8,128)S(1)}, f32[20,512]{1,0:T(8,128)S(1)}, u32[]{:S(2)}, u32[]{:S(2)}) collective-permute-start(f32[20,512]{1,0:T(8,128)S(1)} %slice_select_fusion.4), channel_id=1, source_target_pairs={{0,128},{1,129},{2,130},{3,131},{4,132},{5,133},{6,134},{7,135},{8... | collective-permute-start | bytes 122888 | tf_op jit(solution)/shard_map/ppermute | solution.py:68
  156.0 7.1 %collective-permute-start.12 = (f32[20,512]{1,0:T(8,128)S(1)}, f32[20,512]{1,0:T(8,128)S(1)}, u32[]{:S(2)}, u32[]{:S(2)}) collective-permute-start(f32[20,512]{1,0:T(8,128)S(1)} %select_add_fusion.5), channel_id=1, source_target_pairs={{0,4},{1,5},{2,6},{3,7},{4,0},{5,1},{6,2},{7,3},{8,12},{9,13},{10,... | collective-permute-start | bytes 122888 | tf_op jit(solution)/shard_map/ppermute | solution.py:78
  163.1 8.7 %collective-permute-start.13 = (f32[20,512]{1,0:T(8,128)S(1)}, f32[20,512]{1,0:T(8,128)S(1)}, u32[]{:S(2)}, u32[]{:S(2)}) collective-permute-start(f32[20,512]{1,0:T(8,128)S(1)} %add.112), channel_id=1, source_target_pairs={{0,8},{1,9},{2,10},{3,11},{4,12},{5,13},{6,14},{7,15},{8,0},{9,1},... | collective-permute-start | bytes 122888 | tf_op jit(solution)/shard_map/ppermute | solution.py:78
  171.9 13.7 %collective-permute-start.14 = (f32[20,512]{1,0:T(8,128)S(1)}, f32[20,512]{1,0:T(8,128)S(1)}, u32[]{:S(2)}, u32[]{:S(2)}) collective-permute-start(f32[20,512]{1,0:T(8,128)S(1)} %add.113), channel_id=1, source_target_pairs={{0,16},{1,17},{2,18},{3,19},{4,20},{5,21},{6,22},{7,23},{8,24},{9,... | collective-permute-start | bytes 122888 | tf_op jit(solution)/shard_map/ppermute | solution.py:78
  185.6 6.1 %collective-permute-start.15 = (bf16[20,512]{1,0:T(8,128)(2,1)S(1)}, bf16[20,512]{1,0:T(8,128)(2,1)S(1)}, u32[]{:S(2)}, u32[]{:S(2)}) collective-permute-start(bf16[20,512]{1,0:T(8,128)(2,1)S(1)} %multiply_convert_fusion.11), channel_id=1, source_target_pairs={{0,128},{1,129},{2,130},{3,131},{4,132},{5,133},{6,134},{7,135},{8... | collective-permute-start | bytes 61448 | tf_op jit(solution)/shard_map/ppermute | solution.py:68
  191.7 6.5 %collective-permute-start.16 = (bf16[40,512]{1,0:T(8,128)(2,1)S(1)}, bf16[40,512]{1,0:T(8,128)(2,1)S(1)}, u32[]{:S(2)}, u32[]{:S(2)}) collective-permute-start(bf16[40,512]{1,0:T(8,128)(2,1)S(1)} %maximum_select_fusion.5), channel_id=1, source_target_pairs={{0,256},{1,257},{2,258},{3,259},{4,260},{5,261},{6,262},{7,263},{8... | collective-permute-start | bytes 122888 | tf_op jit(solution)/shard_map/ppermute | solution.py:68
  198.3 5.2 %collective-permute-start.17 = (bf16[80,512]{1,0:T(8,128)(2,1)S(1)}, bf16[80,512]{1,0:T(8,128)(2,1)S(1)}, u32[]{:S(2)}, u32[]{:S(2)}) collective-permute-start(bf16[80,512]{1,0:T(8,128)(2,1)S(1)} %maximum_select_fusion.4), channel_id=1, source_target_pairs={{0,2},{1,3},{2,0},{3,1},{4,6},{5,7},{6,4},{7,5},{8,10},{9,11},{10,... | collective-permute-start | bytes 245768 | tf_op jit(solution)/shard_map/ppermute | solution.py:68
  203.5 6.1 %collective-permute-start.18 = (bf16[160,512]{1,0:T(8,128)(2,1)S(1)}, bf16[160,512]{1,0:T(8,128)(2,1)S(1)}, u32[]{:S(2)}, u32[]{:S(2)}) collective-permute-start(bf16[160,512]{1,0:T(8,128)(2,1)S(1)} %maximum_select_fusion.3), channel_id=1, source_target_pairs={{0,64},{1,33},{2,66},{3,35},{4,68},{5,37},{6,70},{7,39},{8,72},{9,... | collective-permute-start | bytes 491528 | tf_op jit(solution)/shard_map/ppermute | solution.py:68
  209.7 7.8 %collective-permute-start.19 = (bf16[320,512]{1,0:T(8,128)(2,1)S(1)}, bf16[320,512]{1,0:T(8,128)(2,1)S(1)}, u32[]{:S(2)}, u32[]{:S(2)}) collective-permute-start(bf16[320,512]{1,0:T(8,128)(2,1)S(1)} %maximum_select_fusion.2), channel_id=1, source_target_pairs={{0,32},{1,65},{2,34},{3,67},{4,36},{5,69},{6,38},{7,71},{8,40},{9,... | collective-permute-start | bytes 983048 | tf_op jit(solution)/shard_map/ppermute | solution.py:68
  217.7 15.1 %collective-permute-start.20 = (bf16[640,512]{1,0:T(8,128)(2,1)S(1)}, bf16[640,512]{1,0:T(8,128)(2,1)S(1)}, u32[]{:S(2)}, u32[]{:S(2)}) collective-permute-start(bf16[640,512]{1,0:T(8,128)(2,1)S(1)} %maximum_select_fusion.1), channel_id=1, source_target_pairs={{0,1},{1,0},{2,3},{3,2},{4,5},{5,4},{6,7},{7,6},{8,9},{9,8},{10,11... | collective-permute-start | bytes 1966088 | tf_op jit(solution)/shard_map/ppermute | solution.py:68
  (17 other events, 50.8 us)

commit v10 on v9

--- a/solution.py
+++ b/solution.py
@@ -57,7 +57,7 @@
     return (local_grad, ahead_rows, (past_term, now_term, mix_term))
 
 
-HALVING_STEPS = ((1, 1), (32, 64), (64, 32), (2, 2), (256, 256), (128, 128))
+HALVING_STEPS = ((1, 1), (32, 64), (64, 32), (2, 256), (256, 2), (128, 128))
 AXES = ("dp", "tm")
 BUTTERFLY_STEPS = (("tm", 4), ("tm", 8), ("tm", 16))
 

time: 236 us -> 235 us (level)
  starting transfers between devices: 127 us -> 132 us
  waiting for transfers between devices: 80.9 us -> 76.1 us
    ppermute x12, starting transfers between devices: 82.4 us -> 85.4 us  [paired(): return lax.ppermute(value, AXES, pairs)]
    ppermute x12, waiting for transfers between devices: 31 us -> 28.3 us  [paired(): return lax.ppermute(value, AXES, pairs)]
where the time goes in v10:
time: 235 us
  starting transfers between devices  132 us (56%)
  waiting for transfers between devices  76.1 us (32%)
  matrix products  14.5 us (6%)
  local copies, waits for them, and re-layouts  5.84 us (2%)
  other arithmetic  5.15 us (2%)
    ppermute x12, starting transfers between devices, paired(): return lax.ppermute(value, AXES, pairs)  85.4 us
    ppermute x6, waiting for transfers between devices, shifted(): lax.ppermute(value, axis, [(source, source + steps) for source in range(l...  40 us
    ppermute x12, waiting for transfers between devices, paired(): return lax.ppermute(value, AXES, pairs)  28.3 us
    ppermute x6, starting transfers between devices, shifted(): lax.ppermute(value, axis, [(source, source + steps) for source in range(l...  25.3 us
    ppermute x3, starting transfers between devices, exchange(): lax.ppermute(value, axis, [(source, source ^ mask) for source in range(co...  21.1 us
    ppermute x3, waiting for transfers between devices, exchange(): lax.ppermute(value, axis, [(source, source ^ mask) for source in range(co...  7.78 us
  transfers between devices with their start and end apart: 21, of which 19 were waited for; matrix products, arithmetic and copies ran while one was open for 4% of the time, Pallas kernels for 0%

profile of v10, /device:TPU:1, one launch (start us, length us, event | category | flops | bytes accessed | tf_op | source)
XLA Modules:
  0.0 234.7 jit_solution(8302467036496331131)
XLA Ops:
  1.8 4.9 %collective-permute-start = (bf16[1,512,256]{2,1,0:T(8,128)(2,1)S(1)}, bf16[1,512,256]{2,1,0:T(8,128)(2,1)S(1)}, u32[]{:S(2)}, u32[]{:S(2)}) collective-permute-start(bf16[1,512,256]{2,1,0:T(8,128)(2,1)S(1)} %get-tuple-element.29), channel_id=1, source_target_pairs={{0,1},{1,2},{2,3},{3,4},{4,5},{5,6},{6,7},{7,8},{8,9},{9,10},{10,1... | collective-permute-start | bytes 786440 | tf_op jit(solution)/shard_map/ppermute | solution.py:15
  13.0 7.9 %collective-permute-start.1 = (bf16[1,512,256]{2,1,0:T(8,128)(2,1)S(1)}, bf16[1,512,256]{2,1,0:T(8,128)(2,1)S(1)}, u32[]{:S(2)}, u32[]{:S(2)}) collective-permute-start(bf16[1,512,256]{2,1,0:T(8,128)(2,1)S(1)} %get-tuple-element.27), channel_id=1, source_target_pairs={{0,8},{1,9},{2,10},{3,11},{4,12},{5,13},{6,14},{7,15},{8,16},{9,17... | collective-permute-start | bytes 786440 | tf_op jit(solution)/shard_map/ppermute | solution.py:15
  21.3 5.2 %collective-permute-done.1 = bf16[1,512,256]{2,1,0:T(8,128)(2,1)S(1)} collective-permute-done((bf16[1,512,256]{2,1,0:T(8,128)(2,1)S(1)}, bf16[1,512,256]{2,1,0:T(8,128)(2,1)S(1)}, u32[]{:S(2)}, u32[]{:S(2)}) %collective-permute-start.1) | collective-permute-done | bytes 262176 | tf_op jit(solution)/shard_map/ppermute | solution.py:15
  29.2 8.0 %collective-permute-start.2 = (bf16[1,512,256]{2,1,0:T(8,128)(2,1)S(1)}, bf16[1,512,256]{2,1,0:T(8,128)(2,1)S(1)}, u32[]{:S(2)}, u32[]{:S(2)}) collective-permute-start(bf16[1,512,256]{2,1,0:T(8,128)(2,1)S(1)} %get-tuple-element.10), channel_id=1, source_target_pairs={{0,8},{1,9},{2,10},{3,11},{4,12},{5,13},{6,14},{7,15},{8,16},{9,17... | collective-permute-start | bytes 786440 | tf_op jit(solution)/shard_map/ppermute | solution.py:15
  38.9 9.4 %collective-permute-done.2 = bf16[1,512,256]{2,1,0:T(8,128)(2,1)S(1)} collective-permute-done((bf16[1,512,256]{2,1,0:T(8,128)(2,1)S(1)}, bf16[1,512,256]{2,1,0:T(8,128)(2,1)S(1)}, u32[]{:S(2)}, u32[]{:S(2)}) %collective-permute-start.2) | collective-permute-done | bytes 262176 | tf_op jit(solution)/shard_map/ppermute | solution.py:15
  52.5 16.5 %collective-permute-done.4 = bf16[1,512,256]{2,1,0:T(8,128)(2,1)S(1)} collective-permute-done((bf16[1,512,256]{2,1,0:T(8,128)(2,1)S(1)}, bf16[1,512,256]{2,1,0:T(8,128)(2,1)S(1)}, u32[]{:S(2)}, u32[]{:S(2)}) %collective-permute-start.4) | collective-permute-done | bytes 262176 | tf_op jit(solution)/shard_map/ppermute | solution.py:15
  73.4 33.7 %collective-permute-start.5 = (f32[640,512]{1,0:T(8,128)}, f32[640,512]{1,0:T(8,128)}, u32[]{:S(2)}, u32[]{:S(2)}) collective-permute-start(f32[640,512]{1,0:T(8,128)} %fusion.10), channel_id=1, source_target_pairs={{0,1},{1,0},{2,3},{3,2},{4,5},{5,4},{6,7},{7,6},{8,9},{9,8},{10,11... | collective-permute-start | bytes 3932168 | tf_op jit(solution)/shard_map/ppermute | solution.py:68
  112.0 3.2 %collective-permute-start.6 = (f32[320,512]{1,0:T(8,128)S(1)}, f32[320,512]{1,0:T(8,128)S(1)}, u32[]{:S(2)}, u32[]{:S(2)}) collective-permute-start(f32[320,512]{1,0:T(8,128)S(1)} %slice_select_fusion), channel_id=1, source_target_pairs={{0,32},{1,65},{2,34},{3,67},{4,36},{5,69},{6,38},{7,71},{8,40},{9,... | collective-permute-start | bytes 1966088 | tf_op jit(solution)/shard_map/ppermute | solution.py:68
  117.9 6.3 %collective-permute-done.7 = bf16[1,512,256]{2,1,0:T(8,128)(2,1)} collective-permute-done((bf16[1,512,256]{2,1,0:T(8,128)(2,1)}, bf16[1,512,256]{2,1,0:T(8,128)(2,1)}, u32[]{:S(2)}, u32[]{:S(2)}) %collective-permute-start.7) | collective-permute-done | bytes 262176 | tf_op jit(solution)/shard_map/ppermute | solution.py:15
  129.7 5.2 %collective-permute-done.8 = f32[160,512]{1,0:T(8,128)S(1)} collective-permute-done((f32[160,512]{1,0:T(8,128)S(1)}, f32[160,512]{1,0:T(8,128)S(1)}, u32[]{:S(2)}, u32[]{:S(2)}) %collective-permute-start.8) | collective-permute-done | bytes 327712 | tf_op jit(solution)/shard_map/ppermute | solution.py:68
  135.0 4.5 %collective-permute-start.9 = (f32[80,512]{1,0:T(8,128)S(1)}, f32[80,512]{1,0:T(8,128)S(1)}, u32[]{:S(2)}, u32[]{:S(2)}) collective-permute-start(f32[80,512]{1,0:T(8,128)S(1)} %slice_select_fusion.2), channel_id=1, source_target_pairs={{0,2},{1,257},{2,0},{3,259},{4,6},{5,261},{6,4},{7,263},{8,10},{9,... | collective-permute-start | bytes 491528 | tf_op jit(solution)/shard_map/ppermute | solution.py:68
  139.5 3.1 %collective-permute-done.9 = f32[80,512]{1,0:T(8,128)S(1)} collective-permute-done((f32[80,512]{1,0:T(8,128)S(1)}, f32[80,512]{1,0:T(8,128)S(1)}, u32[]{:S(2)}, u32[]{:S(2)}) %collective-permute-start.9) | collective-permute-done | bytes 163872 | tf_op jit(solution)/shard_map/ppermute | solution.py:68
  148.2 4.6 %collective-permute-start.11 = (f32[20,512]{1,0:T(8,128)S(1)}, f32[20,512]{1,0:T(8,128)S(1)}, u32[]{:S(2)}, u32[]{:S(2)}) collective-permute-start(f32[20,512]{1,0:T(8,128)S(1)} %slice_select_fusion.4), channel_id=1, source_target_pairs={{0,128},{1,129},{2,130},{3,131},{4,132},{5,133},{6,134},{7,135},{8... | collective-permute-start | bytes 122888 | tf_op jit(solution)/shard_map/ppermute | solution.py:68
  154.5 5.0 %collective-permute-start.12 = (f32[20,512]{1,0:T(8,128)S(1)}, f32[20,512]{1,0:T(8,128)S(1)}, u32[]{:S(2)}, u32[]{:S(2)}) collective-permute-start(f32[20,512]{1,0:T(8,128)S(1)} %select_add_fusion.5), channel_id=1, source_target_pairs={{0,4},{1,5},{2,6},{3,7},{4,0},{5,1},{6,2},{7,3},{8,12},{9,13},{10,... | collective-permute-start | bytes 122888 | tf_op jit(solution)/shard_map/ppermute | solution.py:78
  161.1 6.8 %collective-permute-start.13 = (f32[20,512]{1,0:T(8,128)S(1)}, f32[20,512]{1,0:T(8,128)S(1)}, u32[]{:S(2)}, u32[]{:S(2)}) collective-permute-start(f32[20,512]{1,0:T(8,128)S(1)} %add.112), channel_id=1, source_target_pairs={{0,8},{1,9},{2,10},{3,11},{4,12},{5,13},{6,14},{7,15},{8,0},{9,1},... | collective-permute-start | bytes 122888 | tf_op jit(solution)/shard_map/ppermute | solution.py:78
  169.8 9.3 %collective-permute-start.14 = (f32[20,512]{1,0:T(8,128)S(1)}, f32[20,512]{1,0:T(8,128)S(1)}, u32[]{:S(2)}, u32[]{:S(2)}) collective-permute-start(f32[20,512]{1,0:T(8,128)S(1)} %add.113), channel_id=1, source_target_pairs={{0,16},{1,17},{2,18},{3,19},{4,20},{5,21},{6,22},{7,23},{8,24},{9,... | collective-permute-start | bytes 122888 | tf_op jit(solution)/shard_map/ppermute | solution.py:78
  179.1 4.4 %collective-permute-done.14 = f32[20,512]{1,0:T(8,128)S(1)} collective-permute-done((f32[20,512]{1,0:T(8,128)S(1)}, f32[20,512]{1,0:T(8,128)S(1)}, u32[]{:S(2)}, u32[]{:S(2)}) %collective-permute-start.14) | collective-permute-done | bytes 40992 | tf_op jit(solution)/shard_map/ppermute | solution.py:78
  183.5 4.8 %collective-permute-start.15 = (bf16[20,512]{1,0:T(8,128)(2,1)S(1)}, bf16[20,512]{1,0:T(8,128)(2,1)S(1)}, u32[]{:S(2)}, u32[]{:S(2)}) collective-permute-start(bf16[20,512]{1,0:T(8,128)(2,1)S(1)} %multiply_convert_fusion.11), channel_id=1, source_target_pairs={{0,128},{1,129},{2,130},{3,131},{4,132},{5,133},{6,134},{7,135},{8... | collective-permute-start | bytes 61448 | tf_op jit(solution)/shard_map/ppermute | solution.py:68
  189.6 3.2 %collective-permute-start.16 = (bf16[40,512]{1,0:T(8,128)(2,1)S(1)}, bf16[40,512]{1,0:T(8,128)(2,1)S(1)}, u32[]{:S(2)}, u32[]{:S(2)}) collective-permute-start(bf16[40,512]{1,0:T(8,128)(2,1)S(1)} %maximum_select_fusion.5), channel_id=1, source_target_pairs={{0,256},{1,3},{2,258},{3,1},{4,260},{5,7},{6,262},{7,5},{8,264},{9... | collective-permute-start | bytes 122888 | tf_op jit(solution)/shard_map/ppermute | solution.py:68
  194.4 4.6 %collective-permute-start.17 = (bf16[80,512]{1,0:T(8,128)(2,1)S(1)}, bf16[80,512]{1,0:T(8,128)(2,1)S(1)}, u32[]{:S(2)}, u32[]{:S(2)}) collective-permute-start(bf16[80,512]{1,0:T(8,128)(2,1)S(1)} %maximum_select_fusion.4), channel_id=1, source_target_pairs={{0,2},{1,257},{2,0},{3,259},{4,6},{5,261},{6,4},{7,263},{8,10},{9,... | collective-permute-start | bytes 245768 | tf_op jit(solution)/shard_map/ppermute | solution.py:68
  201.1 3.1 %collective-permute-start.18 = (bf16[160,512]{1,0:T(8,128)(2,1)S(1)}, bf16[160,512]{1,0:T(8,128)(2,1)S(1)}, u32[]{:S(2)}, u32[]{:S(2)}) collective-permute-start(bf16[160,512]{1,0:T(8,128)(2,1)S(1)} %maximum_select_fusion.3), channel_id=1, source_target_pairs={{0,64},{1,33},{2,66},{3,35},{4,68},{5,37},{6,70},{7,39},{8,72},{9,... | collective-permute-start | bytes 491528 | tf_op jit(solution)/shard_map/ppermute | solution.py:68
  207.2 3.2 %collective-permute-start.19 = (bf16[320,512]{1,0:T(8,128)(2,1)S(1)}, bf16[320,512]{1,0:T(8,128)(2,1)S(1)}, u32[]{:S(2)}, u32[]{:S(2)}) collective-permute-start(bf16[320,512]{1,0:T(8,128)(2,1)S(1)} %maximum_select_fusion.2), channel_id=1, source_target_pairs={{0,32},{1,65},{2,34},{3,67},{4,36},{5,69},{6,38},{7,71},{8,40},{9,... | collective-permute-start | bytes 983048 | tf_op jit(solution)/shard_map/ppermute | solution.py:68
  210.4 4.7 %collective-permute-done.19 = bf16[320,512]{1,0:T(8,128)(2,1)S(1)} collective-permute-done((bf16[320,512]{1,0:T(8,128)(2,1)S(1)}, bf16[320,512]{1,0:T(8,128)(2,1)S(1)}, u32[]{:S(2)}, u32[]{:S(2)}) %collective-permute-start.19) | collective-permute-done | bytes 327712 | tf_op jit(solution)/shard_map/ppermute | solution.py:68
  215.3 15.4 %collective-permute-start.20 = (bf16[640,512]{1,0:T(8,128)(2,1)S(1)}, bf16[640,512]{1,0:T(8,128)(2,1)S(1)}, u32[]{:S(2)}, u32[]{:S(2)}) collective-permute-start(bf16[640,512]{1,0:T(8,128)(2,1)S(1)} %maximum_select_fusion.1), channel_id=1, source_target_pairs={{0,1},{1,0},{2,3},{3,2},{4,5},{5,4},{6,7},{7,6},{8,9},{9,8},{10,11... | collective-permute-start | bytes 1966088 | tf_op jit(solution)/shard_map/ppermute | solution.py:68
  (111 shorter events, 56.5 us)
Async XLA Ops:
  0.6 25.8 %copy-start = (bf16[256,512]{1,0:T(8,128)(2,1)S(1)}, bf16[256,512]{1,0:T(8,128)(2,1)}, u32[]{:S(2)}) copy-start(bf16[256,512]{1,0:T(8,128)(2,1)} %param.13) | copy-start | bytes 786436
  1.8 9.2 %collective-permute-start = (bf16[1,512,256]{2,1,0:T(8,128)(2,1)S(1)}, bf16[1,512,256]{2,1,0:T(8,128)(2,1)S(1)}, u32[]{:S(2)}, u32[]{:S(2)}) collective-permute-start(bf16[1,512,256]{2,1,0:T(8,128)(2,1)S(1)} %get-tuple-element.29), channel_id=1, source_target_pairs={{0,1},{1,2},{2,3},{3,4},{4,5},{5,6},{6,7},{7,8},{8,9},{9,10},{10,1... | collective-permute-start | bytes 786440 | tf_op jit(solution)/shard_map/ppermute | solution.py:15
  13.0 13.5 %collective-permute-start.1 = (bf16[1,512,256]{2,1,0:T(8,128)(2,1)S(1)}, bf16[1,512,256]{2,1,0:T(8,128)(2,1)S(1)}, u32[]{:S(2)}, u32[]{:S(2)}) collective-permute-start(bf16[1,512,256]{2,1,0:T(8,128)(2,1)S(1)} %get-tuple-element.27), channel_id=1, source_target_pairs={{0,8},{1,9},{2,10},{3,11},{4,12},{5,13},{6,14},{7,15},{8,16},{9,17... | collective-permute-start | bytes 786440 | tf_op jit(solution)/shard_map/ppermute | solution.py:15
  29.2 19.1 %collective-permute-start.2 = (bf16[1,512,256]{2,1,0:T(8,128)(2,1)S(1)}, bf16[1,512,256]{2,1,0:T(8,128)(2,1)S(1)}, u32[]{:S(2)}, u32[]{:S(2)}) collective-permute-start(bf16[1,512,256]{2,1,0:T(8,128)(2,1)S(1)} %get-tuple-element.10), channel_id=1, source_target_pairs={{0,8},{1,9},{2,10},{3,11},{4,12},{5,13},{6,14},{7,15},{8,16},{9,17... | collective-permute-start | bytes 786440 | tf_op jit(solution)/shard_map/ppermute | solution.py:15
  37.2 15.2 %collective-permute-start.3 = (bf16[1,512,256]{2,1,0:T(8,128)(2,1)S(1)}, bf16[1,512,256]{2,1,0:T(8,128)(2,1)S(1)}, u32[]{:S(2)}, u32[]{:S(2)}) collective-permute-start(bf16[1,512,256]{2,1,0:T(8,128)(2,1)S(1)} %fusion.4), channel_id=1, source_target_pairs={{8,0},{9,1},{10,2},{11,3},{12,4},{13,5},{14,6},{15,7},{16,8},{17,9... | collective-permute-start | bytes 786440 | tf_op jit(solution)/shard_map/ppermute | solution.py:15
  49.8 19.2 %collective-permute-start.4 = (bf16[1,512,256]{2,1,0:T(8,128)(2,1)S(1)}, bf16[1,512,256]{2,1,0:T(8,128)(2,1)S(1)}, u32[]{:S(2)}, u32[]{:S(2)}) collective-permute-start(bf16[1,512,256]{2,1,0:T(8,128)(2,1)S(1)} %fusion.5), channel_id=1, source_target_pairs={{8,0},{9,1},{10,2},{11,3},{12,4},{13,5},{14,6},{15,7},{16,8},{17,9... | collective-permute-start | bytes 786440 | tf_op jit(solution)/shard_map/ppermute | solution.py:15
  51.4 20.3 %copy-start.9 = (f32[256,256]{1,0:T(8,128)}, f32[256,256]{1,0:T(8,128)S(1)}, u32[]{:S(2)}) copy-start(f32[256,256]{1,0:T(8,128)S(1)} %convolution_add_fusion.9) | copy-start | bytes 786436
  72.0 35.1 %copy-start.12 = (bf16[256,512]{1,0:T(8,128)(2,1)S(1)}, bf16[256,512]{1,0:T(8,128)(2,1)}, u32[]{:S(2)}) copy-start(bf16[256,512]{1,0:T(8,128)(2,1)} %param.10) | copy-start | bytes 786436
  73.4 36.7 %collective-permute-start.5 = (f32[640,512]{1,0:T(8,128)}, f32[640,512]{1,0:T(8,128)}, u32[]{:S(2)}, u32[]{:S(2)}) collective-permute-start(f32[640,512]{1,0:T(8,128)} %fusion.10), channel_id=1, source_target_pairs={{0,1},{1,0},{2,3},{3,2},{4,5},{5,4},{6,7},{7,6},{8,9},{9,8},{10,11... | collective-permute-start | bytes 3932168 | tf_op jit(solution)/shard_map/ppermute | solution.py:68
  112.0 14.9 %collective-permute-start.6 = (f32[320,512]{1,0:T(8,128)S(1)}, f32[320,512]{1,0:T(8,128)S(1)}, u32[]{:S(2)}, u32[]{:S(2)}) collective-permute-start(f32[320,512]{1,0:T(8,128)S(1)} %slice_select_fusion), channel_id=1, source_target_pairs={{0,32},{1,65},{2,34},{3,67},{4,36},{5,69},{6,38},{7,71},{8,40},{9,... | collective-permute-start | bytes 1966088 | tf_op jit(solution)/shard_map/ppermute | solution.py:68
  116.0 8.2 %collective-permute-start.7 = (bf16[1,512,256]{2,1,0:T(8,128)(2,1)}, bf16[1,512,256]{2,1,0:T(8,128)(2,1)}, u32[]{:S(2)}, u32[]{:S(2)}) collective-permute-start(bf16[1,512,256]{2,1,0:T(8,128)(2,1)} %get-tuple-element.26), channel_id=1, source_target_pairs={{1,0},{2,1},{3,2},{4,3},{5,4},{6,5},{7,6},{8,7},{9,8},{10,9},{11,1... | collective-permute-start | bytes 786440 | tf_op jit(solution)/shard_map/ppermute | solution.py:15
  127.1 7.8 %collective-permute-start.8 = (f32[160,512]{1,0:T(8,128)S(1)}, f32[160,512]{1,0:T(8,128)S(1)}, u32[]{:S(2)}, u32[]{:S(2)}) collective-permute-start(f32[160,512]{1,0:T(8,128)S(1)} %slice_select_fusion.1), channel_id=1, source_target_pairs={{0,64},{1,33},{2,66},{3,35},{4,68},{5,37},{6,70},{7,39},{8,72},{9,... | collective-permute-start | bytes 983048 | tf_op jit(solution)/shard_map/ppermute | solution.py:68
  135.0 7.6 %collective-permute-start.9 = (f32[80,512]{1,0:T(8,128)S(1)}, f32[80,512]{1,0:T(8,128)S(1)}, u32[]{:S(2)}, u32[]{:S(2)}) collective-permute-start(f32[80,512]{1,0:T(8,128)S(1)} %slice_select_fusion.2), channel_id=1, source_target_pairs={{0,2},{1,257},{2,0},{3,259},{4,6},{5,261},{6,4},{7,263},{8,10},{9,... | collective-permute-start | bytes 491528 | tf_op jit(solution)/shard_map/ppermute | solution.py:68
  142.7 5.5 %collective-permute-start.10 = (f32[40,512]{1,0:T(8,128)S(1)}, f32[40,512]{1,0:T(8,128)S(1)}, u32[]{:S(2)}, u32[]{:S(2)}) collective-permute-start(f32[40,512]{1,0:T(8,128)S(1)} %slice_select_fusion.3), channel_id=1, source_target_pairs={{0,256},{1,3},{2,258},{3,1},{4,260},{5,7},{6,262},{7,5},{8,264},{9... | collective-permute-start | bytes 245768 | tf_op jit(solution)/shard_map/ppermute | solution.py:68
  148.2 6.3 %collective-permute-start.11 = (f32[20,512]{1,0:T(8,128)S(1)}, f32[20,512]{1,0:T(8,128)S(1)}, u32[]{:S(2)}, u32[]{:S(2)}) collective-permute-start(f32[20,512]{1,0:T(8,128)S(1)} %slice_select_fusion.4), channel_id=1, source_target_pairs={{0,128},{1,129},{2,130},{3,131},{4,132},{5,133},{6,134},{7,135},{8... | collective-permute-start | bytes 122888 | tf_op jit(solution)/shard_map/ppermute | solution.py:68
  154.5 6.5 %collective-permute-start.12 = (f32[20,512]{1,0:T(8,128)S(1)}, f32[20,512]{1,0:T(8,128)S(1)}, u32[]{:S(2)}, u32[]{:S(2)}) collective-permute-start(f32[20,512]{1,0:T(8,128)S(1)} %select_add_fusion.5), channel_id=1, source_target_pairs={{0,4},{1,5},{2,6},{3,7},{4,0},{5,1},{6,2},{7,3},{8,12},{9,13},{10,... | collective-permute-start | bytes 122888 | tf_op jit(solution)/shard_map/ppermute | solution.py:78
  161.1 8.7 %collective-permute-start.13 = (f32[20,512]{1,0:T(8,128)S(1)}, f32[20,512]{1,0:T(8,128)S(1)}, u32[]{:S(2)}, u32[]{:S(2)}) collective-permute-start(f32[20,512]{1,0:T(8,128)S(1)} %add.112), channel_id=1, source_target_pairs={{0,8},{1,9},{2,10},{3,11},{4,12},{5,13},{6,14},{7,15},{8,0},{9,1},... | collective-permute-start | bytes 122888 | tf_op jit(solution)/shard_map/ppermute | solution.py:78
  169.8 13.7 %collective-permute-start.14 = (f32[20,512]{1,0:T(8,128)S(1)}, f32[20,512]{1,0:T(8,128)S(1)}, u32[]{:S(2)}, u32[]{:S(2)}) collective-permute-start(f32[20,512]{1,0:T(8,128)S(1)} %add.113), channel_id=1, source_target_pairs={{0,16},{1,17},{2,18},{3,19},{4,20},{5,21},{6,22},{7,23},{8,24},{9,... | collective-permute-start | bytes 122888 | tf_op jit(solution)/shard_map/ppermute | solution.py:78
  183.5 6.1 %collective-permute-start.15 = (bf16[20,512]{1,0:T(8,128)(2,1)S(1)}, bf16[20,512]{1,0:T(8,128)(2,1)S(1)}, u32[]{:S(2)}, u32[]{:S(2)}) collective-permute-start(bf16[20,512]{1,0:T(8,128)(2,1)S(1)} %multiply_convert_fusion.11), channel_id=1, source_target_pairs={{0,128},{1,129},{2,130},{3,131},{4,132},{5,133},{6,134},{7,135},{8... | collective-permute-start | bytes 61448 | tf_op jit(solution)/shard_map/ppermute | solution.py:68
  189.6 4.7 %collective-permute-start.16 = (bf16[40,512]{1,0:T(8,128)(2,1)S(1)}, bf16[40,512]{1,0:T(8,128)(2,1)S(1)}, u32[]{:S(2)}, u32[]{:S(2)}) collective-permute-start(bf16[40,512]{1,0:T(8,128)(2,1)S(1)} %maximum_select_fusion.5), channel_id=1, source_target_pairs={{0,256},{1,3},{2,258},{3,1},{4,260},{5,7},{6,262},{7,5},{8,264},{9... | collective-permute-start | bytes 122888 | tf_op jit(solution)/shard_map/ppermute | solution.py:68
  194.4 6.7 %collective-permute-start.17 = (bf16[80,512]{1,0:T(8,128)(2,1)S(1)}, bf16[80,512]{1,0:T(8,128)(2,1)S(1)}, u32[]{:S(2)}, u32[]{:S(2)}) collective-permute-start(bf16[80,512]{1,0:T(8,128)(2,1)S(1)} %maximum_select_fusion.4), channel_id=1, source_target_pairs={{0,2},{1,257},{2,0},{3,259},{4,6},{5,261},{6,4},{7,263},{8,10},{9,... | collective-permute-start | bytes 245768 | tf_op jit(solution)/shard_map/ppermute | solution.py:68
  201.1 6.1 %collective-permute-start.18 = (bf16[160,512]{1,0:T(8,128)(2,1)S(1)}, bf16[160,512]{1,0:T(8,128)(2,1)S(1)}, u32[]{:S(2)}, u32[]{:S(2)}) collective-permute-start(bf16[160,512]{1,0:T(8,128)(2,1)S(1)} %maximum_select_fusion.3), channel_id=1, source_target_pairs={{0,64},{1,33},{2,66},{3,35},{4,68},{5,37},{6,70},{7,39},{8,72},{9,... | collective-permute-start | bytes 491528 | tf_op jit(solution)/shard_map/ppermute | solution.py:68
  207.2 7.8 %collective-permute-start.19 = (bf16[320,512]{1,0:T(8,128)(2,1)S(1)}, bf16[320,512]{1,0:T(8,128)(2,1)S(1)}, u32[]{:S(2)}, u32[]{:S(2)}) collective-permute-start(bf16[320,512]{1,0:T(8,128)(2,1)S(1)} %maximum_select_fusion.2), channel_id=1, source_target_pairs={{0,32},{1,65},{2,34},{3,67},{4,36},{5,69},{6,38},{7,71},{8,40},{9,... | collective-permute-start | bytes 983048 | tf_op jit(solution)/shard_map/ppermute | solution.py:68
  215.3 17.1 %collective-permute-start.20 = (bf16[640,512]{1,0:T(8,128)(2,1)S(1)}, bf16[640,512]{1,0:T(8,128)(2,1)S(1)}, u32[]{:S(2)}, u32[]{:S(2)}) collective-permute-start(bf16[640,512]{1,0:T(8,128)(2,1)S(1)} %maximum_select_fusion.1), channel_id=1, source_target_pairs={{0,1},{1,0},{2,3},{3,2},{4,5},{5,4},{6,7},{7,6},{8,9},{9,8},{10,11... | collective-permute-start | bytes 1966088 | tf_op jit(solution)/shard_map/ppermute | solution.py:68
  (17 other events, 50.8 us)

commit v11 on v10

--- a/solution.py
+++ b/solution.py
@@ -132,9 +132,10 @@
     )
     hidden_activation = first_layer_stash[3]
     distant_offsets = SECOND_DILATION // number_of_steps
-    chunk_rows = number_of_steps // 2
+    chunk_count = 4
+    chunk_rows = number_of_steps // chunk_count
     local_parts, arrived_parts, term_parts, past_parts = [], [], [], []
-    for chunk in range(2):
+    for chunk in range(chunk_count):
         rows = slice(chunk * chunk_rows, (chunk + 1) * chunk_rows)
         hidden_chunk = hidden_activation[:, rows, :]
         if chunk:
@@ -162,7 +163,7 @@
         term_parts.append(chunk_terms)
     local_two = jnp.concatenate(local_parts, axis=1)
     arrived_back = jnp.concatenate(arrived_parts, axis=1)
-    second_layer_terms = tuple(first + second for first, second in zip(*term_parts))
+    second_layer_terms = tuple(sum(members[1:], members[0]) for members in zip(*term_parts))
     hidden_gradient = (local_two + arrived_back.astype(jnp.float32)).astype(jnp.bfloat16)
     local_one, forward_rows_first, first_layer_terms = backward_layer(
         signal,

time: 235 us -> 236 us (level)
  waiting for transfers between devices: 76.1 us -> 72.1 us
  matrix products: 14.5 us -> 17.5 us
    ppermute x6 -> x10, starting transfers between devices: 25.3 us -> 45.4 us  [shifted(): lax.ppermute(value, axis, [(source, source + steps) for source in range(l...]
    ppermute x12, starting transfers between devices: 85.4 us -> 68.6 us  [paired(): return lax.ppermute(value, AXES, pairs)]
    ppermute x6 -> x10, waiting for transfers between devices: 40 us -> 31.9 us  [shifted(): lax.ppermute(value, axis, [(source, source + steps) for source in range(l...]
    ppermute x12, waiting for transfers between devices: 28.3 us -> 31.2 us  [paired(): return lax.ppermute(value, AXES, pairs)]
  transfers between devices with their start and end apart: 21 -> 25, of which waited for: 19 -> 22; matrix products, arithmetic and copies ran while one was open for 4% -> 6% of each run, Pallas kernels for 0% -> 0%
where the time goes in v11:
time: 236 us; the launch traced here: 235 us
  starting transfers between devices  133 us (56%)
  waiting for transfers between devices  72.1 us (31%)
  matrix products  17.5 us (7%)
  local copies, waits for them, and re-layouts  5.26 us (2%)
  other arithmetic  5.14 us (2%)
    ppermute x12, starting transfers between devices, paired(): return lax.ppermute(value, AXES, pairs)  68.6 us
    ppermute x10, starting transfers between devices, shifted(): lax.ppermute(value, axis, [(source, source + steps) for source in range(l...  45.4 us
    ppermute x10, waiting for transfers between devices, shifted(): lax.ppermute(value, axis, [(source, source + steps) for source in range(l...  31.9 us
    ppermute x12, waiting for transfers between devices, paired(): return lax.ppermute(value, AXES, pairs)  31.2 us
    ppermute x3, starting transfers between devices, exchange(): lax.ppermute(value, axis, [(source, source ^ mask) for source in range(co...  19.2 us
    ppermute x3, waiting for transfers between devices, exchange(): lax.ppermute(value, axis, [(source, source ^ mask) for source in range(co...  8.97 us
  transfers between devices with their start and end apart: 25, of which 22 were waited for; matrix products, arithmetic and copies ran while one was open for 6% of the time, Pallas kernels for 0%

profile of v11, /device:TPU:1, one launch (start us, length us, event | category | flops | bytes accessed | tf_op | source)
XLA Modules:
  0.0 234.6 jit_solution(18157615134960921662)
XLA Ops:
  1.8 4.9 %collective-permute-start = (bf16[1,512,256]{2,1,0:T(8,128)(2,1)S(1)}, bf16[1,512,256]{2,1,0:T(8,128)(2,1)S(1)}, u32[]{:S(2)}, u32[]{:S(2)}) collective-permute-start(bf16[1,512,256]{2,1,0:T(8,128)(2,1)S(1)} %get-tuple-element.39), channel_id=1, source_target_pairs={{0,1},{1,2},{2,3},{3,4},{4,5},{5,6},{6,7},{7,8},{8,9},{9,10},{10,1... | collective-permute-start | bytes 786440 | tf_op jit(solution)/shard_map/ppermute | solution.py:15
  13.0 8.0 %collective-permute-start.1 = (bf16[1,256,256]{2,1,0:T(8,128)(2,1)S(1)}, bf16[1,256,256]{2,1,0:T(8,128)(2,1)S(1)}, u32[]{:S(2)}, u32[]{:S(2)}) collective-permute-start(bf16[1,256,256]{2,1,0:T(8,128)(2,1)S(1)} %get-tuple-element.35), channel_id=1, source_target_pairs={{0,8},{1,9},{2,10},{3,11},{4,12},{5,13},{6,14},{7,15},{8,16},{9,17... | collective-permute-start | bytes 393224 | tf_op jit(solution)/shard_map/ppermute | solution.py:15
  24.3 9.2 %collective-permute-start.2 = (bf16[1,256,256]{2,1,0:T(8,128)(2,1)S(1)}, bf16[1,256,256]{2,1,0:T(8,128)(2,1)S(1)}, u32[]{:S(2)}, u32[]{:S(2)}) collective-permute-start(bf16[1,256,256]{2,1,0:T(8,128)(2,1)S(1)} %get-tuple-element.12), channel_id=1, source_target_pairs={{0,8},{1,9},{2,10},{3,11},{4,12},{5,13},{6,14},{7,15},{8,16},{9,17... | collective-permute-start | bytes 393224 | tf_op jit(solution)/shard_map/ppermute | solution.py:15
  35.7 8.1 %collective-permute-start.3 = (bf16[1,256,256]{2,1,0:T(8,128)(2,1)S(1)}, bf16[1,256,256]{2,1,0:T(8,128)(2,1)S(1)}, u32[]{:S(2)}, u32[]{:S(2)}) collective-permute-start(bf16[1,256,256]{2,1,0:T(8,128)(2,1)S(1)} %get-tuple-element.13), channel_id=1, source_target_pairs={{0,8},{1,9},{2,10},{3,11},{4,12},{5,13},{6,14},{7,15},{8,16},{9,17... | collective-permute-start | bytes 393224 | tf_op jit(solution)/shard_map/ppermute | solution.py:15
  47.3 6.4 %collective-permute-done.3 = bf16[1,256,256]{2,1,0:T(8,128)(2,1)S(1)} collective-permute-done((bf16[1,256,256]{2,1,0:T(8,128)(2,1)S(1)}, bf16[1,256,256]{2,1,0:T(8,128)(2,1)S(1)}, u32[]{:S(2)}, u32[]{:S(2)}) %collective-permute-start.3) | collective-permute-done | bytes 131104 | tf_op jit(solution)/shard_map/ppermute | solution.py:15
  53.7 8.0 %collective-permute-start.4 = (bf16[1,256,256]{2,1,0:T(8,128)(2,1)S(1)}, bf16[1,256,256]{2,1,0:T(8,128)(2,1)S(1)}, u32[]{:S(2)}, u32[]{:S(2)}) collective-permute-start(bf16[1,256,256]{2,1,0:T(8,128)(2,1)S(1)} %get-tuple-element.14), channel_id=1, source_target_pairs={{0,8},{1,9},{2,10},{3,11},{4,12},{5,13},{6,14},{7,15},{8,16},{9,17... | collective-permute-start | bytes 393224 | tf_op jit(solution)/shard_map/ppermute | solution.py:15
  70.7 5.7 %collective-permute-done.7 = bf16[1,256,256]{2,1,0:T(8,128)(2,1)S(1)} collective-permute-done((bf16[1,256,256]{2,1,0:T(8,128)(2,1)S(1)}, bf16[1,256,256]{2,1,0:T(8,128)(2,1)S(1)}, u32[]{:S(2)}, u32[]{:S(2)}) %collective-permute-start.7) | collective-permute-done | bytes 131104 | tf_op jit(solution)/shard_map/ppermute | solution.py:15
  76.4 7.1 %collective-permute-done.8 = bf16[1,256,256]{2,1,0:T(8,128)(2,1)S(1)} collective-permute-done((bf16[1,256,256]{2,1,0:T(8,128)(2,1)S(1)}, bf16[1,256,256]{2,1,0:T(8,128)(2,1)S(1)}, u32[]{:S(2)}, u32[]{:S(2)}) %collective-permute-start.8) | collective-permute-done | bytes 131104 | tf_op jit(solution)/shard_map/ppermute | solution.py:15
  87.9 17.7 %collective-permute-start.9 = (f32[640,512]{1,0:T(8,128)}, f32[640,512]{1,0:T(8,128)}, u32[]{:S(2)}, u32[]{:S(2)}) collective-permute-start(f32[640,512]{1,0:T(8,128)} %fusion.14), channel_id=1, source_target_pairs={{0,1},{1,0},{2,3},{3,2},{4,5},{5,4},{6,7},{7,6},{8,9},{9,8},{10,11... | collective-permute-start | bytes 3932168 | tf_op jit(solution)/shard_map/ppermute | solution.py:68
  116.6 6.1 %collective-permute-done.11 = bf16[1,512,256]{2,1,0:T(8,128)(2,1)} collective-permute-done((bf16[1,512,256]{2,1,0:T(8,128)(2,1)}, bf16[1,512,256]{2,1,0:T(8,128)(2,1)}, u32[]{:S(2)}, u32[]{:S(2)}) %collective-permute-start.11) | collective-permute-done | bytes 262176 | tf_op jit(solution)/shard_map/ppermute | solution.py:15
  127.8 5.7 %collective-permute-done.12 = f32[160,512]{1,0:T(8,128)S(1)} collective-permute-done((f32[160,512]{1,0:T(8,128)S(1)}, f32[160,512]{1,0:T(8,128)S(1)}, u32[]{:S(2)}, u32[]{:S(2)}) %collective-permute-start.12) | collective-permute-done | bytes 327712 | tf_op jit(solution)/shard_map/ppermute | solution.py:68
  133.6 4.7 %collective-permute-start.13 = (f32[80,512]{1,0:T(8,128)S(1)}, f32[80,512]{1,0:T(8,128)S(1)}, u32[]{:S(2)}, u32[]{:S(2)}) collective-permute-start(f32[80,512]{1,0:T(8,128)S(1)} %slice_select_fusion.2), channel_id=1, source_target_pairs={{0,2},{1,257},{2,0},{3,259},{4,6},{5,261},{6,4},{7,263},{8,10},{9,... | collective-permute-start | bytes 491528 | tf_op jit(solution)/shard_map/ppermute | solution.py:68
  143.1 3.5 %collective-permute-done.14 = f32[40,512]{1,0:T(8,128)S(1)} collective-permute-done((f32[40,512]{1,0:T(8,128)S(1)}, f32[40,512]{1,0:T(8,128)S(1)}, u32[]{:S(2)}, u32[]{:S(2)}) %collective-permute-start.14) | collective-permute-done | bytes 81952 | tf_op jit(solution)/shard_map/ppermute | solution.py:68
  146.7 4.5 %collective-permute-start.15 = (f32[20,512]{1,0:T(8,128)S(1)}, f32[20,512]{1,0:T(8,128)S(1)}, u32[]{:S(2)}, u32[]{:S(2)}) collective-permute-start(f32[20,512]{1,0:T(8,128)S(1)} %slice_select_fusion.4), channel_id=1, source_target_pairs={{0,128},{1,129},{2,130},{3,131},{4,132},{5,133},{6,134},{7,135},{8... | collective-permute-start | bytes 122888 | tf_op jit(solution)/shard_map/ppermute | solution.py:68
  153.1 3.5 %collective-permute-start.16 = (f32[20,512]{1,0:T(8,128)S(1)}, f32[20,512]{1,0:T(8,128)S(1)}, u32[]{:S(2)}, u32[]{:S(2)}) collective-permute-start(f32[20,512]{1,0:T(8,128)S(1)} %select_add_fusion.5), channel_id=1, source_target_pairs={{0,4},{1,5},{2,6},{3,7},{4,0},{5,1},{6,2},{7,3},{8,12},{9,13},{10,... | collective-permute-start | bytes 122888 | tf_op jit(solution)/shard_map/ppermute | solution.py:78
  158.8 5.2 %collective-permute-start.17 = (f32[20,512]{1,0:T(8,128)S(1)}, f32[20,512]{1,0:T(8,128)S(1)}, u32[]{:S(2)}, u32[]{:S(2)}) collective-permute-start(f32[20,512]{1,0:T(8,128)S(1)} %add.160), channel_id=1, source_target_pairs={{0,8},{1,9},{2,10},{3,11},{4,12},{5,13},{6,14},{7,15},{8,0},{9,1},... | collective-permute-start | bytes 122888 | tf_op jit(solution)/shard_map/ppermute | solution.py:78
  164.1 3.5 %collective-permute-done.17 = f32[20,512]{1,0:T(8,128)S(1)} collective-permute-done((f32[20,512]{1,0:T(8,128)S(1)}, f32[20,512]{1,0:T(8,128)S(1)}, u32[]{:S(2)}, u32[]{:S(2)}) %collective-permute-start.17) | collective-permute-done | bytes 40992 | tf_op jit(solution)/shard_map/ppermute | solution.py:78
  167.6 10.4 %collective-permute-start.18 = (f32[20,512]{1,0:T(8,128)S(1)}, f32[20,512]{1,0:T(8,128)S(1)}, u32[]{:S(2)}, u32[]{:S(2)}) collective-permute-start(f32[20,512]{1,0:T(8,128)S(1)} %add.161), channel_id=1, source_target_pairs={{0,16},{1,17},{2,18},{3,19},{4,20},{5,21},{6,22},{7,23},{8,24},{9,... | collective-permute-start | bytes 122888 | tf_op jit(solution)/shard_map/ppermute | solution.py:78
  178.0 3.3 %collective-permute-done.18 = f32[20,512]{1,0:T(8,128)S(1)} collective-permute-done((f32[20,512]{1,0:T(8,128)S(1)}, f32[20,512]{1,0:T(8,128)S(1)}, u32[]{:S(2)}, u32[]{:S(2)}) %collective-permute-start.18) | collective-permute-done | bytes 40992 | tf_op jit(solution)/shard_map/ppermute | solution.py:78
  181.3 4.6 %collective-permute-start.19 = (bf16[20,512]{1,0:T(8,128)(2,1)S(1)}, bf16[20,512]{1,0:T(8,128)(2,1)S(1)}, u32[]{:S(2)}, u32[]{:S(2)}) collective-permute-start(bf16[20,512]{1,0:T(8,128)(2,1)S(1)} %multiply_convert_fusion.19), channel_id=1, source_target_pairs={{0,128},{1,129},{2,130},{3,131},{4,132},{5,133},{6,134},{7,135},{8... | collective-permute-start | bytes 61448 | tf_op jit(solution)/shard_map/ppermute | solution.py:68
  192.2 4.8 %collective-permute-start.21 = (bf16[80,512]{1,0:T(8,128)(2,1)S(1)}, bf16[80,512]{1,0:T(8,128)(2,1)S(1)}, u32[]{:S(2)}, u32[]{:S(2)}) collective-permute-start(bf16[80,512]{1,0:T(8,128)(2,1)S(1)} %maximum_select_fusion.4), channel_id=1, source_target_pairs={{0,2},{1,257},{2,0},{3,259},{4,6},{5,261},{6,4},{7,263},{8,10},{9,... | collective-permute-start | bytes 245768 | tf_op jit(solution)/shard_map/ppermute | solution.py:68
  201.6 3.4 %collective-permute-done.22 = bf16[160,512]{1,0:T(8,128)(2,1)S(1)} collective-permute-done((bf16[160,512]{1,0:T(8,128)(2,1)S(1)}, bf16[160,512]{1,0:T(8,128)(2,1)S(1)}, u32[]{:S(2)}, u32[]{:S(2)}) %collective-permute-start.22) | collective-permute-done | bytes 163872 | tf_op jit(solution)/shard_map/ppermute | solution.py:68
  207.2 5.7 %collective-permute-done.23 = bf16[320,512]{1,0:T(8,128)(2,1)S(1)} collective-permute-done((bf16[320,512]{1,0:T(8,128)(2,1)S(1)}, bf16[320,512]{1,0:T(8,128)(2,1)S(1)}, u32[]{:S(2)}, u32[]{:S(2)}) %collective-permute-start.23) | collective-permute-done | bytes 327712 | tf_op jit(solution)/shard_map/ppermute | solution.py:68
  213.1 17.5 %collective-permute-start.24 = (bf16[640,512]{1,0:T(8,128)(2,1)S(1)}, bf16[640,512]{1,0:T(8,128)(2,1)S(1)}, u32[]{:S(2)}, u32[]{:S(2)}) collective-permute-start(bf16[640,512]{1,0:T(8,128)(2,1)S(1)} %maximum_select_fusion.1), channel_id=1, source_target_pairs={{0,1},{1,0},{2,3},{3,2},{4,5},{5,4},{6,7},{7,6},{8,9},{9,8},{10,11... | collective-permute-start | bytes 1966088 | tf_op jit(solution)/shard_map/ppermute | solution.py:68
  (135 shorter events, 71.6 us)
Async XLA Ops:
  1.8 9.2 %collective-permute-start = (bf16[1,512,256]{2,1,0:T(8,128)(2,1)S(1)}, bf16[1,512,256]{2,1,0:T(8,128)(2,1)S(1)}, u32[]{:S(2)}, u32[]{:S(2)}) collective-permute-start(bf16[1,512,256]{2,1,0:T(8,128)(2,1)S(1)} %get-tuple-element.39), channel_id=1, source_target_pairs={{0,1},{1,2},{2,3},{3,4},{4,5},{5,6},{6,7},{7,8},{8,9},{9,10},{10,1... | collective-permute-start | bytes 786440 | tf_op jit(solution)/shard_map/ppermute | solution.py:15
  13.0 9.9 %collective-permute-start.1 = (bf16[1,256,256]{2,1,0:T(8,128)(2,1)S(1)}, bf16[1,256,256]{2,1,0:T(8,128)(2,1)S(1)}, u32[]{:S(2)}, u32[]{:S(2)}) collective-permute-start(bf16[1,256,256]{2,1,0:T(8,128)(2,1)S(1)} %get-tuple-element.35), channel_id=1, source_target_pairs={{0,8},{1,9},{2,10},{3,11},{4,12},{5,13},{6,14},{7,15},{8,16},{9,17... | collective-permute-start | bytes 393224 | tf_op jit(solution)/shard_map/ppermute | solution.py:15
  24.3 11.4 %collective-permute-start.2 = (bf16[1,256,256]{2,1,0:T(8,128)(2,1)S(1)}, bf16[1,256,256]{2,1,0:T(8,128)(2,1)S(1)}, u32[]{:S(2)}, u32[]{:S(2)}) collective-permute-start(bf16[1,256,256]{2,1,0:T(8,128)(2,1)S(1)} %get-tuple-element.12), channel_id=1, source_target_pairs={{0,8},{1,9},{2,10},{3,11},{4,12},{5,13},{6,14},{7,15},{8,16},{9,17... | collective-permute-start | bytes 393224 | tf_op jit(solution)/shard_map/ppermute | solution.py:15
  33.8 36.9 %collective-permute-start.5 = (bf16[1,256,256]{2,1,0:T(8,128)(2,1)S(1)}, bf16[1,256,256]{2,1,0:T(8,128)(2,1)S(1)}, u32[]{:S(2)}, u32[]{:S(2)}) collective-permute-start(bf16[1,256,256]{2,1,0:T(8,128)(2,1)S(1)} %fusion.6), channel_id=1, source_target_pairs={{8,0},{9,1},{10,2},{11,3},{12,4},{13,5},{14,6},{15,7},{16,8},{17,9... | collective-permute-start | bytes 393224 | tf_op jit(solution)/shard_map/ppermute | solution.py:15
  35.7 18.0 %collective-permute-start.3 = (bf16[1,256,256]{2,1,0:T(8,128)(2,1)S(1)}, bf16[1,256,256]{2,1,0:T(8,128)(2,1)S(1)}, u32[]{:S(2)}, u32[]{:S(2)}) collective-permute-start(bf16[1,256,256]{2,1,0:T(8,128)(2,1)S(1)} %get-tuple-element.13), channel_id=1, source_target_pairs={{0,8},{1,9},{2,10},{3,11},{4,12},{5,13},{6,14},{7,15},{8,16},{9,17... | collective-permute-start | bytes 393224 | tf_op jit(solution)/shard_map/ppermute | solution.py:15
  45.7 25.0 %collective-permute-start.6 = (bf16[1,256,256]{2,1,0:T(8,128)(2,1)S(1)}, bf16[1,256,256]{2,1,0:T(8,128)(2,1)S(1)}, u32[]{:S(2)}, u32[]{:S(2)}) collective-permute-start(bf16[1,256,256]{2,1,0:T(8,128)(2,1)S(1)} %fusion.7), channel_id=1, source_target_pairs={{8,0},{9,1},{10,2},{11,3},{12,4},{13,5},{14,6},{15,7},{16,8},{17,9... | collective-permute-start | bytes 393224 | tf_op jit(solution)/shard_map/ppermute | solution.py:15
  53.7 13.5 %collective-permute-start.4 = (bf16[1,256,256]{2,1,0:T(8,128)(2,1)S(1)}, bf16[1,256,256]{2,1,0:T(8,128)(2,1)S(1)}, u32[]{:S(2)}, u32[]{:S(2)}) collective-permute-start(bf16[1,256,256]{2,1,0:T(8,128)(2,1)S(1)} %get-tuple-element.14), channel_id=1, source_target_pairs={{0,8},{1,9},{2,10},{3,11},{4,12},{5,13},{6,14},{7,15},{8,16},{9,17... | collective-permute-start | bytes 393224 | tf_op jit(solution)/shard_map/ppermute | solution.py:15
  63.1 13.3 %collective-permute-start.7 = (bf16[1,256,256]{2,1,0:T(8,128)(2,1)S(1)}, bf16[1,256,256]{2,1,0:T(8,128)(2,1)S(1)}, u32[]{:S(2)}, u32[]{:S(2)}) collective-permute-start(bf16[1,256,256]{2,1,0:T(8,128)(2,1)S(1)} %fusion.8), channel_id=1, source_target_pairs={{8,0},{9,1},{10,2},{11,3},{12,4},{13,5},{14,6},{15,7},{16,8},{17,9... | collective-permute-start | bytes 393224 | tf_op jit(solution)/shard_map/ppermute | solution.py:15
  68.0 15.5 %collective-permute-start.8 = (bf16[1,256,256]{2,1,0:T(8,128)(2,1)S(1)}, bf16[1,256,256]{2,1,0:T(8,128)(2,1)S(1)}, u32[]{:S(2)}, u32[]{:S(2)}) collective-permute-start(bf16[1,256,256]{2,1,0:T(8,128)(2,1)S(1)} %fusion.9), channel_id=1, source_target_pairs={{8,0},{9,1},{10,2},{11,3},{12,4},{13,5},{14,6},{15,7},{16,8},{17,9... | collective-permute-start | bytes 393224 | tf_op jit(solution)/shard_map/ppermute | solution.py:15
  87.9 20.7 %collective-permute-start.9 = (f32[640,512]{1,0:T(8,128)}, f32[640,512]{1,0:T(8,128)}, u32[]{:S(2)}, u32[]{:S(2)}) collective-permute-start(f32[640,512]{1,0:T(8,128)} %fusion.14), channel_id=1, source_target_pairs={{0,1},{1,0},{2,3},{3,2},{4,5},{5,4},{6,7},{7,6},{8,9},{9,8},{10,11... | collective-permute-start | bytes 3932168 | tf_op jit(solution)/shard_map/ppermute | solution.py:68
  110.5 14.9 %collective-permute-start.10 = (f32[320,512]{1,0:T(8,128)S(1)}, f32[320,512]{1,0:T(8,128)S(1)}, u32[]{:S(2)}, u32[]{:S(2)}) collective-permute-start(f32[320,512]{1,0:T(8,128)S(1)} %slice_select_fusion), channel_id=1, source_target_pairs={{0,32},{1,65},{2,34},{3,67},{4,36},{5,69},{6,38},{7,71},{8,40},{9,... | collective-permute-start | bytes 1966088 | tf_op jit(solution)/shard_map/ppermute | solution.py:68
  114.5 8.2 %collective-permute-start.11 = (bf16[1,512,256]{2,1,0:T(8,128)(2,1)}, bf16[1,512,256]{2,1,0:T(8,128)(2,1)}, u32[]{:S(2)}, u32[]{:S(2)}) collective-permute-start(bf16[1,512,256]{2,1,0:T(8,128)(2,1)} %get-tuple-element.34), channel_id=1, source_target_pairs={{1,0},{2,1},{3,2},{4,3},{5,4},{6,5},{7,6},{8,7},{9,8},{10,9},{11,1... | collective-permute-start | bytes 786440 | tf_op jit(solution)/shard_map/ppermute | solution.py:15
  125.7 7.8 %collective-permute-start.12 = (f32[160,512]{1,0:T(8,128)S(1)}, f32[160,512]{1,0:T(8,128)S(1)}, u32[]{:S(2)}, u32[]{:S(2)}) collective-permute-start(f32[160,512]{1,0:T(8,128)S(1)} %slice_select_fusion.1), channel_id=1, source_target_pairs={{0,64},{1,33},{2,66},{3,35},{4,68},{5,37},{6,70},{7,39},{8,72},{9,... | collective-permute-start | bytes 983048 | tf_op jit(solution)/shard_map/ppermute | solution.py:68
  133.6 7.6 %collective-permute-start.13 = (f32[80,512]{1,0:T(8,128)S(1)}, f32[80,512]{1,0:T(8,128)S(1)}, u32[]{:S(2)}, u32[]{:S(2)}) collective-permute-start(f32[80,512]{1,0:T(8,128)S(1)} %slice_select_fusion.2), channel_id=1, source_target_pairs={{0,2},{1,257},{2,0},{3,259},{4,6},{5,261},{6,4},{7,263},{8,10},{9,... | collective-permute-start | bytes 491528 | tf_op jit(solution)/shard_map/ppermute | solution.py:68
  141.2 5.5 %collective-permute-start.14 = (f32[40,512]{1,0:T(8,128)S(1)}, f32[40,512]{1,0:T(8,128)S(1)}, u32[]{:S(2)}, u32[]{:S(2)}) collective-permute-start(f32[40,512]{1,0:T(8,128)S(1)} %slice_select_fusion.3), channel_id=1, source_target_pairs={{0,256},{1,3},{2,258},{3,1},{4,260},{5,7},{6,262},{7,5},{8,264},{9... | collective-permute-start | bytes 245768 | tf_op jit(solution)/shard_map/ppermute | solution.py:68
  146.7 6.3 %collective-permute-start.15 = (f32[20,512]{1,0:T(8,128)S(1)}, f32[20,512]{1,0:T(8,128)S(1)}, u32[]{:S(2)}, u32[]{:S(2)}) collective-permute-start(f32[20,512]{1,0:T(8,128)S(1)} %slice_select_fusion.4), channel_id=1, source_target_pairs={{0,128},{1,129},{2,130},{3,131},{4,132},{5,133},{6,134},{7,135},{8... | collective-permute-start | bytes 122888 | tf_op jit(solution)/shard_map/ppermute | solution.py:68
  153.1 5.7 %collective-permute-start.16 = (f32[20,512]{1,0:T(8,128)S(1)}, f32[20,512]{1,0:T(8,128)S(1)}, u32[]{:S(2)}, u32[]{:S(2)}) collective-permute-start(f32[20,512]{1,0:T(8,128)S(1)} %select_add_fusion.5), channel_id=1, source_target_pairs={{0,4},{1,5},{2,6},{3,7},{4,0},{5,1},{6,2},{7,3},{8,12},{9,13},{10,... | collective-permute-start | bytes 122888 | tf_op jit(solution)/shard_map/ppermute | solution.py:78
  158.8 8.7 %collective-permute-start.17 = (f32[20,512]{1,0:T(8,128)S(1)}, f32[20,512]{1,0:T(8,128)S(1)}, u32[]{:S(2)}, u32[]{:S(2)}) collective-permute-start(f32[20,512]{1,0:T(8,128)S(1)} %add.160), channel_id=1, source_target_pairs={{0,8},{1,9},{2,10},{3,11},{4,12},{5,13},{6,14},{7,15},{8,0},{9,1},... | collective-permute-start | bytes 122888 | tf_op jit(solution)/shard_map/ppermute | solution.py:78
  167.6 13.7 %collective-permute-start.18 = (f32[20,512]{1,0:T(8,128)S(1)}, f32[20,512]{1,0:T(8,128)S(1)}, u32[]{:S(2)}, u32[]{:S(2)}) collective-permute-start(f32[20,512]{1,0:T(8,128)S(1)} %add.161), channel_id=1, source_target_pairs={{0,16},{1,17},{2,18},{3,19},{4,20},{5,21},{6,22},{7,23},{8,24},{9,... | collective-permute-start | bytes 122888 | tf_op jit(solution)/shard_map/ppermute | solution.py:78
  181.3 6.1 %collective-permute-start.19 = (bf16[20,512]{1,0:T(8,128)(2,1)S(1)}, bf16[20,512]{1,0:T(8,128)(2,1)S(1)}, u32[]{:S(2)}, u32[]{:S(2)}) collective-permute-start(bf16[20,512]{1,0:T(8,128)(2,1)S(1)} %multiply_convert_fusion.19), channel_id=1, source_target_pairs={{0,128},{1,129},{2,130},{3,131},{4,132},{5,133},{6,134},{7,135},{8... | collective-permute-start | bytes 61448 | tf_op jit(solution)/shard_map/ppermute | solution.py:68
  192.2 6.7 %collective-permute-start.21 = (bf16[80,512]{1,0:T(8,128)(2,1)S(1)}, bf16[80,512]{1,0:T(8,128)(2,1)S(1)}, u32[]{:S(2)}, u32[]{:S(2)}) collective-permute-start(bf16[80,512]{1,0:T(8,128)(2,1)S(1)} %maximum_select_fusion.4), channel_id=1, source_target_pairs={{0,2},{1,257},{2,0},{3,259},{4,6},{5,261},{6,4},{7,263},{8,10},{9,... | collective-permute-start | bytes 245768 | tf_op jit(solution)/shard_map/ppermute | solution.py:68
  198.9 6.1 %collective-permute-start.22 = (bf16[160,512]{1,0:T(8,128)(2,1)S(1)}, bf16[160,512]{1,0:T(8,128)(2,1)S(1)}, u32[]{:S(2)}, u32[]{:S(2)}) collective-permute-start(bf16[160,512]{1,0:T(8,128)(2,1)S(1)} %maximum_select_fusion.3), channel_id=1, source_target_pairs={{0,64},{1,33},{2,66},{3,35},{4,68},{5,37},{6,70},{7,39},{8,72},{9,... | collective-permute-start | bytes 491528 | tf_op jit(solution)/shard_map/ppermute | solution.py:68
  205.1 7.8 %collective-permute-start.23 = (bf16[320,512]{1,0:T(8,128)(2,1)S(1)}, bf16[320,512]{1,0:T(8,128)(2,1)S(1)}, u32[]{:S(2)}, u32[]{:S(2)}) collective-permute-start(bf16[320,512]{1,0:T(8,128)(2,1)S(1)} %maximum_select_fusion.2), channel_id=1, source_target_pairs={{0,32},{1,65},{2,34},{3,67},{4,36},{5,69},{6,38},{7,71},{8,40},{9,... | collective-permute-start | bytes 983048 | tf_op jit(solution)/shard_map/ppermute | solution.py:68
  213.1 19.2 %collective-permute-start.24 = (bf16[640,512]{1,0:T(8,128)(2,1)S(1)}, bf16[640,512]{1,0:T(8,128)(2,1)S(1)}, u32[]{:S(2)}, u32[]{:S(2)}) collective-permute-start(bf16[640,512]{1,0:T(8,128)(2,1)S(1)} %maximum_select_fusion.1), channel_id=1, source_target_pairs={{0,1},{1,0},{2,3},{3,2},{4,5},{5,4},{6,7},{7,6},{8,9},{9,8},{10,11... | collective-permute-start | bytes 1966088 | tf_op jit(solution)/shard_map/ppermute | solution.py:68
  (21 other events, 119.7 us)
